TPU v7x, 512 devices: a whole 4x8x8 slice. The times are simulated.
512 devices in a mesh: sep: 8 (over y), row: 8 (over z), col: 8 (over x, core).
Axes of the slice: x: 4, y: 8, z: 8, core: 2. Of those that a mesh axis runs over, the one named last changes fastest.
Arguments:
- right_sides: float32 [2, 16, 32768], P(None, None, ('sep', 'row', 'col')), may hold values from -6 to 6
- inverse_diag: float32 [8, 4096, 4096], P('sep', ('row', 'col')), may hold values from -0.09375 to 0.09375
- lower_blocks: float32 [8, 2048, 4096], P('sep', ('row', 'col')), may hold values from -0.09375 to 0.09375
- targets: int32 [8, 2048], P('sep', ('row', 'col')), may hold values from 0 to 32767, as said below
- counts: int32 [8, 64], P('sep', ('row', 'col')), may hold values from 0 to 32, as said below
Outputs:
- solution: float32 [2, 16, 32768], P(None, None, ('sep', 'row', 'col'))
Inputs may be any that keep to these rules, and one draw needn't show every extreme that they name: For every separator s and lower row j: targets[s, j] // 4096 > s, except for the last separator whose counts are all zero; and (targets[s, j] % 4096) // 64 == j // 32. The last separator's counts are zero; every other separator has a block with exactly 32 live rows, and the others at least one.
All inputs are finite; a program needn't handle non-finite values.
Results may differ from a plain program's by a relative error of at most 0.0001.
Values sent between devices are 32-bit elements; how exact they have to be, the bound alone decides.
No kernel may reach another device: no remote copies, remote signals or barrier semaphores. Data moves between devices by JAX's collectives and lax.ppermute only.
A program may use at most 64 MiB of HBM per device.

v0:
```python
import jax
import jax.numpy as jnp
from jax import lax
from jax.sharding import PartitionSpec as P

W = 4096


def passed_along(block, axis, distance):
    devices = range(lax.axis_size(axis))
    route = [(i - distance, i) for i in devices if i - distance in devices]
    return lax.ppermute(block, axis, route)


def shards(right_sides, inverse_diag, lower_blocks, targets, counts):
    levels = lax.axis_size("sep")
    own_level = lax.axis_index("sep")
    batches = right_sides.shape[0]
    width_rhs = right_sides.shape[1]
    own_rows = right_sides.shape[2]
    diag_rows = inverse_diag[0]
    lower_rows = lower_blocks[0]
    lower_count = lower_rows.shape[0]
    live = jnp.arange(lower_count, dtype=jnp.int32) < counts[0, 0]
    places = targets[0] // W * own_rows + targets[0] % own_rows

    def solve_piece(segment):
        return lax.dot_general(
            segment,
            diag_rows,
            (((1,), (1,)), ((), ())),
            precision=lax.Precision.HIGHEST,
            preferred_element_type=jnp.float32,
        )

    def lower_piece(segment):
        return lax.dot_general(
            segment,
            lower_rows,
            (((1,), (1,)), ((), ())),
            precision=lax.Precision.HIGHEST,
            preferred_element_type=jnp.float32,
        )

    def one_turn(turn, state):
        carried, solved_all = state
        batch_now = turn // levels
        active = turn % levels == own_level
        batch_now = jnp.clip(batch_now, 0, batches - 1)
        given = lax.dynamic_index_in_dim(right_sides, batch_now, 0, keepdims=False)
        resid = given - lax.dynamic_slice_in_dim(carried, own_level * own_rows, own_rows, 1)
        solved = solve_piece(lax.all_gather(resid, ("row", "col"), axis=1, tiled=True))
        update = lower_piece(lax.all_gather(solved, ("row", "col"), axis=1, tiled=True))
        update = jnp.where(live[None, :], update, jnp.float32(0.0))
        carried = carried.at[:, places].add(update)
        former = lax.dynamic_index_in_dim(solved_all, batch_now, 0, keepdims=False)
        solved_all = lax.dynamic_update_index_in_dim(
            solved_all, jnp.where(active, solved, former), batch_now, 0
        )
        carried = passed_along(carried, "sep", 1)
        return (carried, solved_all)

    turns = batches * levels
    start_carry = jnp.zeros((width_rhs, levels * own_rows), jnp.float32)
    start_solved = jnp.zeros(right_sides.shape, jnp.float32)
    final_carry, solution = lax.fori_loop(0, turns, one_turn, (start_carry, start_solved))
    return solution


def solution(mesh):
    placed = (
        P(None, None, ("sep", "row", "col")),
        P("sep", ("row", "col"), None),
        P("sep", ("row", "col"), None),
        P("sep", ("row", "col")),
        P("sep", ("row", "col")),
    )
    return jax.shard_map(
        shards,
        mesh=mesh,
        in_specs=placed,
        out_specs=P(None, None, ("sep", "row", "col")),
        check_vma=False,
    )
```

profile of v0, /device:TPU:33, one launch (start us, length us, event | category | flops | bytes accessed | tf_op | source)
XLA Modules:
  0.0 1837.5 jit_solution(4809233854240847362)
XLA Ops:
  1.4 1835.4 %while.18 = (s32[]{:T(128)}, f32[16,512]{0,1:T(8,128)S(1)}, f32[2,16,64]{2,1,0:T(8,128)S(1)}, s32[32]{0:T(128)S(1)}, f32[2,16,64]{2,1,0:T(8,128)S(1)}, /*index=5...) while((s32[]{:T(128)}, f32[16,512]{0,1:T(8,128)S(1)}, ...), condition=%wide.region_2.3_spmd.clone, body=%wide.region_0.2_spmd.clone.sunk | while | flops 75500688 | bytes 11338590 | solution.py:66
  1.6 57.0 %all-gather.6 = f32[64,64,16]{1,2,0:T(8,128)S(1)} all-gather(f32[1,64,16]{1,2,0:T(8,128)S(1)} %fusion.22), channel_id=1, replica_groups=mesh['sep'=8,'row'=8,'col'=8] {'row','col'}, dimensions={0}, use_global_device_ids=true | all-gather | bytes 266240 | tf_op jit(solution)/shard_map/while/body/eval_jaxpr/all_gather | solution.py:52
  60.8 49.5 %all-gather.7 = f32[64,64,16]{1,2,0:T(8,128)S(1)} all-gather(f32[1,64,16]{1,2,0:T(8,128)S(1)} %bitcast.71), channel_id=1, replica_groups=mesh['sep'=8,'row'=8,'col'=8] {'row','col'}, dimensions={0}, use_global_device_ids=true | all-gather | bytes 266240 | tf_op jit(solution)/shard_map/while/body/eval_jaxpr/all_gather | solution.py:53
  113.0 2.3 collective-permute-start
  115.3 8.5 collective-permute-done
  124.0 48.8 %all-gather.6 = f32[64,64,16]{1,2,0:T(8,128)S(1)} all-gather(f32[1,64,16]{1,2,0:T(8,128)S(1)} %fusion.22), channel_id=1, replica_groups=mesh['sep'=8,'row'=8,'col'=8] {'row','col'}, dimensions={0}, use_global_device_ids=true | all-gather | bytes 266240 | tf_op jit(solution)/shard_map/while/body/eval_jaxpr/all_gather | solution.py:52
  175.0 49.5 %all-gather.7 = f32[64,64,16]{1,2,0:T(8,128)S(1)} all-gather(f32[1,64,16]{1,2,0:T(8,128)S(1)} %bitcast.71), channel_id=1, replica_groups=mesh['sep'=8,'row'=8,'col'=8] {'row','col'}, dimensions={0}, use_global_device_ids=true | all-gather | bytes 266240 | tf_op jit(solution)/shard_map/while/body/eval_jaxpr/all_gather | solution.py:53
  227.2 1.9 collective-permute-start
  229.1 8.9 collective-permute-done
  238.2 48.8 %all-gather.6 = f32[64,64,16]{1,2,0:T(8,128)S(1)} all-gather(f32[1,64,16]{1,2,0:T(8,128)S(1)} %fusion.22), channel_id=1, replica_groups=mesh['sep'=8,'row'=8,'col'=8] {'row','col'}, dimensions={0}, use_global_device_ids=true | all-gather | bytes 266240 | tf_op jit(solution)/shard_map/while/body/eval_jaxpr/all_gather | solution.py:52
  289.2 49.5 %all-gather.7 = f32[64,64,16]{1,2,0:T(8,128)S(1)} all-gather(f32[1,64,16]{1,2,0:T(8,128)S(1)} %bitcast.71), channel_id=1, replica_groups=mesh['sep'=8,'row'=8,'col'=8] {'row','col'}, dimensions={0}, use_global_device_ids=true | all-gather | bytes 266240 | tf_op jit(solution)/shard_map/while/body/eval_jaxpr/all_gather | solution.py:53
  341.4 1.9 collective-permute-start
  343.3 8.9 collective-permute-done
  352.4 48.8 %all-gather.6 = f32[64,64,16]{1,2,0:T(8,128)S(1)} all-gather(f32[1,64,16]{1,2,0:T(8,128)S(1)} %fusion.22), channel_id=1, replica_groups=mesh['sep'=8,'row'=8,'col'=8] {'row','col'}, dimensions={0}, use_global_device_ids=true | all-gather | bytes 266240 | tf_op jit(solution)/shard_map/while/body/eval_jaxpr/all_gather | solution.py:52
  403.4 49.5 %all-gather.7 = f32[64,64,16]{1,2,0:T(8,128)S(1)} all-gather(f32[1,64,16]{1,2,0:T(8,128)S(1)} %bitcast.71), channel_id=1, replica_groups=mesh['sep'=8,'row'=8,'col'=8] {'row','col'}, dimensions={0}, use_global_device_ids=true | all-gather | bytes 266240 | tf_op jit(solution)/shard_map/while/body/eval_jaxpr/all_gather | solution.py:53
  455.6 1.9 collective-permute-start
  457.5 8.9 collective-permute-done
  466.6 48.8 %all-gather.6 = f32[64,64,16]{1,2,0:T(8,128)S(1)} all-gather(f32[1,64,16]{1,2,0:T(8,128)S(1)} %fusion.22), channel_id=1, replica_groups=mesh['sep'=8,'row'=8,'col'=8] {'row','col'}, dimensions={0}, use_global_device_ids=true | all-gather | bytes 266240 | tf_op jit(solution)/shard_map/while/body/eval_jaxpr/all_gather | solution.py:52
  517.6 49.5 %all-gather.7 = f32[64,64,16]{1,2,0:T(8,128)S(1)} all-gather(f32[1,64,16]{1,2,0:T(8,128)S(1)} %bitcast.71), channel_id=1, replica_groups=mesh['sep'=8,'row'=8,'col'=8] {'row','col'}, dimensions={0}, use_global_device_ids=true | all-gather | bytes 266240 | tf_op jit(solution)/shard_map/while/body/eval_jaxpr/all_gather | solution.py:53
  569.8 1.9 collective-permute-start
  571.7 8.9 collective-permute-done
  580.8 48.8 %all-gather.6 = f32[64,64,16]{1,2,0:T(8,128)S(1)} all-gather(f32[1,64,16]{1,2,0:T(8,128)S(1)} %fusion.22), channel_id=1, replica_groups=mesh['sep'=8,'row'=8,'col'=8] {'row','col'}, dimensions={0}, use_global_device_ids=true | all-gather | bytes 266240 | tf_op jit(solution)/shard_map/while/body/eval_jaxpr/all_gather | solution.py:52
  631.8 49.5 %all-gather.7 = f32[64,64,16]{1,2,0:T(8,128)S(1)} all-gather(f32[1,64,16]{1,2,0:T(8,128)S(1)} %bitcast.71), channel_id=1, replica_groups=mesh['sep'=8,'row'=8,'col'=8] {'row','col'}, dimensions={0}, use_global_device_ids=true | all-gather | bytes 266240 | tf_op jit(solution)/shard_map/while/body/eval_jaxpr/all_gather | solution.py:53
  684.0 1.9 collective-permute-start
  685.9 8.9 collective-permute-done
  695.0 48.8 %all-gather.6 = f32[64,64,16]{1,2,0:T(8,128)S(1)} all-gather(f32[1,64,16]{1,2,0:T(8,128)S(1)} %fusion.22), channel_id=1, replica_groups=mesh['sep'=8,'row'=8,'col'=8] {'row','col'}, dimensions={0}, use_global_device_ids=true | all-gather | bytes 266240 | tf_op jit(solution)/shard_map/while/body/eval_jaxpr/all_gather | solution.py:52
  746.0 49.5 %all-gather.7 = f32[64,64,16]{1,2,0:T(8,128)S(1)} all-gather(f32[1,64,16]{1,2,0:T(8,128)S(1)} %bitcast.71), channel_id=1, replica_groups=mesh['sep'=8,'row'=8,'col'=8] {'row','col'}, dimensions={0}, use_global_device_ids=true | all-gather | bytes 266240 | tf_op jit(solution)/shard_map/while/body/eval_jaxpr/all_gather | solution.py:53
  798.2 1.9 collective-permute-start
  800.1 8.9 collective-permute-done
  809.2 48.8 %all-gather.6 = f32[64,64,16]{1,2,0:T(8,128)S(1)} all-gather(f32[1,64,16]{1,2,0:T(8,128)S(1)} %fusion.22), channel_id=1, replica_groups=mesh['sep'=8,'row'=8,'col'=8] {'row','col'}, dimensions={0}, use_global_device_ids=true | all-gather | bytes 266240 | tf_op jit(solution)/shard_map/while/body/eval_jaxpr/all_gather | solution.py:52
  860.2 49.5 %all-gather.7 = f32[64,64,16]{1,2,0:T(8,128)S(1)} all-gather(f32[1,64,16]{1,2,0:T(8,128)S(1)} %bitcast.71), channel_id=1, replica_groups=mesh['sep'=8,'row'=8,'col'=8] {'row','col'}, dimensions={0}, use_global_device_ids=true | all-gather | bytes 266240 | tf_op jit(solution)/shard_map/while/body/eval_jaxpr/all_gather | solution.py:53
  912.4 1.9 collective-permute-start
  914.3 8.9 collective-permute-done
  923.4 48.8 %all-gather.6 = f32[64,64,16]{1,2,0:T(8,128)S(1)} all-gather(f32[1,64,16]{1,2,0:T(8,128)S(1)} %fusion.22), channel_id=1, replica_groups=mesh['sep'=8,'row'=8,'col'=8] {'row','col'}, dimensions={0}, use_global_device_ids=true | all-gather | bytes 266240 | tf_op jit(solution)/shard_map/while/body/eval_jaxpr/all_gather | solution.py:52
  974.4 49.5 %all-gather.7 = f32[64,64,16]{1,2,0:T(8,128)S(1)} all-gather(f32[1,64,16]{1,2,0:T(8,128)S(1)} %bitcast.71), channel_id=1, replica_groups=mesh['sep'=8,'row'=8,'col'=8] {'row','col'}, dimensions={0}, use_global_device_ids=true | all-gather | bytes 266240 | tf_op jit(solution)/shard_map/while/body/eval_jaxpr/all_gather | solution.py:53
  1026.6 1.9 collective-permute-start
  1028.5 8.9 collective-permute-done
  1037.6 48.8 %all-gather.6 = f32[64,64,16]{1,2,0:T(8,128)S(1)} all-gather(f32[1,64,16]{1,2,0:T(8,128)S(1)} %fusion.22), channel_id=1, replica_groups=mesh['sep'=8,'row'=8,'col'=8] {'row','col'}, dimensions={0}, use_global_device_ids=true | all-gather | bytes 266240 | tf_op jit(solution)/shard_map/while/body/eval_jaxpr/all_gather | solution.py:52
  1088.6 49.5 %all-gather.7 = f32[64,64,16]{1,2,0:T(8,128)S(1)} all-gather(f32[1,64,16]{1,2,0:T(8,128)S(1)} %bitcast.71), channel_id=1, replica_groups=mesh['sep'=8,'row'=8,'col'=8] {'row','col'}, dimensions={0}, use_global_device_ids=true | all-gather | bytes 266240 | tf_op jit(solution)/shard_map/while/body/eval_jaxpr/all_gather | solution.py:53
  1140.8 1.9 collective-permute-start
  1142.7 8.9 collective-permute-done
  1151.8 48.8 %all-gather.6 = f32[64,64,16]{1,2,0:T(8,128)S(1)} all-gather(f32[1,64,16]{1,2,0:T(8,128)S(1)} %fusion.22), channel_id=1, replica_groups=mesh['sep'=8,'row'=8,'col'=8] {'row','col'}, dimensions={0}, use_global_device_ids=true | all-gather | bytes 266240 | tf_op jit(solution)/shard_map/while/body/eval_jaxpr/all_gather | solution.py:52
  1202.8 49.5 %all-gather.7 = f32[64,64,16]{1,2,0:T(8,128)S(1)} all-gather(f32[1,64,16]{1,2,0:T(8,128)S(1)} %bitcast.71), channel_id=1, replica_groups=mesh['sep'=8,'row'=8,'col'=8] {'row','col'}, dimensions={0}, use_global_device_ids=true | all-gather | bytes 266240 | tf_op jit(solution)/shard_map/while/body/eval_jaxpr/all_gather | solution.py:53
  1255.0 1.9 collective-permute-start
  1256.9 8.9 collective-permute-done
  1266.0 48.8 %all-gather.6 = f32[64,64,16]{1,2,0:T(8,128)S(1)} all-gather(f32[1,64,16]{1,2,0:T(8,128)S(1)} %fusion.22), channel_id=1, replica_groups=mesh['sep'=8,'row'=8,'col'=8] {'row','col'}, dimensions={0}, use_global_device_ids=true | all-gather | bytes 266240 | tf_op jit(solution)/shard_map/while/body/eval_jaxpr/all_gather | solution.py:52
  1317.0 49.5 %all-gather.7 = f32[64,64,16]{1,2,0:T(8,128)S(1)} all-gather(f32[1,64,16]{1,2,0:T(8,128)S(1)} %bitcast.71), channel_id=1, replica_groups=mesh['sep'=8,'row'=8,'col'=8] {'row','col'}, dimensions={0}, use_global_device_ids=true | all-gather | bytes 266240 | tf_op jit(solution)/shard_map/while/body/eval_jaxpr/all_gather | solution.py:53
  1369.2 1.9 collective-permute-start
  1371.1 8.9 collective-permute-done
  1380.2 48.8 %all-gather.6 = f32[64,64,16]{1,2,0:T(8,128)S(1)} all-gather(f32[1,64,16]{1,2,0:T(8,128)S(1)} %fusion.22), channel_id=1, replica_groups=mesh['sep'=8,'row'=8,'col'=8] {'row','col'}, dimensions={0}, use_global_device_ids=true | all-gather | bytes 266240 | tf_op jit(solution)/shard_map/while/body/eval_jaxpr/all_gather | solution.py:52
  1431.2 49.5 %all-gather.7 = f32[64,64,16]{1,2,0:T(8,128)S(1)} all-gather(f32[1,64,16]{1,2,0:T(8,128)S(1)} %bitcast.71), channel_id=1, replica_groups=mesh['sep'=8,'row'=8,'col'=8] {'row','col'}, dimensions={0}, use_global_device_ids=true | all-gather | bytes 266240 | tf_op jit(solution)/shard_map/while/body/eval_jaxpr/all_gather | solution.py:53
  1483.4 1.9 collective-permute-start
  1485.3 8.9 collective-permute-done
  1494.4 48.8 %all-gather.6 = f32[64,64,16]{1,2,0:T(8,128)S(1)} all-gather(f32[1,64,16]{1,2,0:T(8,128)S(1)} %fusion.22), channel_id=1, replica_groups=mesh['sep'=8,'row'=8,'col'=8] {'row','col'}, dimensions={0}, use_global_device_ids=true | all-gather | bytes 266240 | tf_op jit(solution)/shard_map/while/body/eval_jaxpr/all_gather | solution.py:52
  1545.4 49.5 %all-gather.7 = f32[64,64,16]{1,2,0:T(8,128)S(1)} all-gather(f32[1,64,16]{1,2,0:T(8,128)S(1)} %bitcast.71), channel_id=1, replica_groups=mesh['sep'=8,'row'=8,'col'=8] {'row','col'}, dimensions={0}, use_global_device_ids=true | all-gather | bytes 266240 | tf_op jit(solution)/shard_map/while/body/eval_jaxpr/all_gather | solution.py:53
  1597.6 1.9 collective-permute-start
  1599.6 8.9 collective-permute-done
  1608.7 48.8 %all-gather.6 = f32[64,64,16]{1,2,0:T(8,128)S(1)} all-gather(f32[1,64,16]{1,2,0:T(8,128)S(1)} %fusion.22), channel_id=1, replica_groups=mesh['sep'=8,'row'=8,'col'=8] {'row','col'}, dimensions={0}, use_global_device_ids=true | all-gather | bytes 266240 | tf_op jit(solution)/shard_map/while/body/eval_jaxpr/all_gather | solution.py:52
  1659.6 49.5 %all-gather.7 = f32[64,64,16]{1,2,0:T(8,128)S(1)} all-gather(f32[1,64,16]{1,2,0:T(8,128)S(1)} %bitcast.71), channel_id=1, replica_groups=mesh['sep'=8,'row'=8,'col'=8] {'row','col'}, dimensions={0}, use_global_device_ids=true | all-gather | bytes 266240 | tf_op jit(solution)/shard_map/while/body/eval_jaxpr/all_gather | solution.py:53
  1711.8 1.9 collective-permute-start
  1713.8 8.9 collective-permute-done
  1722.9 48.8 %all-gather.6 = f32[64,64,16]{1,2,0:T(8,128)S(1)} all-gather(f32[1,64,16]{1,2,0:T(8,128)S(1)} %fusion.22), channel_id=1, replica_groups=mesh['sep'=8,'row'=8,'col'=8] {'row','col'}, dimensions={0}, use_global_device_ids=true | all-gather | bytes 266240 | tf_op jit(solution)/shard_map/while/body/eval_jaxpr/all_gather | solution.py:52
  1773.8 49.5 %all-gather.7 = f32[64,64,16]{1,2,0:T(8,128)S(1)} all-gather(f32[1,64,16]{1,2,0:T(8,128)S(1)} %bitcast.71), channel_id=1, replica_groups=mesh['sep'=8,'row'=8,'col'=8] {'row','col'}, dimensions={0}, use_global_device_ids=true | all-gather | bytes 266240 | tf_op jit(solution)/shard_map/while/body/eval_jaxpr/all_gather | solution.py:53
  1828.0 8.9 collective-permute-done
  (298 shorter events, 83.6 us)
Async XLA Ops:
  0.0 0.7 copy-start.4
  0.7 0.7 copy-start.3
  58.6 1.2 copy-start
  110.4 1.0 copy-start.1
  113.0 10.8 collective-permute-start
  172.8 1.2 copy-start
  224.6 1.0 copy-start.1
  227.2 10.8 collective-permute-start
  287.0 1.2 copy-start
  338.9 1.0 copy-start.1
  341.4 10.8 collective-permute-start
  401.2 1.2 copy-start
  453.1 1.0 copy-start.1
  455.6 10.8 collective-permute-start
  515.4 1.2 copy-start
  567.3 1.0 copy-start.1
  569.8 10.8 collective-permute-start
  629.6 1.2 copy-start
  681.5 1.0 copy-start.1
  684.0 10.8 collective-permute-start
  743.8 1.2 copy-start
  795.7 1.0 copy-start.1
  798.2 10.8 collective-permute-start
  858.0 1.2 copy-start
  909.9 1.0 copy-start.1
  912.4 10.8 collective-permute-start
  972.2 1.2 copy-start
  1024.1 1.0 copy-start.1
  1026.6 10.8 collective-permute-start
  1086.4 1.2 copy-start
  1138.3 1.0 copy-start.1
  1140.8 10.8 collective-permute-start
  1200.6 1.2 copy-start
  1252.5 1.0 copy-start.1
  1255.0 10.8 collective-permute-start
  1314.8 1.2 copy-start
  1366.7 1.0 copy-start.1
  1369.2 10.8 collective-permute-start
  1429.1 1.2 copy-start
  1480.9 1.0 copy-start.1
  1483.4 10.8 collective-permute-start
  1543.3 1.2 copy-start
  1595.1 1.0 copy-start.1
  1597.6 10.8 collective-permute-start
  1657.5 1.2 copy-start
  1709.3 1.0 copy-start.1
  1711.8 10.8 collective-permute-start
  1771.7 1.2 copy-start
  1823.5 1.0 copy-start.1
  1826.0 10.8 collective-permute-start
  1836.9 0.6 copy-start.2
where the time goes:
time: 1840 us
  blocking collectives  1580 us (86%)
  waiting for transfers between devices  142 us (8%)
  local copies, waits for them, and re-layouts  33.2 us (2%)
  starting transfers between devices  31.1 us (2%)
  other arithmetic  25.5 us (1%)
  matrix products  23 us (1%)
    all_gather x16, blocking collectives, one_turn(): lax.all_gather(solved, ('row', 'col'), axis=1, tiled=True)  792 us
    all_gather x16, blocking collectives, one_turn(): lax.all_gather(resid, ('row', 'col'), axis=1, tiled=True)  789 us
    ppermute x16, waiting for transfers between devices, passed_along(): return lax.ppermute(block, axis, route)  142 us
  transfers between devices with their start and end apart: 16, of which 16 were waited for; matrix products, arithmetic and copies ran while one was open for 0% of the time, Pallas kernels for 0%

commit v1 on v0

v1 whole, which is shorter than its diff:
```python
import jax
import jax.numpy as jnp
from jax import lax
from jax.sharding import PartitionSpec as P


def passed_along(block, axis, distance):
    devices = range(lax.axis_size(axis))
    route = [(i - distance, i) for i in devices if i - distance in devices]
    return lax.ppermute(block, axis, route)


def shards(right_sides, inverse_diag, lower_blocks, targets, counts):
    levels = lax.axis_size("sep")
    own_level = lax.axis_index("sep")
    batches, width_rhs, own_rows = right_sides.shape
    width = inverse_diag.shape[-1]
    given = right_sides.reshape(batches * width_rhs, own_rows)
    diag_rows = inverse_diag[0]
    lower_rows = lower_blocks[0]
    lower_count = lower_rows.shape[0]
    live = jnp.arange(lower_count, dtype=jnp.int32) < counts[0, 0]
    places = targets[0] // width * own_rows + targets[0] % own_rows

    def solve_piece(segment):
        return lax.dot_general(
            segment,
            diag_rows,
            (((1,), (1,)), ((), ())),
            precision=lax.Precision.HIGHEST,
            preferred_element_type=jnp.float32,
        )

    def lower_piece(segment):
        return lax.dot_general(
            segment,
            lower_rows,
            (((1,), (1,)), ((), ())),
            precision=lax.Precision.HIGHEST,
            preferred_element_type=jnp.float32,
        )

    def one_level(level, state):
        carried, solution = state
        resid = given - lax.dynamic_slice_in_dim(carried, level * own_rows, own_rows, 1)
        solved = solve_piece(lax.all_gather(resid, ("row", "col"), axis=1, tiled=True))
        solution = jnp.where(own_level == level, solved, solution)
        update = lower_piece(lax.all_gather(solved, ("row", "col"), axis=1, tiled=True))
        update = jnp.where(live[None, :], update, jnp.float32(0.0))
        carried = carried.at[:, places].add(update)
        return passed_along(carried, "sep", 1), solution

    carried = jnp.zeros((given.shape[0], levels * own_rows), jnp.float32)
    solution = jnp.zeros_like(given)
    carried, solution = lax.fori_loop(0, levels - 1, one_level, (carried, solution))
    last = levels - 1
    resid = given - carried[:, last * own_rows:]
    solved = solve_piece(lax.all_gather(resid, ("row", "col"), axis=1, tiled=True))
    solution = jnp.where(own_level == last, solved, solution)
    return solution.reshape(batches, width_rhs, own_rows)


def solution(mesh):
    placed = (
        P(None, None, ("sep", "row", "col")),
        P("sep", ("row", "col"), None),
        P("sep", ("row", "col"), None),
        P("sep", ("row", "col")),
        P("sep", ("row", "col")),
    )
    return jax.shard_map(
        shards,
        mesh=mesh,
        in_specs=placed,
        out_specs=P(None, None, ("sep", "row", "col")),
        check_vma=False,
    )
```

time: 1840 us -> 873 us (0.47)
  blocking collectives: 1580 us -> 746 us
  waiting for transfers between devices: 142 us -> 61.8 us
    all_gather x32 -> x15, blocking collectives: 1580 us -> 746 us  [the longest x7 350 us: one_level(): lax.all_gather(resid, ('row', 'col'), axis=1, tiled=True)]
    ppermute x16 -> x7, waiting for transfers between devices: 142 us -> 61.8 us  [passed_along(): return lax.ppermute(block, axis, route)]
  transfers between devices with their start and end apart: 16 -> 7, of which waited for: 16 -> 7; matrix products, arithmetic and copies ran while one was open for 0% -> 0% of each run, Pallas kernels for 0% -> 0%
where the time goes in v1:
time: 873 us; the launch traced here: 872 us
  blocking collectives  746 us (85%)
  waiting for transfers between devices  61.8 us (7%)
  local copies, waits for them, and re-layouts  25.6 us (3%)
  starting transfers between devices  13.8 us (2%)
  matrix products  12.1 us (1%)
  other arithmetic  11.3 us (1%)
    all_gather x7, blocking collectives, one_level(): lax.all_gather(resid, ('row', 'col'), axis=1, tiled=True)  350 us
    all_gather x7, blocking collectives, one_level(): lax.all_gather(solved, ('row', 'col'), axis=1, tiled=True)  347 us
    ppermute x7, waiting for transfers between devices, passed_along(): return lax.ppermute(block, axis, route)  61.8 us
    all_gather x1, blocking collectives, shards(): lax.all_gather(resid, ('row', 'col'), axis=1, tiled=True)  49 us
  transfers between devices with their start and end apart: 7, of which 7 were waited for; matrix products, arithmetic and copies ran while one was open for 0% of the time, Pallas kernels for 0%

profile of v1, /device:TPU:33, one launch (start us, length us, event | category | flops | bytes accessed | tf_op | source)
XLA Modules:
  0.0 871.5 jit_solution(13566988338382411557)
XLA Ops:
  0.0 0.8 copy.29
  0.8 0.6 copy-done.4
  1.5 816.8 %while.16 = (s32[]{:T(128)}, f32[32,512]{0,1:T(8,128)S(1)}, f32[32,64]{1,0:T(8,128)S(1)}, s32[32]{0:T(128)S(1)}, f32[32,64]{0,1:T(8,128)S(1)}, /*index=5*/f32[64...) while((s32[]{:T(128)}, f32[32,512]{0,1:T(8,128)S(1)}, ...), condition=%wide.region_2.3_spmd.clone, body=%wide.region_0.2_spmd.clone.sunk | while | flops 151003264 | bytes 14787303 | solution.py:55
  1.8 57.0 %all-gather.7 = f32[64,64,32]{1,2,0:T(8,128)S(1)} all-gather(f32[1,64,32]{1,2,0:T(8,128)S(1)} %subtract_bitcast_fusion.2), channel_id=1, replica_groups=mesh['sep'=8,'row'=8,'col'=8] {'row','col'}, dimensions={0}, use_global_device_ids=true | all-gather | bytes 532480 | tf_op jit(solution)/shard_map/while/body/eval_jaxpr/all_gather | solution.py:46
  58.8 0.6 copy.39
  59.8 0.9 copy-done
  60.7 1.0 select_select_fusion.2
  61.6 49.6 %all-gather.8 = f32[64,64,32]{1,2,0:T(8,128)S(1)} all-gather(f32[1,64,32]{1,2,0:T(8,128)S(1)} %bitcast.68), channel_id=1, replica_groups=mesh['sep'=8,'row'=8,'col'=8] {'row','col'}, dimensions={0}, use_global_device_ids=true | all-gather | bytes 532480 | tf_op jit(solution)/shard_map/while/body/eval_jaxpr/all_gather | solution.py:48
  111.2 0.6 copy.40
  112.2 0.6 iota_compare_fusion.2
  113.5 0.9 scatter_fusion
  114.4 2.3 collective-permute-start
  116.7 8.5 collective-permute-done
  125.5 48.8 %all-gather.7 = f32[64,64,32]{1,2,0:T(8,128)S(1)} all-gather(f32[1,64,32]{1,2,0:T(8,128)S(1)} %subtract_bitcast_fusion.2), channel_id=1, replica_groups=mesh['sep'=8,'row'=8,'col'=8] {'row','col'}, dimensions={0}, use_global_device_ids=true | all-gather | bytes 532480 | tf_op jit(solution)/shard_map/while/body/eval_jaxpr/all_gather | solution.py:46
  175.3 0.9 copy-done
  176.2 1.0 select_select_fusion.2
  177.1 49.6 %all-gather.8 = f32[64,64,32]{1,2,0:T(8,128)S(1)} all-gather(f32[1,64,32]{1,2,0:T(8,128)S(1)} %bitcast.68), channel_id=1, replica_groups=mesh['sep'=8,'row'=8,'col'=8] {'row','col'}, dimensions={0}, use_global_device_ids=true | all-gather | bytes 532480 | tf_op jit(solution)/shard_map/while/body/eval_jaxpr/all_gather | solution.py:48
  227.7 0.6 iota_compare_fusion.2
  229.0 0.9 scatter_fusion
  229.9 1.9 collective-permute-start
  231.8 8.9 %collective-permute-done = f32[32,512]{0,1:T(8,128)S(1)} collective-permute-done((f32[32,512]{0,1:T(8,128)S(1)}, f32[32,512]{0,1:T(8,128)S(1)}, u32[]{:S(2)}, u32[]{:S(2)}) %collective-permute-start) | collective-permute-done | bytes 65568 | tf_op jit(solution)/shard_map/while/body/eval_jaxpr/ppermute | solution.py:10
  241.0 48.8 %all-gather.7 = f32[64,64,32]{1,2,0:T(8,128)S(1)} all-gather(f32[1,64,32]{1,2,0:T(8,128)S(1)} %subtract_bitcast_fusion.2), channel_id=1, replica_groups=mesh['sep'=8,'row'=8,'col'=8] {'row','col'}, dimensions={0}, use_global_device_ids=true | all-gather | bytes 532480 | tf_op jit(solution)/shard_map/while/body/eval_jaxpr/all_gather | solution.py:46
  290.8 0.9 copy-done
  291.7 1.0 select_select_fusion.2
  292.6 49.6 %all-gather.8 = f32[64,64,32]{1,2,0:T(8,128)S(1)} all-gather(f32[1,64,32]{1,2,0:T(8,128)S(1)} %bitcast.68), channel_id=1, replica_groups=mesh['sep'=8,'row'=8,'col'=8] {'row','col'}, dimensions={0}, use_global_device_ids=true | all-gather | bytes 532480 | tf_op jit(solution)/shard_map/while/body/eval_jaxpr/all_gather | solution.py:48
  343.2 0.6 iota_compare_fusion.2
  344.5 0.9 scatter_fusion
  345.4 1.9 collective-permute-start
  347.3 8.9 %collective-permute-done = f32[32,512]{0,1:T(8,128)S(1)} collective-permute-done((f32[32,512]{0,1:T(8,128)S(1)}, f32[32,512]{0,1:T(8,128)S(1)}, u32[]{:S(2)}, u32[]{:S(2)}) %collective-permute-start) | collective-permute-done | bytes 65568 | tf_op jit(solution)/shard_map/while/body/eval_jaxpr/ppermute | solution.py:10
  356.5 48.8 %all-gather.7 = f32[64,64,32]{1,2,0:T(8,128)S(1)} all-gather(f32[1,64,32]{1,2,0:T(8,128)S(1)} %subtract_bitcast_fusion.2), channel_id=1, replica_groups=mesh['sep'=8,'row'=8,'col'=8] {'row','col'}, dimensions={0}, use_global_device_ids=true | all-gather | bytes 532480 | tf_op jit(solution)/shard_map/while/body/eval_jaxpr/all_gather | solution.py:46
  406.4 0.9 copy-done
  407.2 1.0 select_select_fusion.2
  408.2 49.6 %all-gather.8 = f32[64,64,32]{1,2,0:T(8,128)S(1)} all-gather(f32[1,64,32]{1,2,0:T(8,128)S(1)} %bitcast.68), channel_id=1, replica_groups=mesh['sep'=8,'row'=8,'col'=8] {'row','col'}, dimensions={0}, use_global_device_ids=true | all-gather | bytes 532480 | tf_op jit(solution)/shard_map/while/body/eval_jaxpr/all_gather | solution.py:48
  458.8 0.6 iota_compare_fusion.2
  460.1 0.9 scatter_fusion
  460.9 1.9 collective-permute-start
  462.9 8.9 %collective-permute-done = f32[32,512]{0,1:T(8,128)S(1)} collective-permute-done((f32[32,512]{0,1:T(8,128)S(1)}, f32[32,512]{0,1:T(8,128)S(1)}, u32[]{:S(2)}, u32[]{:S(2)}) %collective-permute-start) | collective-permute-done | bytes 65568 | tf_op jit(solution)/shard_map/while/body/eval_jaxpr/ppermute | solution.py:10
  472.0 48.8 %all-gather.7 = f32[64,64,32]{1,2,0:T(8,128)S(1)} all-gather(f32[1,64,32]{1,2,0:T(8,128)S(1)} %subtract_bitcast_fusion.2), channel_id=1, replica_groups=mesh['sep'=8,'row'=8,'col'=8] {'row','col'}, dimensions={0}, use_global_device_ids=true | all-gather | bytes 532480 | tf_op jit(solution)/shard_map/while/body/eval_jaxpr/all_gather | solution.py:46
  521.9 0.9 copy-done
  522.7 1.0 select_select_fusion.2
  523.7 49.6 %all-gather.8 = f32[64,64,32]{1,2,0:T(8,128)S(1)} all-gather(f32[1,64,32]{1,2,0:T(8,128)S(1)} %bitcast.68), channel_id=1, replica_groups=mesh['sep'=8,'row'=8,'col'=8] {'row','col'}, dimensions={0}, use_global_device_ids=true | all-gather | bytes 532480 | tf_op jit(solution)/shard_map/while/body/eval_jaxpr/all_gather | solution.py:48
  574.3 0.6 iota_compare_fusion.2
  575.6 0.9 scatter_fusion
  576.4 1.9 collective-permute-start
  578.4 8.9 %collective-permute-done = f32[32,512]{0,1:T(8,128)S(1)} collective-permute-done((f32[32,512]{0,1:T(8,128)S(1)}, f32[32,512]{0,1:T(8,128)S(1)}, u32[]{:S(2)}, u32[]{:S(2)}) %collective-permute-start) | collective-permute-done | bytes 65568 | tf_op jit(solution)/shard_map/while/body/eval_jaxpr/ppermute | solution.py:10
  587.6 48.8 %all-gather.7 = f32[64,64,32]{1,2,0:T(8,128)S(1)} all-gather(f32[1,64,32]{1,2,0:T(8,128)S(1)} %subtract_bitcast_fusion.2), channel_id=1, replica_groups=mesh['sep'=8,'row'=8,'col'=8] {'row','col'}, dimensions={0}, use_global_device_ids=true | all-gather | bytes 532480 | tf_op jit(solution)/shard_map/while/body/eval_jaxpr/all_gather | solution.py:46
  637.4 0.9 copy-done
  638.2 1.0 select_select_fusion.2
  639.2 49.6 %all-gather.8 = f32[64,64,32]{1,2,0:T(8,128)S(1)} all-gather(f32[1,64,32]{1,2,0:T(8,128)S(1)} %bitcast.68), channel_id=1, replica_groups=mesh['sep'=8,'row'=8,'col'=8] {'row','col'}, dimensions={0}, use_global_device_ids=true | all-gather | bytes 532480 | tf_op jit(solution)/shard_map/while/body/eval_jaxpr/all_gather | solution.py:48
  689.8 0.6 iota_compare_fusion.2
  691.1 0.9 scatter_fusion
  692.0 1.9 collective-permute-start
  693.9 8.9 %collective-permute-done = f32[32,512]{0,1:T(8,128)S(1)} collective-permute-done((f32[32,512]{0,1:T(8,128)S(1)}, f32[32,512]{0,1:T(8,128)S(1)}, u32[]{:S(2)}, u32[]{:S(2)}) %collective-permute-start) | collective-permute-done | bytes 65568 | tf_op jit(solution)/shard_map/while/body/eval_jaxpr/ppermute | solution.py:10
  703.1 48.8 %all-gather.7 = f32[64,64,32]{1,2,0:T(8,128)S(1)} all-gather(f32[1,64,32]{1,2,0:T(8,128)S(1)} %subtract_bitcast_fusion.2), channel_id=1, replica_groups=mesh['sep'=8,'row'=8,'col'=8] {'row','col'}, dimensions={0}, use_global_device_ids=true | all-gather | bytes 532480 | tf_op jit(solution)/shard_map/while/body/eval_jaxpr/all_gather | solution.py:46
  752.9 0.9 copy-done
  753.7 1.0 select_select_fusion.2
  754.7 49.6 %all-gather.8 = f32[64,64,32]{1,2,0:T(8,128)S(1)} all-gather(f32[1,64,32]{1,2,0:T(8,128)S(1)} %bitcast.68), channel_id=1, replica_groups=mesh['sep'=8,'row'=8,'col'=8] {'row','col'}, dimensions={0}, use_global_device_ids=true | all-gather | bytes 532480 | tf_op jit(solution)/shard_map/while/body/eval_jaxpr/all_gather | solution.py:48
  805.3 0.6 iota_compare_fusion.2
  806.6 0.9 scatter_fusion
  807.5 1.9 collective-permute-start
  809.4 8.9 %collective-permute-done = f32[32,512]{0,1:T(8,128)S(1)} collective-permute-done((f32[32,512]{0,1:T(8,128)S(1)}, f32[32,512]{0,1:T(8,128)S(1)}, u32[]{:S(2)}, u32[]{:S(2)}) %collective-permute-start) | collective-permute-done | bytes 65568 | tf_op jit(solution)/shard_map/while/body/eval_jaxpr/ppermute | solution.py:10
  819.1 49.0 %all-gather.2 = f32[64,64,32]{1,2,0:T(8,128)S(1)} all-gather(f32[1,64,32]{1,2,0:T(8,128)S(1)} %fusion.4), channel_id=1, replica_groups=mesh['sep'=8,'row'=8,'col'=8] {'row','col'}, dimensions={0}, use_global_device_ids=true | all-gather | bytes 532480 | tf_op jit(solution)/shard_map/all_gather | solution.py:58
  869.1 0.9 copy-done.1
  870.0 1.6 convolution_select_fusion.1
  (107 shorter events, 20.6 us)
Async XLA Ops:
  0.8 0.7 copy-start.4
  59.4 1.2 copy-start
  111.8 1.0 copy-start.2
  114.4 10.8 %collective-permute-start = (f32[32,512]{0,1:T(8,128)S(1)}, f32[32,512]{0,1:T(8,128)S(1)}, u32[]{:S(2)}, u32[]{:S(2)}) collective-permute-start(f32[32,512]{0,1:T(8,128)S(1)} %scatter_fusion), channel_id=1, source_target_pairs={{0,64},{64,128},{128,192},{192,256},{256,320},{320,384},{384,448},... | collective-permute-start | bytes 196616 | tf_op jit(solution)/shard_map/while/body/eval_jaxpr/ppermute | solution.py:10
  174.9 1.2 copy-start
  227.4 1.0 copy-start.2
  229.9 10.8 %collective-permute-start = (f32[32,512]{0,1:T(8,128)S(1)}, f32[32,512]{0,1:T(8,128)S(1)}, u32[]{:S(2)}, u32[]{:S(2)}) collective-permute-start(f32[32,512]{0,1:T(8,128)S(1)} %scatter_fusion), channel_id=1, source_target_pairs={{0,64},{64,128},{128,192},{192,256},{256,320},{320,384},{384,448},... | collective-permute-start | bytes 196616 | tf_op jit(solution)/shard_map/while/body/eval_jaxpr/ppermute | solution.py:10
  290.5 1.2 copy-start
  342.9 1.0 copy-start.2
  345.4 10.8 %collective-permute-start = (f32[32,512]{0,1:T(8,128)S(1)}, f32[32,512]{0,1:T(8,128)S(1)}, u32[]{:S(2)}, u32[]{:S(2)}) collective-permute-start(f32[32,512]{0,1:T(8,128)S(1)} %scatter_fusion), channel_id=1, source_target_pairs={{0,64},{64,128},{128,192},{192,256},{256,320},{320,384},{384,448},... | collective-permute-start | bytes 196616 | tf_op jit(solution)/shard_map/while/body/eval_jaxpr/ppermute | solution.py:10
  406.0 1.2 copy-start
  458.4 1.0 copy-start.2
  460.9 10.8 %collective-permute-start = (f32[32,512]{0,1:T(8,128)S(1)}, f32[32,512]{0,1:T(8,128)S(1)}, u32[]{:S(2)}, u32[]{:S(2)}) collective-permute-start(f32[32,512]{0,1:T(8,128)S(1)} %scatter_fusion), channel_id=1, source_target_pairs={{0,64},{64,128},{128,192},{192,256},{256,320},{320,384},{384,448},... | collective-permute-start | bytes 196616 | tf_op jit(solution)/shard_map/while/body/eval_jaxpr/ppermute | solution.py:10
  521.5 1.2 copy-start
  573.9 1.0 copy-start.2
  576.4 10.8 %collective-permute-start = (f32[32,512]{0,1:T(8,128)S(1)}, f32[32,512]{0,1:T(8,128)S(1)}, u32[]{:S(2)}, u32[]{:S(2)}) collective-permute-start(f32[32,512]{0,1:T(8,128)S(1)} %scatter_fusion), channel_id=1, source_target_pairs={{0,64},{64,128},{128,192},{192,256},{256,320},{320,384},{384,448},... | collective-permute-start | bytes 196616 | tf_op jit(solution)/shard_map/while/body/eval_jaxpr/ppermute | solution.py:10
  637.0 1.2 copy-start
  689.4 1.0 copy-start.2
  692.0 10.8 %collective-permute-start = (f32[32,512]{0,1:T(8,128)S(1)}, f32[32,512]{0,1:T(8,128)S(1)}, u32[]{:S(2)}, u32[]{:S(2)}) collective-permute-start(f32[32,512]{0,1:T(8,128)S(1)} %scatter_fusion), channel_id=1, source_target_pairs={{0,64},{64,128},{128,192},{192,256},{256,320},{320,384},{384,448},... | collective-permute-start | bytes 196616 | tf_op jit(solution)/shard_map/while/body/eval_jaxpr/ppermute | solution.py:10
  752.5 1.2 copy-start
  804.9 1.0 copy-start.2
  807.5 10.8 %collective-permute-start = (f32[32,512]{0,1:T(8,128)S(1)}, f32[32,512]{0,1:T(8,128)S(1)}, u32[]{:S(2)}, u32[]{:S(2)}) collective-permute-start(f32[32,512]{0,1:T(8,128)S(1)} %scatter_fusion), channel_id=1, source_target_pairs={{0,64},{64,128},{128,192},{192,256},{256,320},{320,384},{384,448},... | collective-permute-start | bytes 196616 | tf_op jit(solution)/shard_map/while/body/eval_jaxpr/ppermute | solution.py:10
  818.3 0.7 copy-start.3
  868.7 1.2 copy-start.1

commit v2 on v1

--- a/solution.py
+++ b/solution.py
@@ -8,6 +8,15 @@
     devices = range(lax.axis_size(axis))
     route = [(i - distance, i) for i in devices if i - distance in devices]
     return lax.ppermute(block, axis, route)
+
+
+def gathered(block, axes):
+    parts = 1
+    for axis in axes:
+        parts *= lax.axis_size(axis)
+    copies = jnp.broadcast_to(block[None], (parts,) + block.shape)
+    pieces = lax.all_to_all(copies, axes, 0, 0, tiled=True)
+    return jnp.transpose(pieces, (1, 0, 2)).reshape(block.shape[0], parts * block.shape[1])
 
 
 def shards(right_sides, inverse_diag, lower_blocks, targets, counts):
@@ -43,9 +52,9 @@
     def one_level(level, state):
         carried, solution = state
         resid = given - lax.dynamic_slice_in_dim(carried, level * own_rows, own_rows, 1)
-        solved = solve_piece(lax.all_gather(resid, ("row", "col"), axis=1, tiled=True))
+        solved = solve_piece(gathered(resid, ("row", "col")))
         solution = jnp.where(own_level == level, solved, solution)
-        update = lower_piece(lax.all_gather(solved, ("row", "col"), axis=1, tiled=True))
+        update = lower_piece(gathered(solved, ("row", "col")))
         update = jnp.where(live[None, :], update, jnp.float32(0.0))
         carried = carried.at[:, places].add(update)
         return passed_along(carried, "sep", 1), solution
@@ -55,7 +64,7 @@
     carried, solution = lax.fori_loop(0, levels - 1, one_level, (carried, solution))
     last = levels - 1
     resid = given - carried[:, last * own_rows:]
-    solved = solve_piece(lax.all_gather(resid, ("row", "col"), axis=1, tiled=True))
+    solved = solve_piece(gathered(resid, ("row", "col")))
     solution = jnp.where(own_level == last, solved, solution)
     return solution.reshape(batches, width_rhs, own_rows)
 

time: 873 us -> 554 us (0.63)
  blocking collectives: 746 us -> 0 us
  waiting for transfers between devices: 61.8 us -> 321 us
  starting transfers between devices: 13.8 us -> 111 us
  local copies, waits for them, and re-layouts: 25.6 us -> 67.8 us
  other arithmetic: 11.3 us -> 38.9 us
    all_gather x15 -> x0, blocking collectives: 746 us -> none  [the longest x7 350 us: one_level(): lax.all_gather(resid, ('row', 'col'), axis=1, tiled=True)]
    all_to_all x0 -> x15, waiting for transfers between devices: none -> 261 us  [gathered(): pieces = lax.all_to_all(copies, axes, 0, 0, tiled=True)]
    all_to_all x0 -> x15, starting transfers between devices: none -> 97.1 us  [gathered(): pieces = lax.all_to_all(copies, axes, 0, 0, tiled=True)]
    all_to_all x0 -> x15, other arithmetic: none -> 28 us  [gathered(): pieces = lax.all_to_all(copies, axes, 0, 0, tiled=True)]
    while x63, local copies, waits for them, and re-layouts: 12.5 us -> 36.9 us
    transpose x0 -> x15, local copies, waits for them, and re-layouts: none -> 9.2 us  [gathered(): jnp.transpose(pieces, (1, 0, 2))]
    all_gather x15 -> x0, local copies, waits for them, and re-layouts: 9.17 us -> none  [the longest x7 4.28 us: one_level(): lax.all_gather(resid, ('row', 'col'), axis=1, tiled=True)]
  transfers between devices with their start and end apart: 7 -> 22, of which waited for: 7 -> 22; matrix products, arithmetic and copies ran while one was open for 0% -> 1% of each run, Pallas kernels for 0% -> 0%
where the time goes in v2:
time: 554 us; the launch traced here: 552 us
  waiting for transfers between devices  321 us (58%)
  starting transfers between devices  111 us (20%)
  local copies, waits for them, and re-layouts  67.8 us (12%)
  other arithmetic  38.9 us (7%)
  matrix products  12.1 us (2%)
    all_to_all x15, waiting for transfers between devices, gathered(): pieces = lax.all_to_all(copies, axes, 0, 0, tiled=True)  261 us
    all_to_all x15, starting transfers between devices, gathered(): pieces = lax.all_to_all(copies, axes, 0, 0, tiled=True)  97.1 us
    ppermute x7, waiting for transfers between devices, passed_along(): return lax.ppermute(block, axis, route)  60.2 us
    while x63, local copies, waits for them, and re-layouts  36.9 us
    all_to_all x15, other arithmetic, gathered(): pieces = lax.all_to_all(copies, axes, 0, 0, tiled=True)  28 us
    ppermute x7, starting transfers between devices, passed_along(): return lax.ppermute(block, axis, route)  13.8 us
  transfers between devices with their start and end apart: 22, of which 22 were waited for; matrix products, arithmetic and copies ran while one was open for 1% of the time, Pallas kernels for 0%

profile of v2, /device:TPU:33, one launch (start us, length us, event | category | flops | bytes accessed | tf_op | source)
XLA Modules:
  0.0 551.8 jit_solution(12718540696505050372)
XLA Ops:
  1.5 517.8 %while.16 = (s32[]{:T(128)}, f32[32,512]{0,1:T(8,128)S(1)}, f32[32,64]{1,0:T(8,128)S(1)}, s32[32]{0:T(128)S(1)}, f32[32,64]{0,1:T(8,128)S(1)}, /*index=5*/f32[64...) while((s32[]{:T(128)}, f32[32,512]{0,1:T(8,128)S(1)}, ...), condition=%wide.region_2.3_spmd.clone, body=%wide.region_0.2_spmd.clone.sunk | while | flops 151003264 | bytes 24093520 | solution.py:64
  1.7 1.5 reshape.77
  3.2 14.0 %all-to-all-start = ((f32[64,1,2048]{2,1,0:T(1,128)}), f32[64,1,2048]{2,1,0:T(1,128)S(1)}, u32[]{:S(2)}, u32[]{:S(2)}) async-start(f32[64,1,2048]{2,1,0:T(1,128)} %reshape.77), calls=%async_computation | async-start | bytes 1048576 | tf_op jit(solution)/shard_map/while/body/eval_jaxpr/all_to_all | solution.py:18
  17.2 17.7 %all-to-all-done = f32[64,1,2048]{2,1,0:T(1,128)S(1)} async-done(((f32[64,1,2048]{2,1,0:T(1,128)}), f32[64,1,2048]{2,1,0:T(1,128)S(1)}, u32[]{:S(2)}, u32[]{:S(2)}) %all-to-all-start) | async-done | bytes 524320 | tf_op jit(solution)/shard_map/while/body/eval_jaxpr/all_to_all | solution.py:18
  35.5 1.9 reduce.5
  40.7 1.5 reshape.80
  42.1 5.7 %all-to-all-start.1 = ((f32[64,1,2048]{2,1,0:T(1,128)}), f32[64,1,2048]{2,1,0:T(1,128)S(1)}, u32[]{:S(2)}, u32[]{:S(2)}) async-start(f32[64,1,2048]{2,1,0:T(1,128)} %reshape.80), calls=%async_computation.1 | async-start | bytes 1048576 | tf_op jit(solution)/shard_map/while/body/eval_jaxpr/all_to_all | solution.py:18
  48.5 17.0 %all-to-all-done.1 = f32[64,1,2048]{2,1,0:T(1,128)S(1)} async-done(((f32[64,1,2048]{2,1,0:T(1,128)}), f32[64,1,2048]{2,1,0:T(1,128)S(1)}, u32[]{:S(2)}, u32[]{:S(2)}) %all-to-all-start.1) | async-done | bytes 524320 | tf_op jit(solution)/shard_map/while/body/eval_jaxpr/all_to_all | solution.py:18
  66.1 1.9 reduce.6
  71.6 2.3 collective-permute-start
  73.9 8.3 %collective-permute-done = f32[32,512]{0,1:T(8,128)S(1)} collective-permute-done((f32[32,512]{0,1:T(8,128)S(1)}, f32[32,512]{0,1:T(8,128)S(1)}, u32[]{:S(2)}, u32[]{:S(2)}) %collective-permute-start) | collective-permute-done | bytes 65568 | tf_op jit(solution)/shard_map/while/body/eval_jaxpr/ppermute | solution.py:10
  82.4 1.5 reshape.77
  83.9 6.2 %all-to-all-start = ((f32[64,1,2048]{2,1,0:T(1,128)}), f32[64,1,2048]{2,1,0:T(1,128)S(1)}, u32[]{:S(2)}, u32[]{:S(2)}) async-start(f32[64,1,2048]{2,1,0:T(1,128)} %reshape.77), calls=%async_computation | async-start | bytes 1048576 | tf_op jit(solution)/shard_map/while/body/eval_jaxpr/all_to_all | solution.py:18
  90.1 17.7 %all-to-all-done = f32[64,1,2048]{2,1,0:T(1,128)S(1)} async-done(((f32[64,1,2048]{2,1,0:T(1,128)}), f32[64,1,2048]{2,1,0:T(1,128)S(1)}, u32[]{:S(2)}, u32[]{:S(2)}) %all-to-all-start) | async-done | bytes 524320 | tf_op jit(solution)/shard_map/while/body/eval_jaxpr/all_to_all | solution.py:18
  108.3 1.9 reduce.5
  115.0 5.7 %all-to-all-start.1 = ((f32[64,1,2048]{2,1,0:T(1,128)}), f32[64,1,2048]{2,1,0:T(1,128)S(1)}, u32[]{:S(2)}, u32[]{:S(2)}) async-start(f32[64,1,2048]{2,1,0:T(1,128)} %reshape.80), calls=%async_computation.1 | async-start | bytes 1048576 | tf_op jit(solution)/shard_map/while/body/eval_jaxpr/all_to_all | solution.py:18
  121.4 17.0 %all-to-all-done.1 = f32[64,1,2048]{2,1,0:T(1,128)S(1)} async-done(((f32[64,1,2048]{2,1,0:T(1,128)}), f32[64,1,2048]{2,1,0:T(1,128)S(1)}, u32[]{:S(2)}, u32[]{:S(2)}) %all-to-all-start.1) | async-done | bytes 524320 | tf_op jit(solution)/shard_map/while/body/eval_jaxpr/all_to_all | solution.py:18
  139.0 1.9 reduce.6
  144.4 1.9 collective-permute-start
  146.3 8.7 %collective-permute-done = f32[32,512]{0,1:T(8,128)S(1)} collective-permute-done((f32[32,512]{0,1:T(8,128)S(1)}, f32[32,512]{0,1:T(8,128)S(1)}, u32[]{:S(2)}, u32[]{:S(2)}) %collective-permute-start) | collective-permute-done | bytes 65568 | tf_op jit(solution)/shard_map/while/body/eval_jaxpr/ppermute | solution.py:10
  156.7 6.2 %all-to-all-start = ((f32[64,1,2048]{2,1,0:T(1,128)}), f32[64,1,2048]{2,1,0:T(1,128)S(1)}, u32[]{:S(2)}, u32[]{:S(2)}) async-start(f32[64,1,2048]{2,1,0:T(1,128)} %reshape.77), calls=%async_computation | async-start | bytes 1048576 | tf_op jit(solution)/shard_map/while/body/eval_jaxpr/all_to_all | solution.py:18
  162.9 17.7 %all-to-all-done = f32[64,1,2048]{2,1,0:T(1,128)S(1)} async-done(((f32[64,1,2048]{2,1,0:T(1,128)}), f32[64,1,2048]{2,1,0:T(1,128)S(1)}, u32[]{:S(2)}, u32[]{:S(2)}) %all-to-all-start) | async-done | bytes 524320 | tf_op jit(solution)/shard_map/while/body/eval_jaxpr/all_to_all | solution.py:18
  181.2 1.9 reduce.5
  187.8 5.7 %all-to-all-start.1 = ((f32[64,1,2048]{2,1,0:T(1,128)}), f32[64,1,2048]{2,1,0:T(1,128)S(1)}, u32[]{:S(2)}, u32[]{:S(2)}) async-start(f32[64,1,2048]{2,1,0:T(1,128)} %reshape.80), calls=%async_computation.1 | async-start | bytes 1048576 | tf_op jit(solution)/shard_map/while/body/eval_jaxpr/all_to_all | solution.py:18
  194.2 17.0 %all-to-all-done.1 = f32[64,1,2048]{2,1,0:T(1,128)S(1)} async-done(((f32[64,1,2048]{2,1,0:T(1,128)}), f32[64,1,2048]{2,1,0:T(1,128)S(1)}, u32[]{:S(2)}, u32[]{:S(2)}) %all-to-all-start.1) | async-done | bytes 524320 | tf_op jit(solution)/shard_map/while/body/eval_jaxpr/all_to_all | solution.py:18
  211.8 1.9 reduce.6
  217.3 1.9 collective-permute-start
  219.2 8.7 %collective-permute-done = f32[32,512]{0,1:T(8,128)S(1)} collective-permute-done((f32[32,512]{0,1:T(8,128)S(1)}, f32[32,512]{0,1:T(8,128)S(1)}, u32[]{:S(2)}, u32[]{:S(2)}) %collective-permute-start) | collective-permute-done | bytes 65568 | tf_op jit(solution)/shard_map/while/body/eval_jaxpr/ppermute | solution.py:10
  229.6 6.2 %all-to-all-start = ((f32[64,1,2048]{2,1,0:T(1,128)}), f32[64,1,2048]{2,1,0:T(1,128)S(1)}, u32[]{:S(2)}, u32[]{:S(2)}) async-start(f32[64,1,2048]{2,1,0:T(1,128)} %reshape.77), calls=%async_computation | async-start | bytes 1048576 | tf_op jit(solution)/shard_map/while/body/eval_jaxpr/all_to_all | solution.py:18
  235.8 17.7 %all-to-all-done = f32[64,1,2048]{2,1,0:T(1,128)S(1)} async-done(((f32[64,1,2048]{2,1,0:T(1,128)}), f32[64,1,2048]{2,1,0:T(1,128)S(1)}, u32[]{:S(2)}, u32[]{:S(2)}) %all-to-all-start) | async-done | bytes 524320 | tf_op jit(solution)/shard_map/while/body/eval_jaxpr/all_to_all | solution.py:18
  254.0 1.9 reduce.5
  260.7 5.7 %all-to-all-start.1 = ((f32[64,1,2048]{2,1,0:T(1,128)}), f32[64,1,2048]{2,1,0:T(1,128)S(1)}, u32[]{:S(2)}, u32[]{:S(2)}) async-start(f32[64,1,2048]{2,1,0:T(1,128)} %reshape.80), calls=%async_computation.1 | async-start | bytes 1048576 | tf_op jit(solution)/shard_map/while/body/eval_jaxpr/all_to_all | solution.py:18
  267.1 17.0 %all-to-all-done.1 = f32[64,1,2048]{2,1,0:T(1,128)S(1)} async-done(((f32[64,1,2048]{2,1,0:T(1,128)}), f32[64,1,2048]{2,1,0:T(1,128)S(1)}, u32[]{:S(2)}, u32[]{:S(2)}) %all-to-all-start.1) | async-done | bytes 524320 | tf_op jit(solution)/shard_map/while/body/eval_jaxpr/all_to_all | solution.py:18
  284.7 1.9 reduce.6
  290.1 1.9 collective-permute-start
  292.0 8.7 %collective-permute-done = f32[32,512]{0,1:T(8,128)S(1)} collective-permute-done((f32[32,512]{0,1:T(8,128)S(1)}, f32[32,512]{0,1:T(8,128)S(1)}, u32[]{:S(2)}, u32[]{:S(2)}) %collective-permute-start) | collective-permute-done | bytes 65568 | tf_op jit(solution)/shard_map/while/body/eval_jaxpr/ppermute | solution.py:10
  302.4 6.2 %all-to-all-start = ((f32[64,1,2048]{2,1,0:T(1,128)}), f32[64,1,2048]{2,1,0:T(1,128)S(1)}, u32[]{:S(2)}, u32[]{:S(2)}) async-start(f32[64,1,2048]{2,1,0:T(1,128)} %reshape.77), calls=%async_computation | async-start | bytes 1048576 | tf_op jit(solution)/shard_map/while/body/eval_jaxpr/all_to_all | solution.py:18
  308.6 17.7 %all-to-all-done = f32[64,1,2048]{2,1,0:T(1,128)S(1)} async-done(((f32[64,1,2048]{2,1,0:T(1,128)}), f32[64,1,2048]{2,1,0:T(1,128)S(1)}, u32[]{:S(2)}, u32[]{:S(2)}) %all-to-all-start) | async-done | bytes 524320 | tf_op jit(solution)/shard_map/while/body/eval_jaxpr/all_to_all | solution.py:18
  326.9 1.9 reduce.5
  333.5 5.7 %all-to-all-start.1 = ((f32[64,1,2048]{2,1,0:T(1,128)}), f32[64,1,2048]{2,1,0:T(1,128)S(1)}, u32[]{:S(2)}, u32[]{:S(2)}) async-start(f32[64,1,2048]{2,1,0:T(1,128)} %reshape.80), calls=%async_computation.1 | async-start | bytes 1048576 | tf_op jit(solution)/shard_map/while/body/eval_jaxpr/all_to_all | solution.py:18
  339.9 17.0 %all-to-all-done.1 = f32[64,1,2048]{2,1,0:T(1,128)S(1)} async-done(((f32[64,1,2048]{2,1,0:T(1,128)}), f32[64,1,2048]{2,1,0:T(1,128)S(1)}, u32[]{:S(2)}, u32[]{:S(2)}) %all-to-all-start.1) | async-done | bytes 524320 | tf_op jit(solution)/shard_map/while/body/eval_jaxpr/all_to_all | solution.py:18
  357.5 1.9 reduce.6
  363.0 1.9 collective-permute-start
  364.9 8.7 %collective-permute-done = f32[32,512]{0,1:T(8,128)S(1)} collective-permute-done((f32[32,512]{0,1:T(8,128)S(1)}, f32[32,512]{0,1:T(8,128)S(1)}, u32[]{:S(2)}, u32[]{:S(2)}) %collective-permute-start) | collective-permute-done | bytes 65568 | tf_op jit(solution)/shard_map/while/body/eval_jaxpr/ppermute | solution.py:10
  375.3 6.2 %all-to-all-start = ((f32[64,1,2048]{2,1,0:T(1,128)}), f32[64,1,2048]{2,1,0:T(1,128)S(1)}, u32[]{:S(2)}, u32[]{:S(2)}) async-start(f32[64,1,2048]{2,1,0:T(1,128)} %reshape.77), calls=%async_computation | async-start | bytes 1048576 | tf_op jit(solution)/shard_map/while/body/eval_jaxpr/all_to_all | solution.py:18
  381.5 17.7 %all-to-all-done = f32[64,1,2048]{2,1,0:T(1,128)S(1)} async-done(((f32[64,1,2048]{2,1,0:T(1,128)}), f32[64,1,2048]{2,1,0:T(1,128)S(1)}, u32[]{:S(2)}, u32[]{:S(2)}) %all-to-all-start) | async-done | bytes 524320 | tf_op jit(solution)/shard_map/while/body/eval_jaxpr/all_to_all | solution.py:18
  399.7 1.9 reduce.5
  406.4 5.7 %all-to-all-start.1 = ((f32[64,1,2048]{2,1,0:T(1,128)}), f32[64,1,2048]{2,1,0:T(1,128)S(1)}, u32[]{:S(2)}, u32[]{:S(2)}) async-start(f32[64,1,2048]{2,1,0:T(1,128)} %reshape.80), calls=%async_computation.1 | async-start | bytes 1048576 | tf_op jit(solution)/shard_map/while/body/eval_jaxpr/all_to_all | solution.py:18
  412.8 17.0 %all-to-all-done.1 = f32[64,1,2048]{2,1,0:T(1,128)S(1)} async-done(((f32[64,1,2048]{2,1,0:T(1,128)}), f32[64,1,2048]{2,1,0:T(1,128)S(1)}, u32[]{:S(2)}, u32[]{:S(2)}) %all-to-all-start.1) | async-done | bytes 524320 | tf_op jit(solution)/shard_map/while/body/eval_jaxpr/all_to_all | solution.py:18
  430.4 1.9 reduce.6
  435.8 1.9 collective-permute-start
  437.7 8.7 %collective-permute-done = f32[32,512]{0,1:T(8,128)S(1)} collective-permute-done((f32[32,512]{0,1:T(8,128)S(1)}, f32[32,512]{0,1:T(8,128)S(1)}, u32[]{:S(2)}, u32[]{:S(2)}) %collective-permute-start) | collective-permute-done | bytes 65568 | tf_op jit(solution)/shard_map/while/body/eval_jaxpr/ppermute | solution.py:10
  448.1 6.2 %all-to-all-start = ((f32[64,1,2048]{2,1,0:T(1,128)}), f32[64,1,2048]{2,1,0:T(1,128)S(1)}, u32[]{:S(2)}, u32[]{:S(2)}) async-start(f32[64,1,2048]{2,1,0:T(1,128)} %reshape.77), calls=%async_computation | async-start | bytes 1048576 | tf_op jit(solution)/shard_map/while/body/eval_jaxpr/all_to_all | solution.py:18
  454.3 17.7 %all-to-all-done = f32[64,1,2048]{2,1,0:T(1,128)S(1)} async-done(((f32[64,1,2048]{2,1,0:T(1,128)}), f32[64,1,2048]{2,1,0:T(1,128)S(1)}, u32[]{:S(2)}, u32[]{:S(2)}) %all-to-all-start) | async-done | bytes 524320 | tf_op jit(solution)/shard_map/while/body/eval_jaxpr/all_to_all | solution.py:18
  472.6 1.9 reduce.5
  479.2 5.7 %all-to-all-start.1 = ((f32[64,1,2048]{2,1,0:T(1,128)}), f32[64,1,2048]{2,1,0:T(1,128)S(1)}, u32[]{:S(2)}, u32[]{:S(2)}) async-start(f32[64,1,2048]{2,1,0:T(1,128)} %reshape.80), calls=%async_computation.1 | async-start | bytes 1048576 | tf_op jit(solution)/shard_map/while/body/eval_jaxpr/all_to_all | solution.py:18
  485.6 17.0 %all-to-all-done.1 = f32[64,1,2048]{2,1,0:T(1,128)S(1)} async-done(((f32[64,1,2048]{2,1,0:T(1,128)}), f32[64,1,2048]{2,1,0:T(1,128)S(1)}, u32[]{:S(2)}, u32[]{:S(2)}) %all-to-all-start.1) | async-done | bytes 524320 | tf_op jit(solution)/shard_map/while/body/eval_jaxpr/all_to_all | solution.py:18
  503.2 1.9 reduce.6
  508.7 1.9 collective-permute-start
  510.6 8.7 %collective-permute-done = f32[32,512]{0,1:T(8,128)S(1)} collective-permute-done((f32[32,512]{0,1:T(8,128)S(1)}, f32[32,512]{0,1:T(8,128)S(1)}, u32[]{:S(2)}, u32[]{:S(2)}) %collective-permute-start) | collective-permute-done | bytes 65568 | tf_op jit(solution)/shard_map/while/body/eval_jaxpr/ppermute | solution.py:10
  521.7 6.2 %all-to-all-start.2 = ((f32[64,1,2048]{2,1,0:T(1,128)}), f32[64,1,2048]{2,1,0:T(1,128)S(1)}, u32[]{:S(2)}, u32[]{:S(2)}) async-start(f32[64,1,2048]{2,1,0:T(1,128)} %reshape.65), calls=%async_computation.2 | async-start | bytes 1048576 | tf_op jit(solution)/shard_map/all_to_all | solution.py:18
  527.8 17.7 %all-to-all-done.2 = f32[64,1,2048]{2,1,0:T(1,128)S(1)} async-done(((f32[64,1,2048]{2,1,0:T(1,128)}), f32[64,1,2048]{2,1,0:T(1,128)S(1)}, u32[]{:S(2)}, u32[]{:S(2)}) %all-to-all-start.2) | async-done | bytes 524320 | tf_op jit(solution)/shard_map/all_to_all | solution.py:18
  546.0 1.9 reduce.2
  550.2 1.6 convolution_select_fusion.1
  (190 shorter events, 84.8 us)
Async XLA Ops:
  0.8 0.7 copy-start.4
  3.2 31.7 %all-to-all-start = ((f32[64,1,2048]{2,1,0:T(1,128)}), f32[64,1,2048]{2,1,0:T(1,128)S(1)}, u32[]{:S(2)}, u32[]{:S(2)}) async-start(f32[64,1,2048]{2,1,0:T(1,128)} %reshape.77), calls=%async_computation | async-start | bytes 1048576 | tf_op jit(solution)/shard_map/while/body/eval_jaxpr/all_to_all | solution.py:18
  38.4 1.2 copy-start
  42.1 23.4 %all-to-all-start.1 = ((f32[64,1,2048]{2,1,0:T(1,128)}), f32[64,1,2048]{2,1,0:T(1,128)S(1)}, u32[]{:S(2)}, u32[]{:S(2)}) async-start(f32[64,1,2048]{2,1,0:T(1,128)} %reshape.80), calls=%async_computation.1 | async-start | bytes 1048576 | tf_op jit(solution)/shard_map/while/body/eval_jaxpr/all_to_all | solution.py:18
  69.0 1.0 copy-start.2
  71.6 10.6 %collective-permute-start = (f32[32,512]{0,1:T(8,128)S(1)}, f32[32,512]{0,1:T(8,128)S(1)}, u32[]{:S(2)}, u32[]{:S(2)}) collective-permute-start(f32[32,512]{0,1:T(8,128)S(1)} %scatter_fusion), channel_id=1, source_target_pairs={{0,64},{64,128},{128,192},{192,256},{256,320},{320,384},{384,448},... | collective-permute-start | bytes 196616 | tf_op jit(solution)/shard_map/while/body/eval_jaxpr/ppermute | solution.py:10
  83.9 23.9 %all-to-all-start = ((f32[64,1,2048]{2,1,0:T(1,128)}), f32[64,1,2048]{2,1,0:T(1,128)S(1)}, u32[]{:S(2)}, u32[]{:S(2)}) async-start(f32[64,1,2048]{2,1,0:T(1,128)} %reshape.77), calls=%async_computation | async-start | bytes 1048576 | tf_op jit(solution)/shard_map/while/body/eval_jaxpr/all_to_all | solution.py:18
  111.2 1.2 copy-start
  115.0 23.4 %all-to-all-start.1 = ((f32[64,1,2048]{2,1,0:T(1,128)}), f32[64,1,2048]{2,1,0:T(1,128)S(1)}, u32[]{:S(2)}, u32[]{:S(2)}) async-start(f32[64,1,2048]{2,1,0:T(1,128)} %reshape.80), calls=%async_computation.1 | async-start | bytes 1048576 | tf_op jit(solution)/shard_map/while/body/eval_jaxpr/all_to_all | solution.py:18
  141.9 1.0 copy-start.2
  144.4 10.6 %collective-permute-start = (f32[32,512]{0,1:T(8,128)S(1)}, f32[32,512]{0,1:T(8,128)S(1)}, u32[]{:S(2)}, u32[]{:S(2)}) collective-permute-start(f32[32,512]{0,1:T(8,128)S(1)} %scatter_fusion), channel_id=1, source_target_pairs={{0,64},{64,128},{128,192},{192,256},{256,320},{320,384},{384,448},... | collective-permute-start | bytes 196616 | tf_op jit(solution)/shard_map/while/body/eval_jaxpr/ppermute | solution.py:10
  156.7 23.9 %all-to-all-start = ((f32[64,1,2048]{2,1,0:T(1,128)}), f32[64,1,2048]{2,1,0:T(1,128)S(1)}, u32[]{:S(2)}, u32[]{:S(2)}) async-start(f32[64,1,2048]{2,1,0:T(1,128)} %reshape.77), calls=%async_computation | async-start | bytes 1048576 | tf_op jit(solution)/shard_map/while/body/eval_jaxpr/all_to_all | solution.py:18
  184.1 1.2 copy-start
  187.8 23.4 %all-to-all-start.1 = ((f32[64,1,2048]{2,1,0:T(1,128)}), f32[64,1,2048]{2,1,0:T(1,128)S(1)}, u32[]{:S(2)}, u32[]{:S(2)}) async-start(f32[64,1,2048]{2,1,0:T(1,128)} %reshape.80), calls=%async_computation.1 | async-start | bytes 1048576 | tf_op jit(solution)/shard_map/while/body/eval_jaxpr/all_to_all | solution.py:18
  214.7 1.0 copy-start.2
  217.3 10.6 %collective-permute-start = (f32[32,512]{0,1:T(8,128)S(1)}, f32[32,512]{0,1:T(8,128)S(1)}, u32[]{:S(2)}, u32[]{:S(2)}) collective-permute-start(f32[32,512]{0,1:T(8,128)S(1)} %scatter_fusion), channel_id=1, source_target_pairs={{0,64},{64,128},{128,192},{192,256},{256,320},{320,384},{384,448},... | collective-permute-start | bytes 196616 | tf_op jit(solution)/shard_map/while/body/eval_jaxpr/ppermute | solution.py:10
  229.6 23.9 %all-to-all-start = ((f32[64,1,2048]{2,1,0:T(1,128)}), f32[64,1,2048]{2,1,0:T(1,128)S(1)}, u32[]{:S(2)}, u32[]{:S(2)}) async-start(f32[64,1,2048]{2,1,0:T(1,128)} %reshape.77), calls=%async_computation | async-start | bytes 1048576 | tf_op jit(solution)/shard_map/while/body/eval_jaxpr/all_to_all | solution.py:18
  256.9 1.2 copy-start
  260.7 23.4 %all-to-all-start.1 = ((f32[64,1,2048]{2,1,0:T(1,128)}), f32[64,1,2048]{2,1,0:T(1,128)S(1)}, u32[]{:S(2)}, u32[]{:S(2)}) async-start(f32[64,1,2048]{2,1,0:T(1,128)} %reshape.80), calls=%async_computation.1 | async-start | bytes 1048576 | tf_op jit(solution)/shard_map/while/body/eval_jaxpr/all_to_all | solution.py:18
  287.6 1.0 copy-start.2
  290.1 10.6 %collective-permute-start = (f32[32,512]{0,1:T(8,128)S(1)}, f32[32,512]{0,1:T(8,128)S(1)}, u32[]{:S(2)}, u32[]{:S(2)}) collective-permute-start(f32[32,512]{0,1:T(8,128)S(1)} %scatter_fusion), channel_id=1, source_target_pairs={{0,64},{64,128},{128,192},{192,256},{256,320},{320,384},{384,448},... | collective-permute-start | bytes 196616 | tf_op jit(solution)/shard_map/while/body/eval_jaxpr/ppermute | solution.py:10
  302.4 23.9 %all-to-all-start = ((f32[64,1,2048]{2,1,0:T(1,128)}), f32[64,1,2048]{2,1,0:T(1,128)S(1)}, u32[]{:S(2)}, u32[]{:S(2)}) async-start(f32[64,1,2048]{2,1,0:T(1,128)} %reshape.77), calls=%async_computation | async-start | bytes 1048576 | tf_op jit(solution)/shard_map/while/body/eval_jaxpr/all_to_all | solution.py:18
  329.8 1.2 copy-start
  333.5 23.4 %all-to-all-start.1 = ((f32[64,1,2048]{2,1,0:T(1,128)}), f32[64,1,2048]{2,1,0:T(1,128)S(1)}, u32[]{:S(2)}, u32[]{:S(2)}) async-start(f32[64,1,2048]{2,1,0:T(1,128)} %reshape.80), calls=%async_computation.1 | async-start | bytes 1048576 | tf_op jit(solution)/shard_map/while/body/eval_jaxpr/all_to_all | solution.py:18
  360.4 1.0 copy-start.2
  363.0 10.6 %collective-permute-start = (f32[32,512]{0,1:T(8,128)S(1)}, f32[32,512]{0,1:T(8,128)S(1)}, u32[]{:S(2)}, u32[]{:S(2)}) collective-permute-start(f32[32,512]{0,1:T(8,128)S(1)} %scatter_fusion), channel_id=1, source_target_pairs={{0,64},{64,128},{128,192},{192,256},{256,320},{320,384},{384,448},... | collective-permute-start | bytes 196616 | tf_op jit(solution)/shard_map/while/body/eval_jaxpr/ppermute | solution.py:10
  375.3 23.9 %all-to-all-start = ((f32[64,1,2048]{2,1,0:T(1,128)}), f32[64,1,2048]{2,1,0:T(1,128)S(1)}, u32[]{:S(2)}, u32[]{:S(2)}) async-start(f32[64,1,2048]{2,1,0:T(1,128)} %reshape.77), calls=%async_computation | async-start | bytes 1048576 | tf_op jit(solution)/shard_map/while/body/eval_jaxpr/all_to_all | solution.py:18
  402.6 1.2 copy-start
  406.4 23.4 %all-to-all-start.1 = ((f32[64,1,2048]{2,1,0:T(1,128)}), f32[64,1,2048]{2,1,0:T(1,128)S(1)}, u32[]{:S(2)}, u32[]{:S(2)}) async-start(f32[64,1,2048]{2,1,0:T(1,128)} %reshape.80), calls=%async_computation.1 | async-start | bytes 1048576 | tf_op jit(solution)/shard_map/while/body/eval_jaxpr/all_to_all | solution.py:18
  433.3 1.0 copy-start.2
  435.8 10.6 %collective-permute-start = (f32[32,512]{0,1:T(8,128)S(1)}, f32[32,512]{0,1:T(8,128)S(1)}, u32[]{:S(2)}, u32[]{:S(2)}) collective-permute-start(f32[32,512]{0,1:T(8,128)S(1)} %scatter_fusion), channel_id=1, source_target_pairs={{0,64},{64,128},{128,192},{192,256},{256,320},{320,384},{384,448},... | collective-permute-start | bytes 196616 | tf_op jit(solution)/shard_map/while/body/eval_jaxpr/ppermute | solution.py:10
  448.1 23.9 %all-to-all-start = ((f32[64,1,2048]{2,1,0:T(1,128)}), f32[64,1,2048]{2,1,0:T(1,128)S(1)}, u32[]{:S(2)}, u32[]{:S(2)}) async-start(f32[64,1,2048]{2,1,0:T(1,128)} %reshape.77), calls=%async_computation | async-start | bytes 1048576 | tf_op jit(solution)/shard_map/while/body/eval_jaxpr/all_to_all | solution.py:18
  475.5 1.2 copy-start
  479.2 23.4 %all-to-all-start.1 = ((f32[64,1,2048]{2,1,0:T(1,128)}), f32[64,1,2048]{2,1,0:T(1,128)S(1)}, u32[]{:S(2)}, u32[]{:S(2)}) async-start(f32[64,1,2048]{2,1,0:T(1,128)} %reshape.80), calls=%async_computation.1 | async-start | bytes 1048576 | tf_op jit(solution)/shard_map/while/body/eval_jaxpr/all_to_all | solution.py:18
  506.1 1.0 copy-start.2
  508.7 10.6 %collective-permute-start = (f32[32,512]{0,1:T(8,128)S(1)}, f32[32,512]{0,1:T(8,128)S(1)}, u32[]{:S(2)}, u32[]{:S(2)}) collective-permute-start(f32[32,512]{0,1:T(8,128)S(1)} %scatter_fusion), channel_id=1, source_target_pairs={{0,64},{64,128},{128,192},{192,256},{256,320},{320,384},{384,448},... | collective-permute-start | bytes 196616 | tf_op jit(solution)/shard_map/while/body/eval_jaxpr/ppermute | solution.py:10
  519.3 0.7 copy-start.3
  521.7 23.9 %all-to-all-start.2 = ((f32[64,1,2048]{2,1,0:T(1,128)}), f32[64,1,2048]{2,1,0:T(1,128)S(1)}, u32[]{:S(2)}, u32[]{:S(2)}) async-start(f32[64,1,2048]{2,1,0:T(1,128)} %reshape.65), calls=%async_computation.2 | async-start | bytes 1048576 | tf_op jit(solution)/shard_map/all_to_all | solution.py:18
  549.0 1.2 copy-start.1

commit v3 on v2

v3 whole, which is shorter than its diff:
```python
import jax
import jax.numpy as jnp
from jax import lax
from jax.sharding import PartitionSpec as P


def passed_along(block, axis, distance):
    devices = range(lax.axis_size(axis))
    route = [(i - distance, i) for i in devices if i - distance in devices]
    return lax.ppermute(block, axis, route)


def stacked(block, axes):
    parts = 1
    for axis in axes:
        parts *= lax.axis_size(axis)
    flat = block.reshape(1, block.size)
    copies = jnp.broadcast_to(flat, (parts, block.size))
    pieces = lax.all_to_all(copies, axes, 0, 0, tiled=True)
    return pieces.reshape(parts * block.shape[0], block.shape[1])


def shards(right_sides, inverse_diag, lower_blocks, targets, counts):
    levels = lax.axis_size("sep")
    own_level = lax.axis_index("sep")
    batches, width_rhs, own_rows = right_sides.shape
    width = inverse_diag.shape[-1]
    axes = ("row", "col")
    given = right_sides.reshape(batches * width_rhs, own_rows).T
    diag_rows = inverse_diag[0]
    lower_rows = lower_blocks[0]
    lower_count = lower_rows.shape[0]
    live = jnp.arange(lower_count, dtype=jnp.int32) < counts[0, 0]
    places = targets[0] // width * own_rows + targets[0] % own_rows

    def times(rows, segment):
        return lax.dot_general(
            rows,
            segment,
            (((1,), (0,)), ((), ())),
            precision=lax.Precision.HIGHEST,
            preferred_element_type=jnp.float32,
        )

    def one_level(level, state):
        carried, solution = state
        resid = given - lax.dynamic_slice_in_dim(carried, level * own_rows, own_rows, 0)
        solved = times(diag_rows, stacked(resid, axes))
        solution = jnp.where(own_level == level, solved, solution)
        update = times(lower_rows, stacked(solved, axes))
        update = jnp.where(live[:, None], update, jnp.float32(0.0))
        carried = carried.at[places, :].add(update)
        return passed_along(carried, "sep", 1), solution

    carried = jnp.zeros((levels * own_rows, given.shape[1]), jnp.float32)
    solution = jnp.zeros_like(given)
    carried, solution = lax.fori_loop(0, levels - 1, one_level, (carried, solution))
    last = levels - 1
    resid = given - carried[last * own_rows:, :]
    solved = times(diag_rows, stacked(resid, axes))
    solution = jnp.where(own_level == last, solved, solution)
    return solution.T.reshape(batches, width_rhs, own_rows)


def solution(mesh):
    placed = (
        P(None, None, ("sep", "row", "col")),
        P("sep", ("row", "col"), None),
        P("sep", ("row", "col"), None),
        P("sep", ("row", "col")),
        P("sep", ("row", "col")),
    )
    return jax.shard_map(
        shards,
        mesh=mesh,
        in_specs=placed,
        out_specs=P(None, None, ("sep", "row", "col")),
        check_vma=False,
    )
```

time: 554 us -> 556 us (level)
  matrix products: 12.1 us -> 60 us
  local copies, waits for them, and re-layouts: 67.8 us -> 30.6 us
  other arithmetic: 38.9 us -> 31.3 us
    dot_general x15, matrix products: 12.1 us -> 60 us  [times(): lax.dot_general(rows, segment, (((1,), (0,)), ((), ())), precision=lax.Pr...]
    while x63 -> x21, local copies, waits for them, and re-layouts: 36.9 us -> 0.17 us
    broadcast_in_dim x16 -> x31, local copies, waits for them, and re-layouts: 1.84 us -> 17.1 us  [the longest x30 17.1 us: stacked(): copies = jnp.broadcast_to(flat, (parts, block.size))]
    transpose x15 -> x0, local copies, waits for them, and re-layouts: 9.2 us -> none  [gathered(): jnp.transpose(pieces, (1, 0, 2))]
    all_to_all x15, other arithmetic: 28 us -> 19.5 us  [stacked(): pieces = lax.all_to_all(copies, axes, 0, 0, tiled=True)]
    all_to_all x15 -> x0, local copies, waits for them, and re-layouts: 8.56 us -> none  [gathered(): pieces = lax.all_to_all(copies, axes, 0, 0, tiled=True)]
    reshape x15, local copies, waits for them, and re-layouts: 5.39 us -> 11.3 us  [stacked(): return pieces.reshape(parts * block.shape[0], block.shape[1])]
where the time goes in v3:
time: 556 us; the launch traced here: 554 us
  waiting for transfers between devices  320 us (58%)
  starting transfers between devices  111 us (20%)
  matrix products  60 us (11%)
  other arithmetic  31.3 us (6%)
  local copies, waits for them, and re-layouts  30.6 us (6%)
    all_to_all x15, waiting for transfers between devices, stacked(): pieces = lax.all_to_all(copies, axes, 0, 0, tiled=True)  260 us
    all_to_all x15, starting transfers between devices, stacked(): pieces = lax.all_to_all(copies, axes, 0, 0, tiled=True)  97.1 us
    ppermute x7, waiting for transfers between devices, passed_along(): return lax.ppermute(block, axis, route)  60.1 us
    dot_general x15, matrix products, times(): lax.dot_general(rows, segment, (((1,), (0,)), ((), ())), precision=lax.Pr...  60 us
    all_to_all x15, other arithmetic, stacked(): pieces = lax.all_to_all(copies, axes, 0, 0, tiled=True)  19.5 us
    broadcast_in_dim x30, local copies, waits for them, and re-layouts, stacked(): copies = jnp.broadcast_to(flat, (parts, block.size))  17.1 us
    ppermute x7, starting transfers between devices, passed_along(): return lax.ppermute(block, axis, route)  13.8 us
    reshape x15, local copies, waits for them, and re-layouts, stacked(): return pieces.reshape(parts * block.shape[0], block.shape[1])  11.3 us
  transfers between devices with their start and end apart: 22, of which 22 were waited for; matrix products, arithmetic and copies ran while one was open for 1% of the time, Pallas kernels for 0%

profile of v3, /device:TPU:33, one launch (start us, length us, event | category | flops | bytes accessed | tf_op | source)
XLA Modules:
  0.0 554.3 jit_solution(6915799703641877977)
XLA Ops:
  1.5 519.6 %while.16 = (s32[]{:T(128)}, f32[512,32]{1,0:T(8,128)S(1)}, f32[64,32]{0,1:T(8,128)S(1)}, s32[32]{0:T(128)S(1)}, f32[64,32]{1,0:T(8,128)S(1)}, /*index=5*/f32[64...) while((s32[]{:T(128)}, f32[512,32]{1,0:T(8,128)S(1)}, ...), condition=%wide.region_2.3_spmd.clone, body=%wide.region_0.2_spmd.clone.sunk | while | flops 151003264 | bytes 13640475 | solution.py:57
  2.7 14.0 %all-to-all-start = ((f32[64,1,2048]{2,1,0:T(1,128)}), f32[64,1,2048]{2,1,0:T(1,128)S(1)}, u32[]{:S(2)}, u32[]{:S(2)}) async-start(f32[64,1,2048]{2,1,0:T(1,128)} %broadcast_in_dim.90), calls=%async_computation | async-start | bytes 1048576 | tf_op jit(solution)/shard_map/while/body/eval_jaxpr/all_to_all | solution.py:19
  16.7 17.7 %all-to-all-done = f32[64,1,2048]{2,1,0:T(1,128)S(1)} async-done(((f32[64,1,2048]{2,1,0:T(1,128)}), f32[64,1,2048]{2,1,0:T(1,128)S(1)}, u32[]{:S(2)}, u32[]{:S(2)}) %all-to-all-start) | async-done | bytes 524320 | tf_op jit(solution)/shard_map/while/body/eval_jaxpr/all_to_all | solution.py:19
  36.3 4.6 select_select_fusion.2
  42.1 5.7 %all-to-all-start.1 = ((f32[64,1,2048]{2,1,0:T(1,128)}), f32[64,1,2048]{2,1,0:T(1,128)S(1)}, u32[]{:S(2)}, u32[]{:S(2)}) async-start(f32[64,1,2048]{2,1,0:T(1,128)} %broadcast_in_dim.92), calls=%async_computation.1 | async-start | bytes 1048576 | tf_op jit(solution)/shard_map/while/body/eval_jaxpr/all_to_all | solution.py:19
  48.6 17.0 %all-to-all-done.1 = f32[64,1,2048]{2,1,0:T(1,128)S(1)} async-done(((f32[64,1,2048]{2,1,0:T(1,128)}), f32[64,1,2048]{2,1,0:T(1,128)S(1)}, u32[]{:S(2)}, u32[]{:S(2)}) %all-to-all-start.1) | async-done | bytes 524320 | tf_op jit(solution)/shard_map/while/body/eval_jaxpr/all_to_all | solution.py:19
  65.5 1.2 reduce.6
  67.5 3.4 fusion.23
  71.8 2.3 collective-permute-start
  74.1 8.3 %collective-permute-done = f32[512,32]{1,0:T(8,128)S(1)} collective-permute-done((f32[512,32]{1,0:T(8,128)S(1)}, f32[512,32]{1,0:T(8,128)S(1)}, u32[]{:S(2)}, u32[]{:S(2)}) %collective-permute-start) | collective-permute-done | bytes 65568 | tf_op jit(solution)/shard_map/while/body/eval_jaxpr/ppermute | solution.py:10
  83.6 6.2 %all-to-all-start = ((f32[64,1,2048]{2,1,0:T(1,128)}), f32[64,1,2048]{2,1,0:T(1,128)S(1)}, u32[]{:S(2)}, u32[]{:S(2)}) async-start(f32[64,1,2048]{2,1,0:T(1,128)} %broadcast_in_dim.90), calls=%async_computation | async-start | bytes 1048576 | tf_op jit(solution)/shard_map/while/body/eval_jaxpr/all_to_all | solution.py:19
  89.8 17.7 %all-to-all-done = f32[64,1,2048]{2,1,0:T(1,128)S(1)} async-done(((f32[64,1,2048]{2,1,0:T(1,128)}), f32[64,1,2048]{2,1,0:T(1,128)S(1)}, u32[]{:S(2)}, u32[]{:S(2)}) %all-to-all-start) | async-done | bytes 524320 | tf_op jit(solution)/shard_map/while/body/eval_jaxpr/all_to_all | solution.py:19
  109.4 4.6 select_select_fusion.2
  115.2 5.7 %all-to-all-start.1 = ((f32[64,1,2048]{2,1,0:T(1,128)}), f32[64,1,2048]{2,1,0:T(1,128)S(1)}, u32[]{:S(2)}, u32[]{:S(2)}) async-start(f32[64,1,2048]{2,1,0:T(1,128)} %broadcast_in_dim.92), calls=%async_computation.1 | async-start | bytes 1048576 | tf_op jit(solution)/shard_map/while/body/eval_jaxpr/all_to_all | solution.py:19
  121.7 17.0 %all-to-all-done.1 = f32[64,1,2048]{2,1,0:T(1,128)S(1)} async-done(((f32[64,1,2048]{2,1,0:T(1,128)}), f32[64,1,2048]{2,1,0:T(1,128)S(1)}, u32[]{:S(2)}, u32[]{:S(2)}) %all-to-all-start.1) | async-done | bytes 524320 | tf_op jit(solution)/shard_map/while/body/eval_jaxpr/all_to_all | solution.py:19
  138.6 1.2 reduce.6
  140.6 3.4 fusion.23
  144.9 1.9 collective-permute-start
  146.8 8.6 %collective-permute-done = f32[512,32]{1,0:T(8,128)S(1)} collective-permute-done((f32[512,32]{1,0:T(8,128)S(1)}, f32[512,32]{1,0:T(8,128)S(1)}, u32[]{:S(2)}, u32[]{:S(2)}) %collective-permute-start) | collective-permute-done | bytes 65568 | tf_op jit(solution)/shard_map/while/body/eval_jaxpr/ppermute | solution.py:10
  156.7 6.2 %all-to-all-start = ((f32[64,1,2048]{2,1,0:T(1,128)}), f32[64,1,2048]{2,1,0:T(1,128)S(1)}, u32[]{:S(2)}, u32[]{:S(2)}) async-start(f32[64,1,2048]{2,1,0:T(1,128)} %broadcast_in_dim.90), calls=%async_computation | async-start | bytes 1048576 | tf_op jit(solution)/shard_map/while/body/eval_jaxpr/all_to_all | solution.py:19
  162.9 17.7 %all-to-all-done = f32[64,1,2048]{2,1,0:T(1,128)S(1)} async-done(((f32[64,1,2048]{2,1,0:T(1,128)}), f32[64,1,2048]{2,1,0:T(1,128)S(1)}, u32[]{:S(2)}, u32[]{:S(2)}) %all-to-all-start) | async-done | bytes 524320 | tf_op jit(solution)/shard_map/while/body/eval_jaxpr/all_to_all | solution.py:19
  182.5 4.6 select_select_fusion.2
  188.3 5.7 %all-to-all-start.1 = ((f32[64,1,2048]{2,1,0:T(1,128)}), f32[64,1,2048]{2,1,0:T(1,128)S(1)}, u32[]{:S(2)}, u32[]{:S(2)}) async-start(f32[64,1,2048]{2,1,0:T(1,128)} %broadcast_in_dim.92), calls=%async_computation.1 | async-start | bytes 1048576 | tf_op jit(solution)/shard_map/while/body/eval_jaxpr/all_to_all | solution.py:19
  194.8 17.0 %all-to-all-done.1 = f32[64,1,2048]{2,1,0:T(1,128)S(1)} async-done(((f32[64,1,2048]{2,1,0:T(1,128)}), f32[64,1,2048]{2,1,0:T(1,128)S(1)}, u32[]{:S(2)}, u32[]{:S(2)}) %all-to-all-start.1) | async-done | bytes 524320 | tf_op jit(solution)/shard_map/while/body/eval_jaxpr/all_to_all | solution.py:19
  213.7 3.4 fusion.23
  218.0 1.9 collective-permute-start
  219.9 8.6 %collective-permute-done = f32[512,32]{1,0:T(8,128)S(1)} collective-permute-done((f32[512,32]{1,0:T(8,128)S(1)}, f32[512,32]{1,0:T(8,128)S(1)}, u32[]{:S(2)}, u32[]{:S(2)}) %collective-permute-start) | collective-permute-done | bytes 65568 | tf_op jit(solution)/shard_map/while/body/eval_jaxpr/ppermute | solution.py:10
  229.8 6.2 %all-to-all-start = ((f32[64,1,2048]{2,1,0:T(1,128)}), f32[64,1,2048]{2,1,0:T(1,128)S(1)}, u32[]{:S(2)}, u32[]{:S(2)}) async-start(f32[64,1,2048]{2,1,0:T(1,128)} %broadcast_in_dim.90), calls=%async_computation | async-start | bytes 1048576 | tf_op jit(solution)/shard_map/while/body/eval_jaxpr/all_to_all | solution.py:19
  236.0 17.7 %all-to-all-done = f32[64,1,2048]{2,1,0:T(1,128)S(1)} async-done(((f32[64,1,2048]{2,1,0:T(1,128)}), f32[64,1,2048]{2,1,0:T(1,128)S(1)}, u32[]{:S(2)}, u32[]{:S(2)}) %all-to-all-start) | async-done | bytes 524320 | tf_op jit(solution)/shard_map/while/body/eval_jaxpr/all_to_all | solution.py:19
  255.6 4.6 select_select_fusion.2
  261.4 5.7 %all-to-all-start.1 = ((f32[64,1,2048]{2,1,0:T(1,128)}), f32[64,1,2048]{2,1,0:T(1,128)S(1)}, u32[]{:S(2)}, u32[]{:S(2)}) async-start(f32[64,1,2048]{2,1,0:T(1,128)} %broadcast_in_dim.92), calls=%async_computation.1 | async-start | bytes 1048576 | tf_op jit(solution)/shard_map/while/body/eval_jaxpr/all_to_all | solution.py:19
  267.9 17.0 %all-to-all-done.1 = f32[64,1,2048]{2,1,0:T(1,128)S(1)} async-done(((f32[64,1,2048]{2,1,0:T(1,128)}), f32[64,1,2048]{2,1,0:T(1,128)S(1)}, u32[]{:S(2)}, u32[]{:S(2)}) %all-to-all-start.1) | async-done | bytes 524320 | tf_op jit(solution)/shard_map/while/body/eval_jaxpr/all_to_all | solution.py:19
  286.7 3.4 fusion.23
  291.1 1.9 collective-permute-start
  293.0 8.6 %collective-permute-done = f32[512,32]{1,0:T(8,128)S(1)} collective-permute-done((f32[512,32]{1,0:T(8,128)S(1)}, f32[512,32]{1,0:T(8,128)S(1)}, u32[]{:S(2)}, u32[]{:S(2)}) %collective-permute-start) | collective-permute-done | bytes 65568 | tf_op jit(solution)/shard_map/while/body/eval_jaxpr/ppermute | solution.py:10
  302.8 6.2 %all-to-all-start = ((f32[64,1,2048]{2,1,0:T(1,128)}), f32[64,1,2048]{2,1,0:T(1,128)S(1)}, u32[]{:S(2)}, u32[]{:S(2)}) async-start(f32[64,1,2048]{2,1,0:T(1,128)} %broadcast_in_dim.90), calls=%async_computation | async-start | bytes 1048576 | tf_op jit(solution)/shard_map/while/body/eval_jaxpr/all_to_all | solution.py:19
  309.1 17.7 %all-to-all-done = f32[64,1,2048]{2,1,0:T(1,128)S(1)} async-done(((f32[64,1,2048]{2,1,0:T(1,128)}), f32[64,1,2048]{2,1,0:T(1,128)S(1)}, u32[]{:S(2)}, u32[]{:S(2)}) %all-to-all-start) | async-done | bytes 524320 | tf_op jit(solution)/shard_map/while/body/eval_jaxpr/all_to_all | solution.py:19
  328.7 4.6 select_select_fusion.2
  334.5 5.7 %all-to-all-start.1 = ((f32[64,1,2048]{2,1,0:T(1,128)}), f32[64,1,2048]{2,1,0:T(1,128)S(1)}, u32[]{:S(2)}, u32[]{:S(2)}) async-start(f32[64,1,2048]{2,1,0:T(1,128)} %broadcast_in_dim.92), calls=%async_computation.1 | async-start | bytes 1048576 | tf_op jit(solution)/shard_map/while/body/eval_jaxpr/all_to_all | solution.py:19
  340.9 17.0 %all-to-all-done.1 = f32[64,1,2048]{2,1,0:T(1,128)S(1)} async-done(((f32[64,1,2048]{2,1,0:T(1,128)}), f32[64,1,2048]{2,1,0:T(1,128)S(1)}, u32[]{:S(2)}, u32[]{:S(2)}) %all-to-all-start.1) | async-done | bytes 524320 | tf_op jit(solution)/shard_map/while/body/eval_jaxpr/all_to_all | solution.py:19
  359.8 3.4 fusion.23
  364.2 1.9 collective-permute-start
  366.1 8.6 %collective-permute-done = f32[512,32]{1,0:T(8,128)S(1)} collective-permute-done((f32[512,32]{1,0:T(8,128)S(1)}, f32[512,32]{1,0:T(8,128)S(1)}, u32[]{:S(2)}, u32[]{:S(2)}) %collective-permute-start) | collective-permute-done | bytes 65568 | tf_op jit(solution)/shard_map/while/body/eval_jaxpr/ppermute | solution.py:10
  375.9 6.2 %all-to-all-start = ((f32[64,1,2048]{2,1,0:T(1,128)}), f32[64,1,2048]{2,1,0:T(1,128)S(1)}, u32[]{:S(2)}, u32[]{:S(2)}) async-start(f32[64,1,2048]{2,1,0:T(1,128)} %broadcast_in_dim.90), calls=%async_computation | async-start | bytes 1048576 | tf_op jit(solution)/shard_map/while/body/eval_jaxpr/all_to_all | solution.py:19
  382.1 17.7 %all-to-all-done = f32[64,1,2048]{2,1,0:T(1,128)S(1)} async-done(((f32[64,1,2048]{2,1,0:T(1,128)}), f32[64,1,2048]{2,1,0:T(1,128)S(1)}, u32[]{:S(2)}, u32[]{:S(2)}) %all-to-all-start) | async-done | bytes 524320 | tf_op jit(solution)/shard_map/while/body/eval_jaxpr/all_to_all | solution.py:19
  401.8 4.6 select_select_fusion.2
  407.6 5.7 %all-to-all-start.1 = ((f32[64,1,2048]{2,1,0:T(1,128)}), f32[64,1,2048]{2,1,0:T(1,128)S(1)}, u32[]{:S(2)}, u32[]{:S(2)}) async-start(f32[64,1,2048]{2,1,0:T(1,128)} %broadcast_in_dim.92), calls=%async_computation.1 | async-start | bytes 1048576 | tf_op jit(solution)/shard_map/while/body/eval_jaxpr/all_to_all | solution.py:19
  414.0 17.0 %all-to-all-done.1 = f32[64,1,2048]{2,1,0:T(1,128)S(1)} async-done(((f32[64,1,2048]{2,1,0:T(1,128)}), f32[64,1,2048]{2,1,0:T(1,128)S(1)}, u32[]{:S(2)}, u32[]{:S(2)}) %all-to-all-start.1) | async-done | bytes 524320 | tf_op jit(solution)/shard_map/while/body/eval_jaxpr/all_to_all | solution.py:19
  432.9 3.4 fusion.23
  437.3 1.9 collective-permute-start
  439.2 8.6 %collective-permute-done = f32[512,32]{1,0:T(8,128)S(1)} collective-permute-done((f32[512,32]{1,0:T(8,128)S(1)}, f32[512,32]{1,0:T(8,128)S(1)}, u32[]{:S(2)}, u32[]{:S(2)}) %collective-permute-start) | collective-permute-done | bytes 65568 | tf_op jit(solution)/shard_map/while/body/eval_jaxpr/ppermute | solution.py:10
  449.0 6.2 %all-to-all-start = ((f32[64,1,2048]{2,1,0:T(1,128)}), f32[64,1,2048]{2,1,0:T(1,128)S(1)}, u32[]{:S(2)}, u32[]{:S(2)}) async-start(f32[64,1,2048]{2,1,0:T(1,128)} %broadcast_in_dim.90), calls=%async_computation | async-start | bytes 1048576 | tf_op jit(solution)/shard_map/while/body/eval_jaxpr/all_to_all | solution.py:19
  455.2 17.7 %all-to-all-done = f32[64,1,2048]{2,1,0:T(1,128)S(1)} async-done(((f32[64,1,2048]{2,1,0:T(1,128)}), f32[64,1,2048]{2,1,0:T(1,128)S(1)}, u32[]{:S(2)}, u32[]{:S(2)}) %all-to-all-start) | async-done | bytes 524320 | tf_op jit(solution)/shard_map/while/body/eval_jaxpr/all_to_all | solution.py:19
  474.8 4.6 select_select_fusion.2
  480.7 5.7 %all-to-all-start.1 = ((f32[64,1,2048]{2,1,0:T(1,128)}), f32[64,1,2048]{2,1,0:T(1,128)S(1)}, u32[]{:S(2)}, u32[]{:S(2)}) async-start(f32[64,1,2048]{2,1,0:T(1,128)} %broadcast_in_dim.92), calls=%async_computation.1 | async-start | bytes 1048576 | tf_op jit(solution)/shard_map/while/body/eval_jaxpr/all_to_all | solution.py:19
  487.1 17.0 %all-to-all-done.1 = f32[64,1,2048]{2,1,0:T(1,128)S(1)} async-done(((f32[64,1,2048]{2,1,0:T(1,128)}), f32[64,1,2048]{2,1,0:T(1,128)S(1)}, u32[]{:S(2)}, u32[]{:S(2)}) %all-to-all-start.1) | async-done | bytes 524320 | tf_op jit(solution)/shard_map/while/body/eval_jaxpr/all_to_all | solution.py:19
  506.0 3.4 fusion.23
  510.3 1.9 collective-permute-start
  512.3 8.6 %collective-permute-done = f32[512,32]{1,0:T(8,128)S(1)} collective-permute-done((f32[512,32]{1,0:T(8,128)S(1)}, f32[512,32]{1,0:T(8,128)S(1)}, u32[]{:S(2)}, u32[]{:S(2)}) %collective-permute-start) | collective-permute-done | bytes 65568 | tf_op jit(solution)/shard_map/while/body/eval_jaxpr/ppermute | solution.py:10
  522.5 6.2 %all-to-all-start.2 = ((f32[64,1,2048]{2,1,0:T(1,128)}), f32[64,1,2048]{2,1,0:T(1,128)S(1)}, u32[]{:S(2)}, u32[]{:S(2)}) async-start(f32[64,1,2048]{2,1,0:T(1,128)} %broadcast_in_dim.72), calls=%async_computation.2 | async-start | bytes 1048576 | tf_op jit(solution)/shard_map/all_to_all | solution.py:19
  528.8 17.7 %all-to-all-done.2 = f32[64,1,2048]{2,1,0:T(1,128)S(1)} async-done(((f32[64,1,2048]{2,1,0:T(1,128)}), f32[64,1,2048]{2,1,0:T(1,128)S(1)}, u32[]{:S(2)}, u32[]{:S(2)}) %all-to-all-start.2) | async-done | bytes 524320 | tf_op jit(solution)/shard_map/all_to_all | solution.py:19
  546.4 2.1 reduce.2
  548.6 1.8 reshape.80
  550.3 4.0 fusion.4
  (130 shorter events, 55.6 us)
Async XLA Ops:
  1.5 519.8 %copy-start.2 = (f32[2,16,64]{2,1,0:T(8,128)S(1)}, f32[2,16,64]{2,1,0:T(8,128)}, u32[]{:S(2)}) copy-start(f32[2,16,64]{2,1,0:T(8,128)} %param.7) | copy-start | bytes 24580
  2.7 31.7 %all-to-all-start = ((f32[64,1,2048]{2,1,0:T(1,128)}), f32[64,1,2048]{2,1,0:T(1,128)S(1)}, u32[]{:S(2)}, u32[]{:S(2)}) async-start(f32[64,1,2048]{2,1,0:T(1,128)} %broadcast_in_dim.90), calls=%async_computation | async-start | bytes 1048576 | tf_op jit(solution)/shard_map/while/body/eval_jaxpr/all_to_all | solution.py:19
  42.1 23.4 %all-to-all-start.1 = ((f32[64,1,2048]{2,1,0:T(1,128)}), f32[64,1,2048]{2,1,0:T(1,128)S(1)}, u32[]{:S(2)}, u32[]{:S(2)}) async-start(f32[64,1,2048]{2,1,0:T(1,128)} %broadcast_in_dim.92), calls=%async_computation.1 | async-start | bytes 1048576 | tf_op jit(solution)/shard_map/while/body/eval_jaxpr/all_to_all | solution.py:19
  47.8 19.6 %copy-start.1 = (f32[32,4096]{1,0:T(8,128)S(1)}, f32[32,4096]{1,0:T(8,128)}, u32[]{:S(2)}) copy-start(f32[32,4096]{1,0:T(8,128)} %get-tuple-element.326) | copy-start | bytes 1572868 | tf_op jit(solution)/shard_map/while
  71.8 10.6 %collective-permute-start = (f32[512,32]{1,0:T(8,128)S(1)}, f32[512,32]{1,0:T(8,128)S(1)}, u32[]{:S(2)}, u32[]{:S(2)}) collective-permute-start(f32[512,32]{1,0:T(8,128)S(1)} %scatter_fusion), channel_id=1, source_target_pairs={{0,64},{64,128},{128,192},{192,256},{256,320},{320,384},{384,448},... | collective-permute-start | bytes 196616 | tf_op jit(solution)/shard_map/while/body/eval_jaxpr/ppermute | solution.py:10
  83.6 23.9 %all-to-all-start = ((f32[64,1,2048]{2,1,0:T(1,128)}), f32[64,1,2048]{2,1,0:T(1,128)S(1)}, u32[]{:S(2)}, u32[]{:S(2)}) async-start(f32[64,1,2048]{2,1,0:T(1,128)} %broadcast_in_dim.90), calls=%async_computation | async-start | bytes 1048576 | tf_op jit(solution)/shard_map/while/body/eval_jaxpr/all_to_all | solution.py:19
  115.2 23.4 %all-to-all-start.1 = ((f32[64,1,2048]{2,1,0:T(1,128)}), f32[64,1,2048]{2,1,0:T(1,128)S(1)}, u32[]{:S(2)}, u32[]{:S(2)}) async-start(f32[64,1,2048]{2,1,0:T(1,128)} %broadcast_in_dim.92), calls=%async_computation.1 | async-start | bytes 1048576 | tf_op jit(solution)/shard_map/while/body/eval_jaxpr/all_to_all | solution.py:19
  120.9 19.6 %copy-start.1 = (f32[32,4096]{1,0:T(8,128)S(1)}, f32[32,4096]{1,0:T(8,128)}, u32[]{:S(2)}) copy-start(f32[32,4096]{1,0:T(8,128)} %get-tuple-element.326) | copy-start | bytes 1572868 | tf_op jit(solution)/shard_map/while
  144.9 10.6 %collective-permute-start = (f32[512,32]{1,0:T(8,128)S(1)}, f32[512,32]{1,0:T(8,128)S(1)}, u32[]{:S(2)}, u32[]{:S(2)}) collective-permute-start(f32[512,32]{1,0:T(8,128)S(1)} %scatter_fusion), channel_id=1, source_target_pairs={{0,64},{64,128},{128,192},{192,256},{256,320},{320,384},{384,448},... | collective-permute-start | bytes 196616 | tf_op jit(solution)/shard_map/while/body/eval_jaxpr/ppermute | solution.py:10
  156.7 23.9 %all-to-all-start = ((f32[64,1,2048]{2,1,0:T(1,128)}), f32[64,1,2048]{2,1,0:T(1,128)S(1)}, u32[]{:S(2)}, u32[]{:S(2)}) async-start(f32[64,1,2048]{2,1,0:T(1,128)} %broadcast_in_dim.90), calls=%async_computation | async-start | bytes 1048576 | tf_op jit(solution)/shard_map/while/body/eval_jaxpr/all_to_all | solution.py:19
  188.3 23.4 %all-to-all-start.1 = ((f32[64,1,2048]{2,1,0:T(1,128)}), f32[64,1,2048]{2,1,0:T(1,128)S(1)}, u32[]{:S(2)}, u32[]{:S(2)}) async-start(f32[64,1,2048]{2,1,0:T(1,128)} %broadcast_in_dim.92), calls=%async_computation.1 | async-start | bytes 1048576 | tf_op jit(solution)/shard_map/while/body/eval_jaxpr/all_to_all | solution.py:19
  194.0 19.6 %copy-start.1 = (f32[32,4096]{1,0:T(8,128)S(1)}, f32[32,4096]{1,0:T(8,128)}, u32[]{:S(2)}) copy-start(f32[32,4096]{1,0:T(8,128)} %get-tuple-element.326) | copy-start | bytes 1572868 | tf_op jit(solution)/shard_map/while
  218.0 10.6 %collective-permute-start = (f32[512,32]{1,0:T(8,128)S(1)}, f32[512,32]{1,0:T(8,128)S(1)}, u32[]{:S(2)}, u32[]{:S(2)}) collective-permute-start(f32[512,32]{1,0:T(8,128)S(1)} %scatter_fusion), channel_id=1, source_target_pairs={{0,64},{64,128},{128,192},{192,256},{256,320},{320,384},{384,448},... | collective-permute-start | bytes 196616 | tf_op jit(solution)/shard_map/while/body/eval_jaxpr/ppermute | solution.py:10
  229.8 23.9 %all-to-all-start = ((f32[64,1,2048]{2,1,0:T(1,128)}), f32[64,1,2048]{2,1,0:T(1,128)S(1)}, u32[]{:S(2)}, u32[]{:S(2)}) async-start(f32[64,1,2048]{2,1,0:T(1,128)} %broadcast_in_dim.90), calls=%async_computation | async-start | bytes 1048576 | tf_op jit(solution)/shard_map/while/body/eval_jaxpr/all_to_all | solution.py:19
  261.4 23.4 %all-to-all-start.1 = ((f32[64,1,2048]{2,1,0:T(1,128)}), f32[64,1,2048]{2,1,0:T(1,128)S(1)}, u32[]{:S(2)}, u32[]{:S(2)}) async-start(f32[64,1,2048]{2,1,0:T(1,128)} %broadcast_in_dim.92), calls=%async_computation.1 | async-start | bytes 1048576 | tf_op jit(solution)/shard_map/while/body/eval_jaxpr/all_to_all | solution.py:19
  267.1 19.6 %copy-start.1 = (f32[32,4096]{1,0:T(8,128)S(1)}, f32[32,4096]{1,0:T(8,128)}, u32[]{:S(2)}) copy-start(f32[32,4096]{1,0:T(8,128)} %get-tuple-element.326) | copy-start | bytes 1572868 | tf_op jit(solution)/shard_map/while
  291.1 10.6 %collective-permute-start = (f32[512,32]{1,0:T(8,128)S(1)}, f32[512,32]{1,0:T(8,128)S(1)}, u32[]{:S(2)}, u32[]{:S(2)}) collective-permute-start(f32[512,32]{1,0:T(8,128)S(1)} %scatter_fusion), channel_id=1, source_target_pairs={{0,64},{64,128},{128,192},{192,256},{256,320},{320,384},{384,448},... | collective-permute-start | bytes 196616 | tf_op jit(solution)/shard_map/while/body/eval_jaxpr/ppermute | solution.py:10
  302.8 23.9 %all-to-all-start = ((f32[64,1,2048]{2,1,0:T(1,128)}), f32[64,1,2048]{2,1,0:T(1,128)S(1)}, u32[]{:S(2)}, u32[]{:S(2)}) async-start(f32[64,1,2048]{2,1,0:T(1,128)} %broadcast_in_dim.90), calls=%async_computation | async-start | bytes 1048576 | tf_op jit(solution)/shard_map/while/body/eval_jaxpr/all_to_all | solution.py:19
  334.5 23.4 %all-to-all-start.1 = ((f32[64,1,2048]{2,1,0:T(1,128)}), f32[64,1,2048]{2,1,0:T(1,128)S(1)}, u32[]{:S(2)}, u32[]{:S(2)}) async-start(f32[64,1,2048]{2,1,0:T(1,128)} %broadcast_in_dim.92), calls=%async_computation.1 | async-start | bytes 1048576 | tf_op jit(solution)/shard_map/while/body/eval_jaxpr/all_to_all | solution.py:19
  340.2 19.6 %copy-start.1 = (f32[32,4096]{1,0:T(8,128)S(1)}, f32[32,4096]{1,0:T(8,128)}, u32[]{:S(2)}) copy-start(f32[32,4096]{1,0:T(8,128)} %get-tuple-element.326) | copy-start | bytes 1572868 | tf_op jit(solution)/shard_map/while
  364.2 10.6 %collective-permute-start = (f32[512,32]{1,0:T(8,128)S(1)}, f32[512,32]{1,0:T(8,128)S(1)}, u32[]{:S(2)}, u32[]{:S(2)}) collective-permute-start(f32[512,32]{1,0:T(8,128)S(1)} %scatter_fusion), channel_id=1, source_target_pairs={{0,64},{64,128},{128,192},{192,256},{256,320},{320,384},{384,448},... | collective-permute-start | bytes 196616 | tf_op jit(solution)/shard_map/while/body/eval_jaxpr/ppermute | solution.py:10
  375.9 23.9 %all-to-all-start = ((f32[64,1,2048]{2,1,0:T(1,128)}), f32[64,1,2048]{2,1,0:T(1,128)S(1)}, u32[]{:S(2)}, u32[]{:S(2)}) async-start(f32[64,1,2048]{2,1,0:T(1,128)} %broadcast_in_dim.90), calls=%async_computation | async-start | bytes 1048576 | tf_op jit(solution)/shard_map/while/body/eval_jaxpr/all_to_all | solution.py:19
  407.6 23.4 %all-to-all-start.1 = ((f32[64,1,2048]{2,1,0:T(1,128)}), f32[64,1,2048]{2,1,0:T(1,128)S(1)}, u32[]{:S(2)}, u32[]{:S(2)}) async-start(f32[64,1,2048]{2,1,0:T(1,128)} %broadcast_in_dim.92), calls=%async_computation.1 | async-start | bytes 1048576 | tf_op jit(solution)/shard_map/while/body/eval_jaxpr/all_to_all | solution.py:19
  413.3 19.6 %copy-start.1 = (f32[32,4096]{1,0:T(8,128)S(1)}, f32[32,4096]{1,0:T(8,128)}, u32[]{:S(2)}) copy-start(f32[32,4096]{1,0:T(8,128)} %get-tuple-element.326) | copy-start | bytes 1572868 | tf_op jit(solution)/shard_map/while
  437.3 10.6 %collective-permute-start = (f32[512,32]{1,0:T(8,128)S(1)}, f32[512,32]{1,0:T(8,128)S(1)}, u32[]{:S(2)}, u32[]{:S(2)}) collective-permute-start(f32[512,32]{1,0:T(8,128)S(1)} %scatter_fusion), channel_id=1, source_target_pairs={{0,64},{64,128},{128,192},{192,256},{256,320},{320,384},{384,448},... | collective-permute-start | bytes 196616 | tf_op jit(solution)/shard_map/while/body/eval_jaxpr/ppermute | solution.py:10
  449.0 23.9 %all-to-all-start = ((f32[64,1,2048]{2,1,0:T(1,128)}), f32[64,1,2048]{2,1,0:T(1,128)S(1)}, u32[]{:S(2)}, u32[]{:S(2)}) async-start(f32[64,1,2048]{2,1,0:T(1,128)} %broadcast_in_dim.90), calls=%async_computation | async-start | bytes 1048576 | tf_op jit(solution)/shard_map/while/body/eval_jaxpr/all_to_all | solution.py:19
  480.7 23.4 %all-to-all-start.1 = ((f32[64,1,2048]{2,1,0:T(1,128)}), f32[64,1,2048]{2,1,0:T(1,128)S(1)}, u32[]{:S(2)}, u32[]{:S(2)}) async-start(f32[64,1,2048]{2,1,0:T(1,128)} %broadcast_in_dim.92), calls=%async_computation.1 | async-start | bytes 1048576 | tf_op jit(solution)/shard_map/while/body/eval_jaxpr/all_to_all | solution.py:19
  486.4 19.6 %copy-start.1 = (f32[32,4096]{1,0:T(8,128)S(1)}, f32[32,4096]{1,0:T(8,128)}, u32[]{:S(2)}) copy-start(f32[32,4096]{1,0:T(8,128)} %get-tuple-element.326) | copy-start | bytes 1572868 | tf_op jit(solution)/shard_map/while
  510.3 10.6 %collective-permute-start = (f32[512,32]{1,0:T(8,128)S(1)}, f32[512,32]{1,0:T(8,128)S(1)}, u32[]{:S(2)}, u32[]{:S(2)}) collective-permute-start(f32[512,32]{1,0:T(8,128)S(1)} %scatter_fusion), channel_id=1, source_target_pairs={{0,64},{64,128},{128,192},{192,256},{256,320},{320,384},{384,448},... | collective-permute-start | bytes 196616 | tf_op jit(solution)/shard_map/while/body/eval_jaxpr/ppermute | solution.py:10
  522.5 23.9 %all-to-all-start.2 = ((f32[64,1,2048]{2,1,0:T(1,128)}), f32[64,1,2048]{2,1,0:T(1,128)S(1)}, u32[]{:S(2)}, u32[]{:S(2)}) async-start(f32[64,1,2048]{2,1,0:T(1,128)} %broadcast_in_dim.72), calls=%async_computation.2 | async-start | bytes 1048576 | tf_op jit(solution)/shard_map/all_to_all | solution.py:19
  528.7 21.6 %copy-start = (f32[64,4096]{1,0:T(8,128)S(1)}, f32[64,4096]{1,0:T(8,128)}, u32[]{:S(2)}) copy-start(f32[64,4096]{1,0:T(8,128)} %get-tuple-element.336) | copy-start | bytes 3145732

commit v4 on v2

--- a/solution.py
+++ b/solution.py
@@ -14,8 +14,8 @@
     parts = 1
     for axis in axes:
         parts *= lax.axis_size(axis)
-    copies = jnp.broadcast_to(block[None], (parts,) + block.shape)
-    pieces = lax.all_to_all(copies, axes, 0, 0, tiled=True)
+    copies = jnp.broadcast_to(block.reshape(1, block.size), (parts, block.size))
+    pieces = lax.all_to_all(copies, axes, 0, 0, tiled=True).reshape((parts,) + block.shape)
     return jnp.transpose(pieces, (1, 0, 2)).reshape(block.shape[0], parts * block.shape[1])
 
 

time: 554 us -> 530 us (0.957)
  local copies, waits for them, and re-layouts: 67.8 us -> 52.8 us
  other arithmetic: 38.9 us -> 29.4 us
    while x63 -> x35, local copies, waits for them, and re-layouts: 36.9 us -> 10.9 us
    broadcast_in_dim x15 -> x30, local copies, waits for them, and re-layouts: 1.82 us -> 17.1 us  [gathered(): copies = jnp.broadcast_to(block.reshape(1, block.size), (parts, block.size))]
    all_to_all x15, other arithmetic: 28 us -> 18.6 us  [gathered(): lax.all_to_all(copies, axes, 0, 0, tiled=True)]
    all_to_all x15 -> x0, local copies, waits for them, and re-layouts: 8.56 us -> none  [gathered(): pieces = lax.all_to_all(copies, axes, 0, 0, tiled=True)]
    reshape x0 -> x15, local copies, waits for them, and re-layouts: none -> 6.15 us  [gathered(): lax.all_to_all(copies, axes, 0, 0, tiled=True)]
where the time goes in v4:
time: 530 us; the launch traced here: 527 us
  waiting for transfers between devices  321 us (61%)
  starting transfers between devices  111 us (21%)
  local copies, waits for them, and re-layouts  52.8 us (10%)
  other arithmetic  29.4 us (6%)
  matrix products  12.1 us (2%)
    all_to_all x15, waiting for transfers between devices, gathered(): lax.all_to_all(copies, axes, 0, 0, tiled=True)  261 us
    all_to_all x15, starting transfers between devices, gathered(): lax.all_to_all(copies, axes, 0, 0, tiled=True)  97.1 us
    ppermute x7, waiting for transfers between devices, passed_along(): return lax.ppermute(block, axis, route)  60.2 us
    all_to_all x15, other arithmetic, gathered(): lax.all_to_all(copies, axes, 0, 0, tiled=True)  18.6 us
    broadcast_in_dim x30, local copies, waits for them, and re-layouts, gathered(): copies = jnp.broadcast_to(block.reshape(1, block.size), (parts, block.size))  17.1 us
    ppermute x7, starting transfers between devices, passed_along(): return lax.ppermute(block, axis, route)  13.8 us
    while x35, local copies, waits for them, and re-layouts  10.9 us
  transfers between devices with their start and end apart: 22, of which 22 were waited for; matrix products, arithmetic and copies ran while one was open for 1% of the time, Pallas kernels for 0%

profile of v4, /device:TPU:33, one launch (start us, length us, event | category | flops | bytes accessed | tf_op | source)
XLA Modules:
  0.0 527.1 jit_solution(16334895458933471196)
XLA Ops:
  1.5 494.7 %while.16 = (s32[]{:T(128)}, f32[32,512]{0,1:T(8,128)S(1)}, f32[32,64]{1,0:T(8,128)S(1)}, s32[32]{0:T(128)S(1)}, f32[32,64]{0,1:T(8,128)S(1)}, /*index=5*/f32[64...) while((s32[]{:T(128)}, f32[32,512]{0,1:T(8,128)S(1)}, ...), condition=%wide.region_2.3_spmd.clone, body=%wide.region_0.2_spmd.clone.sunk | while | flops 151003264 | bytes 22029112 | solution.py:64
  1.7 1.1 broadcast_in_dim.90
  2.8 14.0 %all-to-all-start = ((f32[64,1,2048]{2,1,0:T(1,128)}), f32[64,1,2048]{2,1,0:T(1,128)S(1)}, u32[]{:S(2)}, u32[]{:S(2)}) async-start(f32[64,1,2048]{2,1,0:T(1,128)} %broadcast_in_dim.90), calls=%async_computation | async-start | bytes 1048576 | tf_op jit(solution)/shard_map/while/body/eval_jaxpr/all_to_all | solution.py:18
  16.8 17.7 %all-to-all-done = f32[64,1,2048]{2,1,0:T(1,128)S(1)} async-done(((f32[64,1,2048]{2,1,0:T(1,128)}), f32[64,1,2048]{2,1,0:T(1,128)S(1)}, u32[]{:S(2)}, u32[]{:S(2)}) %all-to-all-start) | async-done | bytes 524320 | tf_op jit(solution)/shard_map/while/body/eval_jaxpr/all_to_all | solution.py:18
  34.5 1.2 reduce.5
  40.1 5.7 %all-to-all-start.1 = ((f32[64,1,2048]{2,1,0:T(1,128)}), f32[64,1,2048]{2,1,0:T(1,128)S(1)}, u32[]{:S(2)}, u32[]{:S(2)}) async-start(f32[64,1,2048]{2,1,0:T(1,128)} %broadcast_in_dim.92), calls=%async_computation.1 | async-start | bytes 1048576 | tf_op jit(solution)/shard_map/while/body/eval_jaxpr/all_to_all | solution.py:18
  46.4 17.0 %all-to-all-done.1 = f32[64,1,2048]{2,1,0:T(1,128)S(1)} async-done(((f32[64,1,2048]{2,1,0:T(1,128)}), f32[64,1,2048]{2,1,0:T(1,128)S(1)}, u32[]{:S(2)}, u32[]{:S(2)}) %all-to-all-start.1) | async-done | bytes 524320 | tf_op jit(solution)/shard_map/while/body/eval_jaxpr/all_to_all | solution.py:18
  63.4 1.2 reduce.6
  68.3 2.3 collective-permute-start
  70.6 8.3 %collective-permute-done = f32[32,512]{0,1:T(8,128)S(1)} collective-permute-done((f32[32,512]{0,1:T(8,128)S(1)}, f32[32,512]{0,1:T(8,128)S(1)}, u32[]{:S(2)}, u32[]{:S(2)}) %collective-permute-start) | collective-permute-done | bytes 65568 | tf_op jit(solution)/shard_map/while/body/eval_jaxpr/ppermute | solution.py:10
  79.0 1.1 broadcast_in_dim.90
  80.1 6.2 %all-to-all-start = ((f32[64,1,2048]{2,1,0:T(1,128)}), f32[64,1,2048]{2,1,0:T(1,128)S(1)}, u32[]{:S(2)}, u32[]{:S(2)}) async-start(f32[64,1,2048]{2,1,0:T(1,128)} %broadcast_in_dim.90), calls=%async_computation | async-start | bytes 1048576 | tf_op jit(solution)/shard_map/while/body/eval_jaxpr/all_to_all | solution.py:18
  86.3 17.7 %all-to-all-done = f32[64,1,2048]{2,1,0:T(1,128)S(1)} async-done(((f32[64,1,2048]{2,1,0:T(1,128)}), f32[64,1,2048]{2,1,0:T(1,128)S(1)}, u32[]{:S(2)}, u32[]{:S(2)}) %all-to-all-start) | async-done | bytes 524320 | tf_op jit(solution)/shard_map/while/body/eval_jaxpr/all_to_all | solution.py:18
  104.0 1.2 reduce.5
  109.6 5.7 %all-to-all-start.1 = ((f32[64,1,2048]{2,1,0:T(1,128)}), f32[64,1,2048]{2,1,0:T(1,128)S(1)}, u32[]{:S(2)}, u32[]{:S(2)}) async-start(f32[64,1,2048]{2,1,0:T(1,128)} %broadcast_in_dim.92), calls=%async_computation.1 | async-start | bytes 1048576 | tf_op jit(solution)/shard_map/while/body/eval_jaxpr/all_to_all | solution.py:18
  116.0 17.0 %all-to-all-done.1 = f32[64,1,2048]{2,1,0:T(1,128)S(1)} async-done(((f32[64,1,2048]{2,1,0:T(1,128)}), f32[64,1,2048]{2,1,0:T(1,128)S(1)}, u32[]{:S(2)}, u32[]{:S(2)}) %all-to-all-start.1) | async-done | bytes 524320 | tf_op jit(solution)/shard_map/while/body/eval_jaxpr/all_to_all | solution.py:18
  133.0 1.2 reduce.6
  137.8 1.9 collective-permute-start
  139.8 8.7 %collective-permute-done = f32[32,512]{0,1:T(8,128)S(1)} collective-permute-done((f32[32,512]{0,1:T(8,128)S(1)}, f32[32,512]{0,1:T(8,128)S(1)}, u32[]{:S(2)}, u32[]{:S(2)}) %collective-permute-start) | collective-permute-done | bytes 65568 | tf_op jit(solution)/shard_map/while/body/eval_jaxpr/ppermute | solution.py:10
  148.6 1.1 broadcast_in_dim.90
  149.7 6.2 %all-to-all-start = ((f32[64,1,2048]{2,1,0:T(1,128)}), f32[64,1,2048]{2,1,0:T(1,128)S(1)}, u32[]{:S(2)}, u32[]{:S(2)}) async-start(f32[64,1,2048]{2,1,0:T(1,128)} %broadcast_in_dim.90), calls=%async_computation | async-start | bytes 1048576 | tf_op jit(solution)/shard_map/while/body/eval_jaxpr/all_to_all | solution.py:18
  155.9 17.7 %all-to-all-done = f32[64,1,2048]{2,1,0:T(1,128)S(1)} async-done(((f32[64,1,2048]{2,1,0:T(1,128)}), f32[64,1,2048]{2,1,0:T(1,128)S(1)}, u32[]{:S(2)}, u32[]{:S(2)}) %all-to-all-start) | async-done | bytes 524320 | tf_op jit(solution)/shard_map/while/body/eval_jaxpr/all_to_all | solution.py:18
  173.6 1.2 reduce.5
  179.2 5.7 %all-to-all-start.1 = ((f32[64,1,2048]{2,1,0:T(1,128)}), f32[64,1,2048]{2,1,0:T(1,128)S(1)}, u32[]{:S(2)}, u32[]{:S(2)}) async-start(f32[64,1,2048]{2,1,0:T(1,128)} %broadcast_in_dim.92), calls=%async_computation.1 | async-start | bytes 1048576 | tf_op jit(solution)/shard_map/while/body/eval_jaxpr/all_to_all | solution.py:18
  185.5 17.0 %all-to-all-done.1 = f32[64,1,2048]{2,1,0:T(1,128)S(1)} async-done(((f32[64,1,2048]{2,1,0:T(1,128)}), f32[64,1,2048]{2,1,0:T(1,128)S(1)}, u32[]{:S(2)}, u32[]{:S(2)}) %all-to-all-start.1) | async-done | bytes 524320 | tf_op jit(solution)/shard_map/while/body/eval_jaxpr/all_to_all | solution.py:18
  202.6 1.2 reduce.6
  207.4 1.9 collective-permute-start
  209.3 8.7 %collective-permute-done = f32[32,512]{0,1:T(8,128)S(1)} collective-permute-done((f32[32,512]{0,1:T(8,128)S(1)}, f32[32,512]{0,1:T(8,128)S(1)}, u32[]{:S(2)}, u32[]{:S(2)}) %collective-permute-start) | collective-permute-done | bytes 65568 | tf_op jit(solution)/shard_map/while/body/eval_jaxpr/ppermute | solution.py:10
  219.2 6.2 %all-to-all-start = ((f32[64,1,2048]{2,1,0:T(1,128)}), f32[64,1,2048]{2,1,0:T(1,128)S(1)}, u32[]{:S(2)}, u32[]{:S(2)}) async-start(f32[64,1,2048]{2,1,0:T(1,128)} %broadcast_in_dim.90), calls=%async_computation | async-start | bytes 1048576 | tf_op jit(solution)/shard_map/while/body/eval_jaxpr/all_to_all | solution.py:18
  225.4 17.7 %all-to-all-done = f32[64,1,2048]{2,1,0:T(1,128)S(1)} async-done(((f32[64,1,2048]{2,1,0:T(1,128)}), f32[64,1,2048]{2,1,0:T(1,128)S(1)}, u32[]{:S(2)}, u32[]{:S(2)}) %all-to-all-start) | async-done | bytes 524320 | tf_op jit(solution)/shard_map/while/body/eval_jaxpr/all_to_all | solution.py:18
  243.1 1.2 reduce.5
  248.7 5.7 %all-to-all-start.1 = ((f32[64,1,2048]{2,1,0:T(1,128)}), f32[64,1,2048]{2,1,0:T(1,128)S(1)}, u32[]{:S(2)}, u32[]{:S(2)}) async-start(f32[64,1,2048]{2,1,0:T(1,128)} %broadcast_in_dim.92), calls=%async_computation.1 | async-start | bytes 1048576 | tf_op jit(solution)/shard_map/while/body/eval_jaxpr/all_to_all | solution.py:18
  255.1 17.0 %all-to-all-done.1 = f32[64,1,2048]{2,1,0:T(1,128)S(1)} async-done(((f32[64,1,2048]{2,1,0:T(1,128)}), f32[64,1,2048]{2,1,0:T(1,128)S(1)}, u32[]{:S(2)}, u32[]{:S(2)}) %all-to-all-start.1) | async-done | bytes 524320 | tf_op jit(solution)/shard_map/while/body/eval_jaxpr/all_to_all | solution.py:18
  272.1 1.2 reduce.6
  276.9 1.9 collective-permute-start
  278.9 8.7 %collective-permute-done = f32[32,512]{0,1:T(8,128)S(1)} collective-permute-done((f32[32,512]{0,1:T(8,128)S(1)}, f32[32,512]{0,1:T(8,128)S(1)}, u32[]{:S(2)}, u32[]{:S(2)}) %collective-permute-start) | collective-permute-done | bytes 65568 | tf_op jit(solution)/shard_map/while/body/eval_jaxpr/ppermute | solution.py:10
  288.8 6.2 %all-to-all-start = ((f32[64,1,2048]{2,1,0:T(1,128)}), f32[64,1,2048]{2,1,0:T(1,128)S(1)}, u32[]{:S(2)}, u32[]{:S(2)}) async-start(f32[64,1,2048]{2,1,0:T(1,128)} %broadcast_in_dim.90), calls=%async_computation | async-start | bytes 1048576 | tf_op jit(solution)/shard_map/while/body/eval_jaxpr/all_to_all | solution.py:18
  295.0 17.7 %all-to-all-done = f32[64,1,2048]{2,1,0:T(1,128)S(1)} async-done(((f32[64,1,2048]{2,1,0:T(1,128)}), f32[64,1,2048]{2,1,0:T(1,128)S(1)}, u32[]{:S(2)}, u32[]{:S(2)}) %all-to-all-start) | async-done | bytes 524320 | tf_op jit(solution)/shard_map/while/body/eval_jaxpr/all_to_all | solution.py:18
  312.7 1.2 reduce.5
  318.3 5.7 %all-to-all-start.1 = ((f32[64,1,2048]{2,1,0:T(1,128)}), f32[64,1,2048]{2,1,0:T(1,128)S(1)}, u32[]{:S(2)}, u32[]{:S(2)}) async-start(f32[64,1,2048]{2,1,0:T(1,128)} %broadcast_in_dim.92), calls=%async_computation.1 | async-start | bytes 1048576 | tf_op jit(solution)/shard_map/while/body/eval_jaxpr/all_to_all | solution.py:18
  324.7 17.0 %all-to-all-done.1 = f32[64,1,2048]{2,1,0:T(1,128)S(1)} async-done(((f32[64,1,2048]{2,1,0:T(1,128)}), f32[64,1,2048]{2,1,0:T(1,128)S(1)}, u32[]{:S(2)}, u32[]{:S(2)}) %all-to-all-start.1) | async-done | bytes 524320 | tf_op jit(solution)/shard_map/while/body/eval_jaxpr/all_to_all | solution.py:18
  341.7 1.2 reduce.6
  346.5 1.9 collective-permute-start
  348.4 8.7 %collective-permute-done = f32[32,512]{0,1:T(8,128)S(1)} collective-permute-done((f32[32,512]{0,1:T(8,128)S(1)}, f32[32,512]{0,1:T(8,128)S(1)}, u32[]{:S(2)}, u32[]{:S(2)}) %collective-permute-start) | collective-permute-done | bytes 65568 | tf_op jit(solution)/shard_map/while/body/eval_jaxpr/ppermute | solution.py:10
  358.4 6.2 %all-to-all-start = ((f32[64,1,2048]{2,1,0:T(1,128)}), f32[64,1,2048]{2,1,0:T(1,128)S(1)}, u32[]{:S(2)}, u32[]{:S(2)}) async-start(f32[64,1,2048]{2,1,0:T(1,128)} %broadcast_in_dim.90), calls=%async_computation | async-start | bytes 1048576 | tf_op jit(solution)/shard_map/while/body/eval_jaxpr/all_to_all | solution.py:18
  364.6 17.7 %all-to-all-done = f32[64,1,2048]{2,1,0:T(1,128)S(1)} async-done(((f32[64,1,2048]{2,1,0:T(1,128)}), f32[64,1,2048]{2,1,0:T(1,128)S(1)}, u32[]{:S(2)}, u32[]{:S(2)}) %all-to-all-start) | async-done | bytes 524320 | tf_op jit(solution)/shard_map/while/body/eval_jaxpr/all_to_all | solution.py:18
  382.2 1.2 reduce.5
  387.9 5.7 %all-to-all-start.1 = ((f32[64,1,2048]{2,1,0:T(1,128)}), f32[64,1,2048]{2,1,0:T(1,128)S(1)}, u32[]{:S(2)}, u32[]{:S(2)}) async-start(f32[64,1,2048]{2,1,0:T(1,128)} %broadcast_in_dim.92), calls=%async_computation.1 | async-start | bytes 1048576 | tf_op jit(solution)/shard_map/while/body/eval_jaxpr/all_to_all | solution.py:18
  394.2 17.0 %all-to-all-done.1 = f32[64,1,2048]{2,1,0:T(1,128)S(1)} async-done(((f32[64,1,2048]{2,1,0:T(1,128)}), f32[64,1,2048]{2,1,0:T(1,128)S(1)}, u32[]{:S(2)}, u32[]{:S(2)}) %all-to-all-start.1) | async-done | bytes 524320 | tf_op jit(solution)/shard_map/while/body/eval_jaxpr/all_to_all | solution.py:18
  411.2 1.2 reduce.6
  416.1 1.9 collective-permute-start
  418.0 8.7 %collective-permute-done = f32[32,512]{0,1:T(8,128)S(1)} collective-permute-done((f32[32,512]{0,1:T(8,128)S(1)}, f32[32,512]{0,1:T(8,128)S(1)}, u32[]{:S(2)}, u32[]{:S(2)}) %collective-permute-start) | collective-permute-done | bytes 65568 | tf_op jit(solution)/shard_map/while/body/eval_jaxpr/ppermute | solution.py:10
  427.9 6.2 %all-to-all-start = ((f32[64,1,2048]{2,1,0:T(1,128)}), f32[64,1,2048]{2,1,0:T(1,128)S(1)}, u32[]{:S(2)}, u32[]{:S(2)}) async-start(f32[64,1,2048]{2,1,0:T(1,128)} %broadcast_in_dim.90), calls=%async_computation | async-start | bytes 1048576 | tf_op jit(solution)/shard_map/while/body/eval_jaxpr/all_to_all | solution.py:18
  434.1 17.7 %all-to-all-done = f32[64,1,2048]{2,1,0:T(1,128)S(1)} async-done(((f32[64,1,2048]{2,1,0:T(1,128)}), f32[64,1,2048]{2,1,0:T(1,128)S(1)}, u32[]{:S(2)}, u32[]{:S(2)}) %all-to-all-start) | async-done | bytes 524320 | tf_op jit(solution)/shard_map/while/body/eval_jaxpr/all_to_all | solution.py:18
  451.8 1.2 reduce.5
  457.4 5.7 %all-to-all-start.1 = ((f32[64,1,2048]{2,1,0:T(1,128)}), f32[64,1,2048]{2,1,0:T(1,128)S(1)}, u32[]{:S(2)}, u32[]{:S(2)}) async-start(f32[64,1,2048]{2,1,0:T(1,128)} %broadcast_in_dim.92), calls=%async_computation.1 | async-start | bytes 1048576 | tf_op jit(solution)/shard_map/while/body/eval_jaxpr/all_to_all | solution.py:18
  463.8 17.0 %all-to-all-done.1 = f32[64,1,2048]{2,1,0:T(1,128)S(1)} async-done(((f32[64,1,2048]{2,1,0:T(1,128)}), f32[64,1,2048]{2,1,0:T(1,128)S(1)}, u32[]{:S(2)}, u32[]{:S(2)}) %all-to-all-start.1) | async-done | bytes 524320 | tf_op jit(solution)/shard_map/while/body/eval_jaxpr/all_to_all | solution.py:18
  480.8 1.2 reduce.6
  485.6 1.9 collective-permute-start
  487.5 8.7 %collective-permute-done = f32[32,512]{0,1:T(8,128)S(1)} collective-permute-done((f32[32,512]{0,1:T(8,128)S(1)}, f32[32,512]{0,1:T(8,128)S(1)}, u32[]{:S(2)}, u32[]{:S(2)}) %collective-permute-start) | collective-permute-done | bytes 65568 | tf_op jit(solution)/shard_map/while/body/eval_jaxpr/ppermute | solution.py:10
  498.2 6.2 %all-to-all-start.2 = ((f32[64,1,2048]{2,1,0:T(1,128)}), f32[64,1,2048]{2,1,0:T(1,128)S(1)}, u32[]{:S(2)}, u32[]{:S(2)}) async-start(f32[64,1,2048]{2,1,0:T(1,128)} %broadcast_in_dim.72), calls=%async_computation.2 | async-start | bytes 1048576 | tf_op jit(solution)/shard_map/all_to_all | solution.py:18
  504.4 17.7 %all-to-all-done.2 = f32[64,1,2048]{2,1,0:T(1,128)S(1)} async-done(((f32[64,1,2048]{2,1,0:T(1,128)}), f32[64,1,2048]{2,1,0:T(1,128)S(1)}, u32[]{:S(2)}, u32[]{:S(2)}) %all-to-all-start.2) | async-done | bytes 524320 | tf_op jit(solution)/shard_map/all_to_all | solution.py:18
  522.0 1.2 reduce.2
  525.6 1.6 convolution_select_fusion.1
  (175 shorter events, 70.9 us)
Async XLA Ops:
  0.8 0.7 copy-start.4
  2.8 31.7 %all-to-all-start = ((f32[64,1,2048]{2,1,0:T(1,128)}), f32[64,1,2048]{2,1,0:T(1,128)S(1)}, u32[]{:S(2)}, u32[]{:S(2)}) async-start(f32[64,1,2048]{2,1,0:T(1,128)} %broadcast_in_dim.90), calls=%async_computation | async-start | bytes 1048576 | tf_op jit(solution)/shard_map/while/body/eval_jaxpr/all_to_all | solution.py:18
  36.7 1.2 copy-start
  40.1 23.4 %all-to-all-start.1 = ((f32[64,1,2048]{2,1,0:T(1,128)}), f32[64,1,2048]{2,1,0:T(1,128)S(1)}, u32[]{:S(2)}, u32[]{:S(2)}) async-start(f32[64,1,2048]{2,1,0:T(1,128)} %broadcast_in_dim.92), calls=%async_computation.1 | async-start | bytes 1048576 | tf_op jit(solution)/shard_map/while/body/eval_jaxpr/all_to_all | solution.py:18
  65.7 1.0 copy-start.2
  68.3 10.6 %collective-permute-start = (f32[32,512]{0,1:T(8,128)S(1)}, f32[32,512]{0,1:T(8,128)S(1)}, u32[]{:S(2)}, u32[]{:S(2)}) collective-permute-start(f32[32,512]{0,1:T(8,128)S(1)} %scatter_fusion), channel_id=1, source_target_pairs={{0,64},{64,128},{128,192},{192,256},{256,320},{320,384},{384,448},... | collective-permute-start | bytes 196616 | tf_op jit(solution)/shard_map/while/body/eval_jaxpr/ppermute | solution.py:10
  80.1 23.9 %all-to-all-start = ((f32[64,1,2048]{2,1,0:T(1,128)}), f32[64,1,2048]{2,1,0:T(1,128)S(1)}, u32[]{:S(2)}, u32[]{:S(2)}) async-start(f32[64,1,2048]{2,1,0:T(1,128)} %broadcast_in_dim.90), calls=%async_computation | async-start | bytes 1048576 | tf_op jit(solution)/shard_map/while/body/eval_jaxpr/all_to_all | solution.py:18
  106.3 1.2 copy-start
  109.6 23.4 %all-to-all-start.1 = ((f32[64,1,2048]{2,1,0:T(1,128)}), f32[64,1,2048]{2,1,0:T(1,128)S(1)}, u32[]{:S(2)}, u32[]{:S(2)}) async-start(f32[64,1,2048]{2,1,0:T(1,128)} %broadcast_in_dim.92), calls=%async_computation.1 | async-start | bytes 1048576 | tf_op jit(solution)/shard_map/while/body/eval_jaxpr/all_to_all | solution.py:18
  135.3 1.0 copy-start.2
  137.8 10.6 %collective-permute-start = (f32[32,512]{0,1:T(8,128)S(1)}, f32[32,512]{0,1:T(8,128)S(1)}, u32[]{:S(2)}, u32[]{:S(2)}) collective-permute-start(f32[32,512]{0,1:T(8,128)S(1)} %scatter_fusion), channel_id=1, source_target_pairs={{0,64},{64,128},{128,192},{192,256},{256,320},{320,384},{384,448},... | collective-permute-start | bytes 196616 | tf_op jit(solution)/shard_map/while/body/eval_jaxpr/ppermute | solution.py:10
  149.7 23.9 %all-to-all-start = ((f32[64,1,2048]{2,1,0:T(1,128)}), f32[64,1,2048]{2,1,0:T(1,128)S(1)}, u32[]{:S(2)}, u32[]{:S(2)}) async-start(f32[64,1,2048]{2,1,0:T(1,128)} %broadcast_in_dim.90), calls=%async_computation | async-start | bytes 1048576 | tf_op jit(solution)/shard_map/while/body/eval_jaxpr/all_to_all | solution.py:18
  175.9 1.2 copy-start
  179.2 23.4 %all-to-all-start.1 = ((f32[64,1,2048]{2,1,0:T(1,128)}), f32[64,1,2048]{2,1,0:T(1,128)S(1)}, u32[]{:S(2)}, u32[]{:S(2)}) async-start(f32[64,1,2048]{2,1,0:T(1,128)} %broadcast_in_dim.92), calls=%async_computation.1 | async-start | bytes 1048576 | tf_op jit(solution)/shard_map/while/body/eval_jaxpr/all_to_all | solution.py:18
  204.8 1.0 copy-start.2
  207.4 10.6 %collective-permute-start = (f32[32,512]{0,1:T(8,128)S(1)}, f32[32,512]{0,1:T(8,128)S(1)}, u32[]{:S(2)}, u32[]{:S(2)}) collective-permute-start(f32[32,512]{0,1:T(8,128)S(1)} %scatter_fusion), channel_id=1, source_target_pairs={{0,64},{64,128},{128,192},{192,256},{256,320},{320,384},{384,448},... | collective-permute-start | bytes 196616 | tf_op jit(solution)/shard_map/while/body/eval_jaxpr/ppermute | solution.py:10
  219.2 23.9 %all-to-all-start = ((f32[64,1,2048]{2,1,0:T(1,128)}), f32[64,1,2048]{2,1,0:T(1,128)S(1)}, u32[]{:S(2)}, u32[]{:S(2)}) async-start(f32[64,1,2048]{2,1,0:T(1,128)} %broadcast_in_dim.90), calls=%async_computation | async-start | bytes 1048576 | tf_op jit(solution)/shard_map/while/body/eval_jaxpr/all_to_all | solution.py:18
  245.4 1.2 copy-start
  248.7 23.4 %all-to-all-start.1 = ((f32[64,1,2048]{2,1,0:T(1,128)}), f32[64,1,2048]{2,1,0:T(1,128)S(1)}, u32[]{:S(2)}, u32[]{:S(2)}) async-start(f32[64,1,2048]{2,1,0:T(1,128)} %broadcast_in_dim.92), calls=%async_computation.1 | async-start | bytes 1048576 | tf_op jit(solution)/shard_map/while/body/eval_jaxpr/all_to_all | solution.py:18
  274.4 1.0 copy-start.2
  276.9 10.6 %collective-permute-start = (f32[32,512]{0,1:T(8,128)S(1)}, f32[32,512]{0,1:T(8,128)S(1)}, u32[]{:S(2)}, u32[]{:S(2)}) collective-permute-start(f32[32,512]{0,1:T(8,128)S(1)} %scatter_fusion), channel_id=1, source_target_pairs={{0,64},{64,128},{128,192},{192,256},{256,320},{320,384},{384,448},... | collective-permute-start | bytes 196616 | tf_op jit(solution)/shard_map/while/body/eval_jaxpr/ppermute | solution.py:10
  288.8 23.9 %all-to-all-start = ((f32[64,1,2048]{2,1,0:T(1,128)}), f32[64,1,2048]{2,1,0:T(1,128)S(1)}, u32[]{:S(2)}, u32[]{:S(2)}) async-start(f32[64,1,2048]{2,1,0:T(1,128)} %broadcast_in_dim.90), calls=%async_computation | async-start | bytes 1048576 | tf_op jit(solution)/shard_map/while/body/eval_jaxpr/all_to_all | solution.py:18
  315.0 1.2 copy-start
  318.3 23.4 %all-to-all-start.1 = ((f32[64,1,2048]{2,1,0:T(1,128)}), f32[64,1,2048]{2,1,0:T(1,128)S(1)}, u32[]{:S(2)}, u32[]{:S(2)}) async-start(f32[64,1,2048]{2,1,0:T(1,128)} %broadcast_in_dim.92), calls=%async_computation.1 | async-start | bytes 1048576 | tf_op jit(solution)/shard_map/while/body/eval_jaxpr/all_to_all | solution.py:18
  344.0 1.0 copy-start.2
  346.5 10.6 %collective-permute-start = (f32[32,512]{0,1:T(8,128)S(1)}, f32[32,512]{0,1:T(8,128)S(1)}, u32[]{:S(2)}, u32[]{:S(2)}) collective-permute-start(f32[32,512]{0,1:T(8,128)S(1)} %scatter_fusion), channel_id=1, source_target_pairs={{0,64},{64,128},{128,192},{192,256},{256,320},{320,384},{384,448},... | collective-permute-start | bytes 196616 | tf_op jit(solution)/shard_map/while/body/eval_jaxpr/ppermute | solution.py:10
  358.4 23.9 %all-to-all-start = ((f32[64,1,2048]{2,1,0:T(1,128)}), f32[64,1,2048]{2,1,0:T(1,128)S(1)}, u32[]{:S(2)}, u32[]{:S(2)}) async-start(f32[64,1,2048]{2,1,0:T(1,128)} %broadcast_in_dim.90), calls=%async_computation | async-start | bytes 1048576 | tf_op jit(solution)/shard_map/while/body/eval_jaxpr/all_to_all | solution.py:18
  384.5 1.2 copy-start
  387.9 23.4 %all-to-all-start.1 = ((f32[64,1,2048]{2,1,0:T(1,128)}), f32[64,1,2048]{2,1,0:T(1,128)S(1)}, u32[]{:S(2)}, u32[]{:S(2)}) async-start(f32[64,1,2048]{2,1,0:T(1,128)} %broadcast_in_dim.92), calls=%async_computation.1 | async-start | bytes 1048576 | tf_op jit(solution)/shard_map/while/body/eval_jaxpr/all_to_all | solution.py:18
  413.5 1.0 copy-start.2
  416.1 10.6 %collective-permute-start = (f32[32,512]{0,1:T(8,128)S(1)}, f32[32,512]{0,1:T(8,128)S(1)}, u32[]{:S(2)}, u32[]{:S(2)}) collective-permute-start(f32[32,512]{0,1:T(8,128)S(1)} %scatter_fusion), channel_id=1, source_target_pairs={{0,64},{64,128},{128,192},{192,256},{256,320},{320,384},{384,448},... | collective-permute-start | bytes 196616 | tf_op jit(solution)/shard_map/while/body/eval_jaxpr/ppermute | solution.py:10
  427.9 23.9 %all-to-all-start = ((f32[64,1,2048]{2,1,0:T(1,128)}), f32[64,1,2048]{2,1,0:T(1,128)S(1)}, u32[]{:S(2)}, u32[]{:S(2)}) async-start(f32[64,1,2048]{2,1,0:T(1,128)} %broadcast_in_dim.90), calls=%async_computation | async-start | bytes 1048576 | tf_op jit(solution)/shard_map/while/body/eval_jaxpr/all_to_all | solution.py:18
  454.1 1.2 copy-start
  457.4 23.4 %all-to-all-start.1 = ((f32[64,1,2048]{2,1,0:T(1,128)}), f32[64,1,2048]{2,1,0:T(1,128)S(1)}, u32[]{:S(2)}, u32[]{:S(2)}) async-start(f32[64,1,2048]{2,1,0:T(1,128)} %broadcast_in_dim.92), calls=%async_computation.1 | async-start | bytes 1048576 | tf_op jit(solution)/shard_map/while/body/eval_jaxpr/all_to_all | solution.py:18
  483.1 1.0 copy-start.2
  485.6 10.6 %collective-permute-start = (f32[32,512]{0,1:T(8,128)S(1)}, f32[32,512]{0,1:T(8,128)S(1)}, u32[]{:S(2)}, u32[]{:S(2)}) collective-permute-start(f32[32,512]{0,1:T(8,128)S(1)} %scatter_fusion), channel_id=1, source_target_pairs={{0,64},{64,128},{128,192},{192,256},{256,320},{320,384},{384,448},... | collective-permute-start | bytes 196616 | tf_op jit(solution)/shard_map/while/body/eval_jaxpr/ppermute | solution.py:10
  496.2 0.7 copy-start.3
  498.2 23.9 %all-to-all-start.2 = ((f32[64,1,2048]{2,1,0:T(1,128)}), f32[64,1,2048]{2,1,0:T(1,128)S(1)}, u32[]{:S(2)}, u32[]{:S(2)}) async-start(f32[64,1,2048]{2,1,0:T(1,128)} %broadcast_in_dim.72), calls=%async_computation.2 | async-start | bytes 1048576 | tf_op jit(solution)/shard_map/all_to_all | solution.py:18
  524.3 1.2 copy-start.1

commit v5 on v4

--- a/solution.py
+++ b/solution.py
@@ -30,6 +30,7 @@
     lower_count = lower_rows.shape[0]
     live = jnp.arange(lower_count, dtype=jnp.int32) < counts[0, 0]
     places = targets[0] // width * own_rows + targets[0] % own_rows
+    axes = ("row", "col")
 
     def solve_piece(segment):
         return lax.dot_general(
@@ -49,22 +50,37 @@
             preferred_element_type=jnp.float32,
         )
 
+    own_col = lax.axis_index("col")
+    group_rows = lax.all_gather(diag_rows, "col", axis=0, tiled=True)
+
+    def finish(solved, carried):
+        update = lower_piece(solved)
+        update = jnp.where(live[None, :], update, jnp.float32(0.0))
+        carried = carried.at[:, places].add(update)
+        return passed_along(carried, "sep", 1)
+
     def one_level(level, state):
         carried, solution = state
         resid = given - lax.dynamic_slice_in_dim(carried, level * own_rows, own_rows, 1)
-        solved = solve_piece(gathered(resid, ("row", "col")))
+        group = lax.dot_general(
+            gathered(resid, axes),
+            group_rows,
+            (((1,), (1,)), ((), ())),
+            precision=lax.Precision.HIGHEST,
+            preferred_element_type=jnp.float32,
+        )
+        solved = lax.dynamic_slice_in_dim(group, own_col * own_rows, own_rows, 1)
         solution = jnp.where(own_level == level, solved, solution)
-        update = lower_piece(gathered(solved, ("row", "col")))
-        update = jnp.where(live[None, :], update, jnp.float32(0.0))
-        carried = carried.at[:, places].add(update)
-        return passed_along(carried, "sep", 1), solution
+        return finish(gathered(group, ("row",)), carried), solution
 
+    solved = solve_piece(gathered(given, axes))
+    solution = jnp.where(own_level == 0, solved, jnp.zeros_like(given))
     carried = jnp.zeros((given.shape[0], levels * own_rows), jnp.float32)
-    solution = jnp.zeros_like(given)
-    carried, solution = lax.fori_loop(0, levels - 1, one_level, (carried, solution))
+    carried = finish(gathered(solved, axes), carried)
+    carried, solution = lax.fori_loop(1, levels - 1, one_level, (carried, solution))
     last = levels - 1
     resid = given - carried[:, last * own_rows:]
-    solved = solve_piece(gathered(resid, ("row", "col")))
+    solved = solve_piece(gathered(resid, axes))
     solution = jnp.where(own_level == last, solved, solution)
     return solution.reshape(batches, width_rhs, own_rows)
 

time: 530 us -> 556 us (1.049)
  blocking collectives: 0 us -> 136 us
  waiting for transfers between devices: 321 us -> 216 us
  matrix products: 12.1 us -> 64.2 us
  starting transfers between devices: 111 us -> 60.3 us
  local copies, waits for them, and re-layouts: 52.8 us -> 33.4 us
  between operations: 0.07 us -> 14.2 us
    all_to_all x0 -> x6, blocking collectives: none -> 136 us  [gathered(): lax.all_to_all(copies, axes, 0, 0, tiled=True)]
    all_to_all x15 -> x9, waiting for transfers between devices: 261 us -> 156 us  [gathered(): lax.all_to_all(copies, axes, 0, 0, tiled=True)]
    dot_general x0 -> x6, matrix products: none -> 58.4 us  [one_level(): lax.dot_general(gathered(resid, axes), group_rows, (((1,), (1,)), ((), ()...]
    all_to_all x15 -> x9, starting transfers between devices: 97.1 us -> 46.3 us  [gathered(): lax.all_to_all(copies, axes, 0, 0, tiled=True)]
    while x36 -> x19, local copies, waits for them, and re-layouts: 11 us -> 2.17 us
    dot_general x8 -> x2, matrix products: 8.23 us -> 1.9 us  [solve_piece(): lax.dot_general(segment, diag_rows, (((1,), (1,)), ((), ())), precision=l...]
    broadcast_in_dim x30 -> x24, local copies, waits for them, and re-layouts: 17.1 us -> 13.1 us  [gathered(): copies = jnp.broadcast_to(block.reshape(1, block.size), (parts, block.size))]
  transfers between devices with their start and end apart: 22 -> 17, of which waited for: 22 -> 16; matrix products, arithmetic and copies ran while one was open for 1% -> 3% of each run, Pallas kernels for 0% -> 0%
where the time goes in v5:
time: 556 us; the launch traced here: 554 us
  waiting for transfers between devices  216 us (39%)
  blocking collectives  136 us (24%)
  matrix products  64.2 us (12%)
  starting transfers between devices  60.3 us (11%)
  local copies, waits for them, and re-layouts  33.4 us (6%)
  other arithmetic  29.8 us (5%)
  between operations  14.2 us (3%)
    all_to_all x9, waiting for transfers between devices, gathered(): lax.all_to_all(copies, axes, 0, 0, tiled=True)  156 us
    all_to_all x6, blocking collectives, gathered(): lax.all_to_all(copies, axes, 0, 0, tiled=True)  136 us
    ppermute x7, waiting for transfers between devices, passed_along(): return lax.ppermute(block, axis, route)  58.9 us
    dot_general x6, matrix products, one_level(): lax.dot_general(gathered(resid, axes), group_rows, (((1,), (1,)), ((), ()...  58.4 us
    all_to_all x9, starting transfers between devices, gathered(): lax.all_to_all(copies, axes, 0, 0, tiled=True)  46.3 us
    all_to_all x15, other arithmetic, gathered(): lax.all_to_all(copies, axes, 0, 0, tiled=True)  18.6 us
    ppermute x7, starting transfers between devices, passed_along(): return lax.ppermute(block, axis, route)  14 us
    broadcast_in_dim x24, local copies, waits for them, and re-layouts, gathered(): copies = jnp.broadcast_to(block.reshape(1, block.size), (parts, block.size))  13.1 us
  transfers between devices with their start and end apart: 17, of which 16 were waited for; matrix products, arithmetic and copies ran while one was open for 3% of the time, Pallas kernels for 0%

profile of v5, /device:TPU:33, one launch (start us, length us, event | category | flops | bytes accessed | tf_op | source)
XLA Modules:
  0.0 554.1 jit_solution(3689530089400419673)
XLA Ops:
  9.2 14.1 %all-to-all-start.2 = ((f32[64,1,2048]{2,1,0:T(1,128)}), f32[64,1,2048]{2,1,0:T(1,128)S(1)}, u32[]{:S(2)}, u32[]{:S(2)}) async-start(f32[64,1,2048]{2,1,0:T(1,128)} %broadcast_in_dim.100), calls=%async_computation.2 | async-start | bytes 1048576 | tf_op jit(solution)/shard_map/all_to_all | solution.py:18
  23.3 17.8 %all-to-all-done.2 = f32[64,1,2048]{2,1,0:T(1,128)S(1)} async-done(((f32[64,1,2048]{2,1,0:T(1,128)}), f32[64,1,2048]{2,1,0:T(1,128)S(1)}, u32[]{:S(2)}, u32[]{:S(2)}) %all-to-all-start.2) | async-done | bytes 524320 | tf_op jit(solution)/shard_map/all_to_all | solution.py:18
  41.1 1.2 reduce.2
  42.8 1.7 copy.28
  44.5 1.6 reshape.265
  48.2 5.7 %all-to-all-start.3 = ((f32[64,1,2048]{2,1,0:T(1,128)}), f32[64,1,2048]{2,1,0:T(1,128)S(1)}, u32[]{:S(2)}, u32[]{:S(2)}) async-start(f32[64,1,2048]{2,1,0:T(1,128)} %broadcast_in_dim.102), calls=%async_computation.3 | async-start | bytes 1048576 | tf_op jit(solution)/shard_map/all_to_all | solution.py:18
  54.6 17.1 %all-to-all-done.3 = f32[64,1,2048]{2,1,0:T(1,128)S(1)} async-done(((f32[64,1,2048]{2,1,0:T(1,128)}), f32[64,1,2048]{2,1,0:T(1,128)S(1)}, u32[]{:S(2)}, u32[]{:S(2)}) %all-to-all-start.3) | async-done | bytes 524320 | tf_op jit(solution)/shard_map/all_to_all | solution.py:18
  71.7 1.2 reduce.3
  75.8 2.5 collective-permute-start.1
  78.4 8.1 %collective-permute-done.1 = f32[32,512]{0,1:T(8,128)S(1)} collective-permute-done((f32[32,512]{0,1:T(8,128)S(1)}, f32[32,512]{0,1:T(8,128)S(1)}, u32[]{:S(2)}, u32[]{:S(2)}) %collective-permute-start.1) | collective-permute-done | bytes 65568 | tf_op jit(solution)/shard_map/ppermute | solution.py:10
  86.5 429.8 %while.18 = (s32[]{:T(128)}, f32[32,512]{0,1:T(8,128)S(1)}, f32[32,64]{1,0:T(8,128)S(1)}, s32[32]{0:T(128)S(1)}, f32[32,64]{0,1:T(8,128)S(1)}, /*index=5*/f32[51...) while((s32[]{:T(128)}, f32[32,512]{0,1:T(8,128)S(1)}, ...), condition=%wide.region_3.4_spmd.clone, body=%wide.region_1.3_spmd.clone.sunk | while | flops 855644288 | bytes 21742304 | solution.py:80
  86.9 23.6 %all_to_all.46 = f32[64,1,2048]{2,1,0:T(1,128)S(1)} all-to-all(f32[64,1,2048]{2,1,0:T(1,128)S(1)} %broadcast_in_dim.128), channel_id=1, replica_groups=mesh['sep'=8,'row'=8,'col'=8] {'row','col'}, dimensions={0} | all-to-all | bytes 1048576 | tf_op jit(solution)/shard_map/while/body/eval_jaxpr/all_to_all | solution.py:18
  110.5 1.2 reduce.7
  113.1 9.7 %fusion.35 = f32[32,512]{1,0:T(8,128)S(1)} fusion(f32[32,4096]{1,0:T(8,128)S(1)} %reshape.310, f32[512,4096]{1,0:T(8,128)} %get-tuple-element.415), kind=kOutput, calls=%fused_computation.42.clone.1 | convolution fusion | flops 805306368 | bytes 8978432 | tf_op jit(solution)/shard_map/while/body/eval_jaxpr/dot_general | solution.py:65
  124.0 3.5 all-to-all-start.1
  128.2 17.3 %all-to-all-done.1 = f32[8,1,16384]{2,1,0:T(1,128)S(1)} async-done(((f32[8,1,16384]{2,1,0:T(1,128)}), f32[8,1,16384]{2,1,0:T(1,128)S(1)}, u32[]{:S(2)}, u32[]{:S(2)}) %all-to-all-start.1) | async-done | bytes 524320 | tf_op jit(solution)/shard_map/while/body/eval_jaxpr/all_to_all | solution.py:18
  145.5 1.2 reduce.8
  148.6 1.9 collective-permute-start
  150.6 8.5 %collective-permute-done = f32[32,512]{0,1:T(8,128)S(1)} collective-permute-done((f32[32,512]{0,1:T(8,128)S(1)}, f32[32,512]{0,1:T(8,128)S(1)}, u32[]{:S(2)}, u32[]{:S(2)}) %collective-permute-start) | collective-permute-done | bytes 65568 | tf_op jit(solution)/shard_map/while/body/eval_jaxpr/ppermute | solution.py:10
  159.5 22.4 %all_to_all.46 = f32[64,1,2048]{2,1,0:T(1,128)S(1)} all-to-all(f32[64,1,2048]{2,1,0:T(1,128)S(1)} %broadcast_in_dim.128), channel_id=1, replica_groups=mesh['sep'=8,'row'=8,'col'=8] {'row','col'}, dimensions={0} | all-to-all | bytes 1048576 | tf_op jit(solution)/shard_map/while/body/eval_jaxpr/all_to_all | solution.py:18
  181.9 1.2 reduce.7
  184.6 9.7 %fusion.35 = f32[32,512]{1,0:T(8,128)S(1)} fusion(f32[32,4096]{1,0:T(8,128)S(1)} %reshape.310, f32[512,4096]{1,0:T(8,128)} %get-tuple-element.415), kind=kOutput, calls=%fused_computation.42.clone.1 | convolution fusion | flops 805306368 | bytes 8978432 | tf_op jit(solution)/shard_map/while/body/eval_jaxpr/dot_general | solution.py:65
  195.4 3.5 all-to-all-start.1
  199.6 17.3 %all-to-all-done.1 = f32[8,1,16384]{2,1,0:T(1,128)S(1)} async-done(((f32[8,1,16384]{2,1,0:T(1,128)}), f32[8,1,16384]{2,1,0:T(1,128)S(1)}, u32[]{:S(2)}, u32[]{:S(2)}) %all-to-all-start.1) | async-done | bytes 524320 | tf_op jit(solution)/shard_map/while/body/eval_jaxpr/all_to_all | solution.py:18
  216.9 1.2 reduce.8
  220.0 1.9 collective-permute-start
  222.0 8.5 %collective-permute-done = f32[32,512]{0,1:T(8,128)S(1)} collective-permute-done((f32[32,512]{0,1:T(8,128)S(1)}, f32[32,512]{0,1:T(8,128)S(1)}, u32[]{:S(2)}, u32[]{:S(2)}) %collective-permute-start) | collective-permute-done | bytes 65568 | tf_op jit(solution)/shard_map/while/body/eval_jaxpr/ppermute | solution.py:10
  231.0 22.4 %all_to_all.46 = f32[64,1,2048]{2,1,0:T(1,128)S(1)} all-to-all(f32[64,1,2048]{2,1,0:T(1,128)S(1)} %broadcast_in_dim.128), channel_id=1, replica_groups=mesh['sep'=8,'row'=8,'col'=8] {'row','col'}, dimensions={0} | all-to-all | bytes 1048576 | tf_op jit(solution)/shard_map/while/body/eval_jaxpr/all_to_all | solution.py:18
  253.4 1.2 reduce.7
  256.0 9.7 %fusion.35 = f32[32,512]{1,0:T(8,128)S(1)} fusion(f32[32,4096]{1,0:T(8,128)S(1)} %reshape.310, f32[512,4096]{1,0:T(8,128)} %get-tuple-element.415), kind=kOutput, calls=%fused_computation.42.clone.1 | convolution fusion | flops 805306368 | bytes 8978432 | tf_op jit(solution)/shard_map/while/body/eval_jaxpr/dot_general | solution.py:65
  266.9 3.5 all-to-all-start.1
  271.1 17.3 %all-to-all-done.1 = f32[8,1,16384]{2,1,0:T(1,128)S(1)} async-done(((f32[8,1,16384]{2,1,0:T(1,128)}), f32[8,1,16384]{2,1,0:T(1,128)S(1)}, u32[]{:S(2)}, u32[]{:S(2)}) %all-to-all-start.1) | async-done | bytes 524320 | tf_op jit(solution)/shard_map/while/body/eval_jaxpr/all_to_all | solution.py:18
  288.3 1.2 reduce.8
  291.5 1.9 collective-permute-start
  293.5 8.5 %collective-permute-done = f32[32,512]{0,1:T(8,128)S(1)} collective-permute-done((f32[32,512]{0,1:T(8,128)S(1)}, f32[32,512]{0,1:T(8,128)S(1)}, u32[]{:S(2)}, u32[]{:S(2)}) %collective-permute-start) | collective-permute-done | bytes 65568 | tf_op jit(solution)/shard_map/while/body/eval_jaxpr/ppermute | solution.py:10
  302.4 22.4 %all_to_all.46 = f32[64,1,2048]{2,1,0:T(1,128)S(1)} all-to-all(f32[64,1,2048]{2,1,0:T(1,128)S(1)} %broadcast_in_dim.128), channel_id=1, replica_groups=mesh['sep'=8,'row'=8,'col'=8] {'row','col'}, dimensions={0} | all-to-all | bytes 1048576 | tf_op jit(solution)/shard_map/while/body/eval_jaxpr/all_to_all | solution.py:18
  324.8 1.2 reduce.7
  327.5 9.7 %fusion.35 = f32[32,512]{1,0:T(8,128)S(1)} fusion(f32[32,4096]{1,0:T(8,128)S(1)} %reshape.310, f32[512,4096]{1,0:T(8,128)} %get-tuple-element.415), kind=kOutput, calls=%fused_computation.42.clone.1 | convolution fusion | flops 805306368 | bytes 8978432 | tf_op jit(solution)/shard_map/while/body/eval_jaxpr/dot_general | solution.py:65
  338.3 3.5 all-to-all-start.1
  342.5 17.3 %all-to-all-done.1 = f32[8,1,16384]{2,1,0:T(1,128)S(1)} async-done(((f32[8,1,16384]{2,1,0:T(1,128)}), f32[8,1,16384]{2,1,0:T(1,128)S(1)}, u32[]{:S(2)}, u32[]{:S(2)}) %all-to-all-start.1) | async-done | bytes 524320 | tf_op jit(solution)/shard_map/while/body/eval_jaxpr/all_to_all | solution.py:18
  359.8 1.2 reduce.8
  362.9 1.9 collective-permute-start
  364.9 8.5 %collective-permute-done = f32[32,512]{0,1:T(8,128)S(1)} collective-permute-done((f32[32,512]{0,1:T(8,128)S(1)}, f32[32,512]{0,1:T(8,128)S(1)}, u32[]{:S(2)}, u32[]{:S(2)}) %collective-permute-start) | collective-permute-done | bytes 65568 | tf_op jit(solution)/shard_map/while/body/eval_jaxpr/ppermute | solution.py:10
  373.9 22.4 %all_to_all.46 = f32[64,1,2048]{2,1,0:T(1,128)S(1)} all-to-all(f32[64,1,2048]{2,1,0:T(1,128)S(1)} %broadcast_in_dim.128), channel_id=1, replica_groups=mesh['sep'=8,'row'=8,'col'=8] {'row','col'}, dimensions={0} | all-to-all | bytes 1048576 | tf_op jit(solution)/shard_map/while/body/eval_jaxpr/all_to_all | solution.py:18
  396.3 1.2 reduce.7
  398.9 9.7 %fusion.35 = f32[32,512]{1,0:T(8,128)S(1)} fusion(f32[32,4096]{1,0:T(8,128)S(1)} %reshape.310, f32[512,4096]{1,0:T(8,128)} %get-tuple-element.415), kind=kOutput, calls=%fused_computation.42.clone.1 | convolution fusion | flops 805306368 | bytes 8978432 | tf_op jit(solution)/shard_map/while/body/eval_jaxpr/dot_general | solution.py:65
  409.8 3.5 all-to-all-start.1
  414.0 17.3 %all-to-all-done.1 = f32[8,1,16384]{2,1,0:T(1,128)S(1)} async-done(((f32[8,1,16384]{2,1,0:T(1,128)}), f32[8,1,16384]{2,1,0:T(1,128)S(1)}, u32[]{:S(2)}, u32[]{:S(2)}) %all-to-all-start.1) | async-done | bytes 524320 | tf_op jit(solution)/shard_map/while/body/eval_jaxpr/all_to_all | solution.py:18
  431.2 1.2 reduce.8
  434.3 1.9 collective-permute-start
  436.4 8.5 %collective-permute-done = f32[32,512]{0,1:T(8,128)S(1)} collective-permute-done((f32[32,512]{0,1:T(8,128)S(1)}, f32[32,512]{0,1:T(8,128)S(1)}, u32[]{:S(2)}, u32[]{:S(2)}) %collective-permute-start) | collective-permute-done | bytes 65568 | tf_op jit(solution)/shard_map/while/body/eval_jaxpr/ppermute | solution.py:10
  445.3 22.4 %all_to_all.46 = f32[64,1,2048]{2,1,0:T(1,128)S(1)} all-to-all(f32[64,1,2048]{2,1,0:T(1,128)S(1)} %broadcast_in_dim.128), channel_id=1, replica_groups=mesh['sep'=8,'row'=8,'col'=8] {'row','col'}, dimensions={0} | all-to-all | bytes 1048576 | tf_op jit(solution)/shard_map/while/body/eval_jaxpr/all_to_all | solution.py:18
  467.7 1.2 reduce.7
  470.3 9.7 %fusion.35 = f32[32,512]{1,0:T(8,128)S(1)} fusion(f32[32,4096]{1,0:T(8,128)S(1)} %reshape.310, f32[512,4096]{1,0:T(8,128)} %get-tuple-element.415), kind=kOutput, calls=%fused_computation.42.clone.1 | convolution fusion | flops 805306368 | bytes 8978432 | tf_op jit(solution)/shard_map/while/body/eval_jaxpr/dot_general | solution.py:65
  481.2 3.5 all-to-all-start.1
  485.4 17.3 %all-to-all-done.1 = f32[8,1,16384]{2,1,0:T(1,128)S(1)} async-done(((f32[8,1,16384]{2,1,0:T(1,128)}), f32[8,1,16384]{2,1,0:T(1,128)S(1)}, u32[]{:S(2)}, u32[]{:S(2)}) %all-to-all-start.1) | async-done | bytes 524320 | tf_op jit(solution)/shard_map/while/body/eval_jaxpr/all_to_all | solution.py:18
  502.7 1.2 reduce.8
  505.8 1.9 collective-permute-start
  507.8 8.5 %collective-permute-done = f32[32,512]{0,1:T(8,128)S(1)} collective-permute-done((f32[32,512]{0,1:T(8,128)S(1)}, f32[32,512]{0,1:T(8,128)S(1)}, u32[]{:S(2)}, u32[]{:S(2)}) %collective-permute-start) | collective-permute-done | bytes 65568 | tf_op jit(solution)/shard_map/while/body/eval_jaxpr/ppermute | solution.py:10
  517.6 5.4 all-to-all-start.4
  523.1 17.8 %all-to-all-done.4 = f32[64,1,2048]{2,1,0:T(1,128)S(1)} async-done(((f32[64,1,2048]{2,1,0:T(1,128)}), f32[64,1,2048]{2,1,0:T(1,128)S(1)}, u32[]{:S(2)}, u32[]{:S(2)}) %all-to-all-start.4) | async-done | bytes 524320 | tf_op jit(solution)/shard_map/all_to_all | solution.py:18
  540.9 1.2 reduce.4
  542.5 1.6 copy.33
  544.1 1.6 reshape.269
  (144 shorter events, 44.6 us)
Async XLA Ops:
  6.5 39.5 %copy-start.1 = (f32[1,64,4096]{2,1,0:T(8,128)S(1)}, f32[1,64,4096]{2,1,0:T(8,128)}, u32[]{:S(2)}) copy-start(f32[1,64,4096]{2,1,0:T(8,128)} %param.8) | copy-start | bytes 3145732
  6.5 48.0 %copy-start.4 = (s32[1,32]{1,0:T(1,128)S(1)}, s32[1,32]{1,0:T(1,128)}, u32[]{:S(2)}) copy-start(s32[1,32]{1,0:T(1,128)} %param.10) | copy-start | bytes 388
  6.5 79.9 %all-gather.3.cloned.1.call-start = ((), (), s32[]{:S(2)}) async-start(), calls=%async_computation.5 | async-start | bytes 9437184 | tf_op jit(solution)/shard_map/all_gather | solution.py:54
  9.2 65.2 %copy-start = (f32[1,32,4096]{2,1,0:T(8,128)S(1)}, f32[1,32,4096]{2,1,0:T(8,128)}, u32[]{:S(2)}) copy-start(f32[1,32,4096]{2,1,0:T(8,128)} %param.9) | copy-start | bytes 1572868
  9.2 31.9 %all-to-all-start.2 = ((f32[64,1,2048]{2,1,0:T(1,128)}), f32[64,1,2048]{2,1,0:T(1,128)S(1)}, u32[]{:S(2)}, u32[]{:S(2)}) async-start(f32[64,1,2048]{2,1,0:T(1,128)} %broadcast_in_dim.100), calls=%async_computation.2 | async-start | bytes 1048576 | tf_op jit(solution)/shard_map/all_to_all | solution.py:18
  23.3 55.0 %copy-start.3 = (f32[2,16,64]{2,1,0:T(8,128)S(1)}, f32[2,16,64]{2,1,0:T(8,128)}, u32[]{:S(2)}) copy-start(f32[2,16,64]{2,1,0:T(8,128)} %param.7) | copy-start | bytes 24580
  48.2 23.5 %all-to-all-start.3 = ((f32[64,1,2048]{2,1,0:T(1,128)}), f32[64,1,2048]{2,1,0:T(1,128)S(1)}, u32[]{:S(2)}, u32[]{:S(2)}) async-start(f32[64,1,2048]{2,1,0:T(1,128)} %broadcast_in_dim.102), calls=%async_computation.3 | async-start | bytes 1048576 | tf_op jit(solution)/shard_map/all_to_all | solution.py:18
  75.8 10.7 %collective-permute-start.1 = (f32[32,512]{0,1:T(8,128)S(1)}, f32[32,512]{0,1:T(8,128)S(1)}, u32[]{:S(2)}, u32[]{:S(2)}) collective-permute-start(f32[32,512]{0,1:T(8,128)S(1)} %scatter_custom_fusion.1), channel_id=1, source_target_pairs={{0,64},{64,128},{128,192},{192,256},{256,320},{320,384},{384,448},... | collective-permute-start | bytes 196616 | tf_op jit(solution)/shard_map/ppermute | solution.py:10
  124.0 21.5 %all-to-all-start.1 = ((f32[8,1,16384]{2,1,0:T(1,128)}), f32[8,1,16384]{2,1,0:T(1,128)S(1)}, u32[]{:S(2)}, u32[]{:S(2)}) async-start(f32[8,1,16384]{2,1,0:T(1,128)} %broadcast_in_dim.129), calls=%async_computation.1 | async-start | bytes 1048576 | tf_op jit(solution)/shard_map/while/body/eval_jaxpr/all_to_all | solution.py:18
  148.6 10.5 %collective-permute-start = (f32[32,512]{0,1:T(8,128)S(1)}, f32[32,512]{0,1:T(8,128)S(1)}, u32[]{:S(2)}, u32[]{:S(2)}) collective-permute-start(f32[32,512]{0,1:T(8,128)S(1)} %scatter_fusion), channel_id=1, source_target_pairs={{0,64},{64,128},{128,192},{192,256},{256,320},{320,384},{384,448},... | collective-permute-start | bytes 196616 | tf_op jit(solution)/shard_map/while/body/eval_jaxpr/ppermute | solution.py:10
  195.4 21.5 %all-to-all-start.1 = ((f32[8,1,16384]{2,1,0:T(1,128)}), f32[8,1,16384]{2,1,0:T(1,128)S(1)}, u32[]{:S(2)}, u32[]{:S(2)}) async-start(f32[8,1,16384]{2,1,0:T(1,128)} %broadcast_in_dim.129), calls=%async_computation.1 | async-start | bytes 1048576 | tf_op jit(solution)/shard_map/while/body/eval_jaxpr/all_to_all | solution.py:18
  220.0 10.5 %collective-permute-start = (f32[32,512]{0,1:T(8,128)S(1)}, f32[32,512]{0,1:T(8,128)S(1)}, u32[]{:S(2)}, u32[]{:S(2)}) collective-permute-start(f32[32,512]{0,1:T(8,128)S(1)} %scatter_fusion), channel_id=1, source_target_pairs={{0,64},{64,128},{128,192},{192,256},{256,320},{320,384},{384,448},... | collective-permute-start | bytes 196616 | tf_op jit(solution)/shard_map/while/body/eval_jaxpr/ppermute | solution.py:10
  266.9 21.5 %all-to-all-start.1 = ((f32[8,1,16384]{2,1,0:T(1,128)}), f32[8,1,16384]{2,1,0:T(1,128)S(1)}, u32[]{:S(2)}, u32[]{:S(2)}) async-start(f32[8,1,16384]{2,1,0:T(1,128)} %broadcast_in_dim.129), calls=%async_computation.1 | async-start | bytes 1048576 | tf_op jit(solution)/shard_map/while/body/eval_jaxpr/all_to_all | solution.py:18
  291.5 10.5 %collective-permute-start = (f32[32,512]{0,1:T(8,128)S(1)}, f32[32,512]{0,1:T(8,128)S(1)}, u32[]{:S(2)}, u32[]{:S(2)}) collective-permute-start(f32[32,512]{0,1:T(8,128)S(1)} %scatter_fusion), channel_id=1, source_target_pairs={{0,64},{64,128},{128,192},{192,256},{256,320},{320,384},{384,448},... | collective-permute-start | bytes 196616 | tf_op jit(solution)/shard_map/while/body/eval_jaxpr/ppermute | solution.py:10
  338.3 21.5 %all-to-all-start.1 = ((f32[8,1,16384]{2,1,0:T(1,128)}), f32[8,1,16384]{2,1,0:T(1,128)S(1)}, u32[]{:S(2)}, u32[]{:S(2)}) async-start(f32[8,1,16384]{2,1,0:T(1,128)} %broadcast_in_dim.129), calls=%async_computation.1 | async-start | bytes 1048576 | tf_op jit(solution)/shard_map/while/body/eval_jaxpr/all_to_all | solution.py:18
  362.9 10.5 %collective-permute-start = (f32[32,512]{0,1:T(8,128)S(1)}, f32[32,512]{0,1:T(8,128)S(1)}, u32[]{:S(2)}, u32[]{:S(2)}) collective-permute-start(f32[32,512]{0,1:T(8,128)S(1)} %scatter_fusion), channel_id=1, source_target_pairs={{0,64},{64,128},{128,192},{192,256},{256,320},{320,384},{384,448},... | collective-permute-start | bytes 196616 | tf_op jit(solution)/shard_map/while/body/eval_jaxpr/ppermute | solution.py:10
  409.8 21.5 %all-to-all-start.1 = ((f32[8,1,16384]{2,1,0:T(1,128)}), f32[8,1,16384]{2,1,0:T(1,128)S(1)}, u32[]{:S(2)}, u32[]{:S(2)}) async-start(f32[8,1,16384]{2,1,0:T(1,128)} %broadcast_in_dim.129), calls=%async_computation.1 | async-start | bytes 1048576 | tf_op jit(solution)/shard_map/while/body/eval_jaxpr/all_to_all | solution.py:18
  434.3 10.5 %collective-permute-start = (f32[32,512]{0,1:T(8,128)S(1)}, f32[32,512]{0,1:T(8,128)S(1)}, u32[]{:S(2)}, u32[]{:S(2)}) collective-permute-start(f32[32,512]{0,1:T(8,128)S(1)} %scatter_fusion), channel_id=1, source_target_pairs={{0,64},{64,128},{128,192},{192,256},{256,320},{320,384},{384,448},... | collective-permute-start | bytes 196616 | tf_op jit(solution)/shard_map/while/body/eval_jaxpr/ppermute | solution.py:10
  481.2 21.5 %all-to-all-start.1 = ((f32[8,1,16384]{2,1,0:T(1,128)}), f32[8,1,16384]{2,1,0:T(1,128)S(1)}, u32[]{:S(2)}, u32[]{:S(2)}) async-start(f32[8,1,16384]{2,1,0:T(1,128)} %broadcast_in_dim.129), calls=%async_computation.1 | async-start | bytes 1048576 | tf_op jit(solution)/shard_map/while/body/eval_jaxpr/all_to_all | solution.py:18
  505.8 10.5 %collective-permute-start = (f32[32,512]{0,1:T(8,128)S(1)}, f32[32,512]{0,1:T(8,128)S(1)}, u32[]{:S(2)}, u32[]{:S(2)}) collective-permute-start(f32[32,512]{0,1:T(8,128)S(1)} %scatter_fusion), channel_id=1, source_target_pairs={{0,64},{64,128},{128,192},{192,256},{256,320},{320,384},{384,448},... | collective-permute-start | bytes 196616 | tf_op jit(solution)/shard_map/while/body/eval_jaxpr/ppermute | solution.py:10
  516.3 29.4 %copy-start.2 = (f32[1,64,4096]{2,1,0:T(8,128)S(1)}, f32[1,64,4096]{2,1,0:T(8,128)}, u32[]{:S(2)}) copy-start(f32[1,64,4096]{2,1,0:T(8,128)} %param.8) | copy-start | bytes 3145732
  517.6 23.2 %all-to-all-start.4 = ((f32[64,1,2048]{2,1,0:T(1,128)}), f32[64,1,2048]{2,1,0:T(1,128)S(1)}, u32[]{:S(2)}, u32[]{:S(2)}) async-start(f32[64,1,2048]{2,1,0:T(1,128)} %broadcast_in_dim.106), calls=%async_computation.4 | async-start | bytes 1048576 | tf_op jit(solution)/shard_map/all_to_all | solution.py:18
Sparse Core Ops, SparseCore 0:
  9.5 68.2 all-gather.2

commit v6 on v4

--- a/solution.py
+++ b/solution.py
@@ -14,7 +14,8 @@
     parts = 1
     for axis in axes:
         parts *= lax.axis_size(axis)
-    copies = jnp.broadcast_to(block.reshape(1, block.size), (parts, block.size))
+    tile = (8, block.size // 8)
+    copies = jnp.broadcast_to(block.reshape((1,) + tile), (parts,) + tile)
     pieces = lax.all_to_all(copies, axes, 0, 0, tiled=True).reshape((parts,) + block.shape)
     return jnp.transpose(pieces, (1, 0, 2)).reshape(block.shape[0], parts * block.shape[1])
 

time: 530 us -> 504 us (0.951)
  other arithmetic: 29.4 us -> 10.8 us
  local copies, waits for them, and re-layouts: 52.8 us -> 46 us
    all_to_all x15 -> x0, other arithmetic: 18.6 us -> none  [gathered(): lax.all_to_all(copies, axes, 0, 0, tiled=True)]
where the time goes in v6:
time: 504 us; the launch traced here: 502 us
  waiting for transfers between devices  321 us (64%)
  starting transfers between devices  111 us (22%)
  local copies, waits for them, and re-layouts  46 us (9%)
  matrix products  12.1 us (2%)
  other arithmetic  10.8 us (2%)
    all_to_all x15, waiting for transfers between devices, gathered(): lax.all_to_all(copies, axes, 0, 0, tiled=True)  261 us
    all_to_all x15, starting transfers between devices, gathered(): lax.all_to_all(copies, axes, 0, 0, tiled=True)  97.1 us
    ppermute x7, waiting for transfers between devices, passed_along(): return lax.ppermute(block, axis, route)  60.1 us
    ppermute x7, starting transfers between devices, passed_along(): return lax.ppermute(block, axis, route)  13.8 us
    broadcast_in_dim x30, local copies, waits for them, and re-layouts, gathered(): copies = jnp.broadcast_to(block.reshape((1,) + tile), (parts,) + tile)  13.6 us
    while x35, local copies, waits for them, and re-layouts  10.9 us
  transfers between devices with their start and end apart: 22, of which 22 were waited for; matrix products, arithmetic and copies ran while one was open for 1% of the time, Pallas kernels for 0%

profile of v6, /device:TPU:33, one launch (start us, length us, event | category | flops | bytes accessed | tf_op | source)
XLA Modules:
  0.0 501.7 jit_solution(3132503752413654730)
XLA Ops:
  1.5 471.0 %while.16 = (s32[]{:T(128)}, f32[32,512]{0,1:T(8,128)S(1)}, f32[32,64]{1,0:T(8,128)S(1)}, s32[32]{0:T(128)S(1)}, f32[32,64]{0,1:T(8,128)S(1)}, /*index=5*/f32[64...) while((s32[]{:T(128)}, f32[32,512]{0,1:T(8,128)S(1)}, ...), condition=%wide.region_2.3_spmd.clone, body=%wide.region_0.2_spmd.clone.sunk | while | flops 151003264 | bytes 19931944 | solution.py:65
  2.5 14.0 %all-to-all-start = ((f32[64,8,256]{2,1,0:T(8,128)}), f32[64,8,256]{2,1,0:T(8,128)S(1)}, u32[]{:S(2)}, u32[]{:S(2)}) async-start(f32[64,8,256]{2,1,0:T(8,128)} %broadcast_in_dim.98), calls=%async_computation | async-start | bytes 1048576 | tf_op jit(solution)/shard_map/while/body/eval_jaxpr/all_to_all | solution.py:19
  16.5 17.7 %all-to-all-done = f32[64,8,256]{2,1,0:T(8,128)S(1)} async-done(((f32[64,8,256]{2,1,0:T(8,128)}), f32[64,8,256]{2,1,0:T(8,128)S(1)}, u32[]{:S(2)}, u32[]{:S(2)}) %all-to-all-start) | async-done | bytes 524320 | tf_op jit(solution)/shard_map/while/body/eval_jaxpr/all_to_all | solution.py:19
  36.3 1.0 select_select_fusion.2
  38.1 5.7 %all-to-all-start.1 = ((f32[64,8,256]{2,1,0:T(8,128)}), f32[64,8,256]{2,1,0:T(8,128)S(1)}, u32[]{:S(2)}, u32[]{:S(2)}) async-start(f32[64,8,256]{2,1,0:T(8,128)} %broadcast_in_dim.100), calls=%async_computation.1 | async-start | bytes 1048576 | tf_op jit(solution)/shard_map/while/body/eval_jaxpr/all_to_all | solution.py:19
  44.5 17.0 %all-to-all-done.1 = f32[64,8,256]{2,1,0:T(8,128)S(1)} async-done(((f32[64,8,256]{2,1,0:T(8,128)}), f32[64,8,256]{2,1,0:T(8,128)S(1)}, u32[]{:S(2)}, u32[]{:S(2)}) %all-to-all-start.1) | async-done | bytes 524320 | tf_op jit(solution)/shard_map/while/body/eval_jaxpr/all_to_all | solution.py:19
  64.0 0.9 scatter_fusion
  64.9 2.3 collective-permute-start
  67.2 8.3 %collective-permute-done = f32[32,512]{0,1:T(8,128)S(1)} collective-permute-done((f32[32,512]{0,1:T(8,128)S(1)}, f32[32,512]{0,1:T(8,128)S(1)}, u32[]{:S(2)}, u32[]{:S(2)}) %collective-permute-start) | collective-permute-done | bytes 65568 | tf_op jit(solution)/shard_map/while/body/eval_jaxpr/ppermute | solution.py:10
  76.5 6.2 %all-to-all-start = ((f32[64,8,256]{2,1,0:T(8,128)}), f32[64,8,256]{2,1,0:T(8,128)S(1)}, u32[]{:S(2)}, u32[]{:S(2)}) async-start(f32[64,8,256]{2,1,0:T(8,128)} %broadcast_in_dim.98), calls=%async_computation | async-start | bytes 1048576 | tf_op jit(solution)/shard_map/while/body/eval_jaxpr/all_to_all | solution.py:19
  82.7 17.7 %all-to-all-done = f32[64,8,256]{2,1,0:T(8,128)S(1)} async-done(((f32[64,8,256]{2,1,0:T(8,128)}), f32[64,8,256]{2,1,0:T(8,128)S(1)}, u32[]{:S(2)}, u32[]{:S(2)}) %all-to-all-start) | async-done | bytes 524320 | tf_op jit(solution)/shard_map/while/body/eval_jaxpr/all_to_all | solution.py:19
  101.6 0.9 copy-done
  102.4 1.0 select_select_fusion.2
  104.3 5.7 %all-to-all-start.1 = ((f32[64,8,256]{2,1,0:T(8,128)}), f32[64,8,256]{2,1,0:T(8,128)S(1)}, u32[]{:S(2)}, u32[]{:S(2)}) async-start(f32[64,8,256]{2,1,0:T(8,128)} %broadcast_in_dim.100), calls=%async_computation.1 | async-start | bytes 1048576 | tf_op jit(solution)/shard_map/while/body/eval_jaxpr/all_to_all | solution.py:19
  110.7 17.0 %all-to-all-done.1 = f32[64,8,256]{2,1,0:T(8,128)S(1)} async-done(((f32[64,8,256]{2,1,0:T(8,128)}), f32[64,8,256]{2,1,0:T(8,128)S(1)}, u32[]{:S(2)}, u32[]{:S(2)}) %all-to-all-start.1) | async-done | bytes 524320 | tf_op jit(solution)/shard_map/while/body/eval_jaxpr/all_to_all | solution.py:19
  130.2 0.9 scatter_fusion
  131.0 1.9 collective-permute-start
  133.0 8.6 %collective-permute-done = f32[32,512]{0,1:T(8,128)S(1)} collective-permute-done((f32[32,512]{0,1:T(8,128)S(1)}, f32[32,512]{0,1:T(8,128)S(1)}, u32[]{:S(2)}, u32[]{:S(2)}) %collective-permute-start) | collective-permute-done | bytes 65568 | tf_op jit(solution)/shard_map/while/body/eval_jaxpr/ppermute | solution.py:10
  142.7 6.2 %all-to-all-start = ((f32[64,8,256]{2,1,0:T(8,128)}), f32[64,8,256]{2,1,0:T(8,128)S(1)}, u32[]{:S(2)}, u32[]{:S(2)}) async-start(f32[64,8,256]{2,1,0:T(8,128)} %broadcast_in_dim.98), calls=%async_computation | async-start | bytes 1048576 | tf_op jit(solution)/shard_map/while/body/eval_jaxpr/all_to_all | solution.py:19
  148.9 17.7 %all-to-all-done = f32[64,8,256]{2,1,0:T(8,128)S(1)} async-done(((f32[64,8,256]{2,1,0:T(8,128)}), f32[64,8,256]{2,1,0:T(8,128)S(1)}, u32[]{:S(2)}, u32[]{:S(2)}) %all-to-all-start) | async-done | bytes 524320 | tf_op jit(solution)/shard_map/while/body/eval_jaxpr/all_to_all | solution.py:19
  168.6 1.0 select_select_fusion.2
  170.5 5.7 %all-to-all-start.1 = ((f32[64,8,256]{2,1,0:T(8,128)}), f32[64,8,256]{2,1,0:T(8,128)S(1)}, u32[]{:S(2)}, u32[]{:S(2)}) async-start(f32[64,8,256]{2,1,0:T(8,128)} %broadcast_in_dim.100), calls=%async_computation.1 | async-start | bytes 1048576 | tf_op jit(solution)/shard_map/while/body/eval_jaxpr/all_to_all | solution.py:19
  176.8 17.0 %all-to-all-done.1 = f32[64,8,256]{2,1,0:T(8,128)S(1)} async-done(((f32[64,8,256]{2,1,0:T(8,128)}), f32[64,8,256]{2,1,0:T(8,128)S(1)}, u32[]{:S(2)}, u32[]{:S(2)}) %all-to-all-start.1) | async-done | bytes 524320 | tf_op jit(solution)/shard_map/while/body/eval_jaxpr/all_to_all | solution.py:19
  196.3 0.9 scatter_fusion
  197.2 1.9 collective-permute-start
  199.1 8.6 %collective-permute-done = f32[32,512]{0,1:T(8,128)S(1)} collective-permute-done((f32[32,512]{0,1:T(8,128)S(1)}, f32[32,512]{0,1:T(8,128)S(1)}, u32[]{:S(2)}, u32[]{:S(2)}) %collective-permute-start) | collective-permute-done | bytes 65568 | tf_op jit(solution)/shard_map/while/body/eval_jaxpr/ppermute | solution.py:10
  208.8 6.2 %all-to-all-start = ((f32[64,8,256]{2,1,0:T(8,128)}), f32[64,8,256]{2,1,0:T(8,128)S(1)}, u32[]{:S(2)}, u32[]{:S(2)}) async-start(f32[64,8,256]{2,1,0:T(8,128)} %broadcast_in_dim.98), calls=%async_computation | async-start | bytes 1048576 | tf_op jit(solution)/shard_map/while/body/eval_jaxpr/all_to_all | solution.py:19
  215.0 17.7 %all-to-all-done = f32[64,8,256]{2,1,0:T(8,128)S(1)} async-done(((f32[64,8,256]{2,1,0:T(8,128)}), f32[64,8,256]{2,1,0:T(8,128)S(1)}, u32[]{:S(2)}, u32[]{:S(2)}) %all-to-all-start) | async-done | bytes 524320 | tf_op jit(solution)/shard_map/while/body/eval_jaxpr/all_to_all | solution.py:19
  234.8 1.0 select_select_fusion.2
  236.6 5.7 %all-to-all-start.1 = ((f32[64,8,256]{2,1,0:T(8,128)}), f32[64,8,256]{2,1,0:T(8,128)S(1)}, u32[]{:S(2)}, u32[]{:S(2)}) async-start(f32[64,8,256]{2,1,0:T(8,128)} %broadcast_in_dim.100), calls=%async_computation.1 | async-start | bytes 1048576 | tf_op jit(solution)/shard_map/while/body/eval_jaxpr/all_to_all | solution.py:19
  243.0 17.0 %all-to-all-done.1 = f32[64,8,256]{2,1,0:T(8,128)S(1)} async-done(((f32[64,8,256]{2,1,0:T(8,128)}), f32[64,8,256]{2,1,0:T(8,128)S(1)}, u32[]{:S(2)}, u32[]{:S(2)}) %all-to-all-start.1) | async-done | bytes 524320 | tf_op jit(solution)/shard_map/while/body/eval_jaxpr/all_to_all | solution.py:19
  262.5 0.9 scatter_fusion
  263.4 1.9 collective-permute-start
  265.3 8.6 %collective-permute-done = f32[32,512]{0,1:T(8,128)S(1)} collective-permute-done((f32[32,512]{0,1:T(8,128)S(1)}, f32[32,512]{0,1:T(8,128)S(1)}, u32[]{:S(2)}, u32[]{:S(2)}) %collective-permute-start) | collective-permute-done | bytes 65568 | tf_op jit(solution)/shard_map/while/body/eval_jaxpr/ppermute | solution.py:10
  275.0 6.2 %all-to-all-start = ((f32[64,8,256]{2,1,0:T(8,128)}), f32[64,8,256]{2,1,0:T(8,128)S(1)}, u32[]{:S(2)}, u32[]{:S(2)}) async-start(f32[64,8,256]{2,1,0:T(8,128)} %broadcast_in_dim.98), calls=%async_computation | async-start | bytes 1048576 | tf_op jit(solution)/shard_map/while/body/eval_jaxpr/all_to_all | solution.py:19
  281.2 17.7 %all-to-all-done = f32[64,8,256]{2,1,0:T(8,128)S(1)} async-done(((f32[64,8,256]{2,1,0:T(8,128)}), f32[64,8,256]{2,1,0:T(8,128)S(1)}, u32[]{:S(2)}, u32[]{:S(2)}) %all-to-all-start) | async-done | bytes 524320 | tf_op jit(solution)/shard_map/while/body/eval_jaxpr/all_to_all | solution.py:19
  300.1 0.9 copy-done
  300.9 1.0 select_select_fusion.2
  302.8 5.7 %all-to-all-start.1 = ((f32[64,8,256]{2,1,0:T(8,128)}), f32[64,8,256]{2,1,0:T(8,128)S(1)}, u32[]{:S(2)}, u32[]{:S(2)}) async-start(f32[64,8,256]{2,1,0:T(8,128)} %broadcast_in_dim.100), calls=%async_computation.1 | async-start | bytes 1048576 | tf_op jit(solution)/shard_map/while/body/eval_jaxpr/all_to_all | solution.py:19
  309.2 17.0 %all-to-all-done.1 = f32[64,8,256]{2,1,0:T(8,128)S(1)} async-done(((f32[64,8,256]{2,1,0:T(8,128)}), f32[64,8,256]{2,1,0:T(8,128)S(1)}, u32[]{:S(2)}, u32[]{:S(2)}) %all-to-all-start.1) | async-done | bytes 524320 | tf_op jit(solution)/shard_map/while/body/eval_jaxpr/all_to_all | solution.py:19
  328.7 0.9 scatter_fusion
  329.5 1.9 collective-permute-start
  331.5 8.6 %collective-permute-done = f32[32,512]{0,1:T(8,128)S(1)} collective-permute-done((f32[32,512]{0,1:T(8,128)S(1)}, f32[32,512]{0,1:T(8,128)S(1)}, u32[]{:S(2)}, u32[]{:S(2)}) %collective-permute-start) | collective-permute-done | bytes 65568 | tf_op jit(solution)/shard_map/while/body/eval_jaxpr/ppermute | solution.py:10
  341.2 6.2 %all-to-all-start = ((f32[64,8,256]{2,1,0:T(8,128)}), f32[64,8,256]{2,1,0:T(8,128)S(1)}, u32[]{:S(2)}, u32[]{:S(2)}) async-start(f32[64,8,256]{2,1,0:T(8,128)} %broadcast_in_dim.98), calls=%async_computation | async-start | bytes 1048576 | tf_op jit(solution)/shard_map/while/body/eval_jaxpr/all_to_all | solution.py:19
  347.4 17.7 %all-to-all-done = f32[64,8,256]{2,1,0:T(8,128)S(1)} async-done(((f32[64,8,256]{2,1,0:T(8,128)}), f32[64,8,256]{2,1,0:T(8,128)S(1)}, u32[]{:S(2)}, u32[]{:S(2)}) %all-to-all-start) | async-done | bytes 524320 | tf_op jit(solution)/shard_map/while/body/eval_jaxpr/all_to_all | solution.py:19
  366.2 0.9 copy-done
  367.1 1.0 select_select_fusion.2
  368.9 5.7 %all-to-all-start.1 = ((f32[64,8,256]{2,1,0:T(8,128)}), f32[64,8,256]{2,1,0:T(8,128)S(1)}, u32[]{:S(2)}, u32[]{:S(2)}) async-start(f32[64,8,256]{2,1,0:T(8,128)} %broadcast_in_dim.100), calls=%async_computation.1 | async-start | bytes 1048576 | tf_op jit(solution)/shard_map/while/body/eval_jaxpr/all_to_all | solution.py:19
  375.3 17.0 %all-to-all-done.1 = f32[64,8,256]{2,1,0:T(8,128)S(1)} async-done(((f32[64,8,256]{2,1,0:T(8,128)}), f32[64,8,256]{2,1,0:T(8,128)S(1)}, u32[]{:S(2)}, u32[]{:S(2)}) %all-to-all-start.1) | async-done | bytes 524320 | tf_op jit(solution)/shard_map/while/body/eval_jaxpr/all_to_all | solution.py:19
  394.8 0.9 scatter_fusion
  395.7 1.9 collective-permute-start
  397.6 8.6 %collective-permute-done = f32[32,512]{0,1:T(8,128)S(1)} collective-permute-done((f32[32,512]{0,1:T(8,128)S(1)}, f32[32,512]{0,1:T(8,128)S(1)}, u32[]{:S(2)}, u32[]{:S(2)}) %collective-permute-start) | collective-permute-done | bytes 65568 | tf_op jit(solution)/shard_map/while/body/eval_jaxpr/ppermute | solution.py:10
  407.3 6.2 %all-to-all-start = ((f32[64,8,256]{2,1,0:T(8,128)}), f32[64,8,256]{2,1,0:T(8,128)S(1)}, u32[]{:S(2)}, u32[]{:S(2)}) async-start(f32[64,8,256]{2,1,0:T(8,128)} %broadcast_in_dim.98), calls=%async_computation | async-start | bytes 1048576 | tf_op jit(solution)/shard_map/while/body/eval_jaxpr/all_to_all | solution.py:19
  413.5 17.7 %all-to-all-done = f32[64,8,256]{2,1,0:T(8,128)S(1)} async-done(((f32[64,8,256]{2,1,0:T(8,128)}), f32[64,8,256]{2,1,0:T(8,128)S(1)}, u32[]{:S(2)}, u32[]{:S(2)}) %all-to-all-start) | async-done | bytes 524320 | tf_op jit(solution)/shard_map/while/body/eval_jaxpr/all_to_all | solution.py:19
  432.4 0.9 copy-done
  433.3 1.0 select_select_fusion.2
  435.1 5.7 %all-to-all-start.1 = ((f32[64,8,256]{2,1,0:T(8,128)}), f32[64,8,256]{2,1,0:T(8,128)S(1)}, u32[]{:S(2)}, u32[]{:S(2)}) async-start(f32[64,8,256]{2,1,0:T(8,128)} %broadcast_in_dim.100), calls=%async_computation.1 | async-start | bytes 1048576 | tf_op jit(solution)/shard_map/while/body/eval_jaxpr/all_to_all | solution.py:19
  441.5 17.0 %all-to-all-done.1 = f32[64,8,256]{2,1,0:T(8,128)S(1)} async-done(((f32[64,8,256]{2,1,0:T(8,128)}), f32[64,8,256]{2,1,0:T(8,128)S(1)}, u32[]{:S(2)}, u32[]{:S(2)}) %all-to-all-start.1) | async-done | bytes 524320 | tf_op jit(solution)/shard_map/while/body/eval_jaxpr/all_to_all | solution.py:19
  461.0 0.9 scatter_fusion
  461.9 1.9 collective-permute-start
  463.8 8.6 %collective-permute-done = f32[32,512]{0,1:T(8,128)S(1)} collective-permute-done((f32[32,512]{0,1:T(8,128)S(1)}, f32[32,512]{0,1:T(8,128)S(1)}, u32[]{:S(2)}, u32[]{:S(2)}) %collective-permute-start) | collective-permute-done | bytes 65568 | tf_op jit(solution)/shard_map/while/body/eval_jaxpr/ppermute | solution.py:10
  474.2 6.2 %all-to-all-start.2 = ((f32[64,8,256]{2,1,0:T(8,128)}), f32[64,8,256]{2,1,0:T(8,128)S(1)}, u32[]{:S(2)}, u32[]{:S(2)}) async-start(f32[64,8,256]{2,1,0:T(8,128)} %broadcast_in_dim.80), calls=%async_computation.2 | async-start | bytes 1048576 | tf_op jit(solution)/shard_map/all_to_all | solution.py:19
  480.4 17.7 %all-to-all-done.2 = f32[64,8,256]{2,1,0:T(8,128)S(1)} async-done(((f32[64,8,256]{2,1,0:T(8,128)}), f32[64,8,256]{2,1,0:T(8,128)S(1)}, u32[]{:S(2)}, u32[]{:S(2)}) %all-to-all-start.2) | async-done | bytes 524320 | tf_op jit(solution)/shard_map/all_to_all | solution.py:19
  500.1 1.6 convolution_select_fusion.1
  (160 shorter events, 51.2 us)
Async XLA Ops:
  0.8 0.7 copy-start.4
  2.5 31.7 %all-to-all-start = ((f32[64,8,256]{2,1,0:T(8,128)}), f32[64,8,256]{2,1,0:T(8,128)S(1)}, u32[]{:S(2)}, u32[]{:S(2)}) async-start(f32[64,8,256]{2,1,0:T(8,128)} %broadcast_in_dim.98), calls=%async_computation | async-start | bytes 1048576 | tf_op jit(solution)/shard_map/while/body/eval_jaxpr/all_to_all | solution.py:19
  35.0 1.2 copy-start
  38.1 23.4 %all-to-all-start.1 = ((f32[64,8,256]{2,1,0:T(8,128)}), f32[64,8,256]{2,1,0:T(8,128)S(1)}, u32[]{:S(2)}, u32[]{:S(2)}) async-start(f32[64,8,256]{2,1,0:T(8,128)} %broadcast_in_dim.100), calls=%async_computation.1 | async-start | bytes 1048576 | tf_op jit(solution)/shard_map/while/body/eval_jaxpr/all_to_all | solution.py:19
  62.3 1.0 copy-start.2
  64.9 10.6 %collective-permute-start = (f32[32,512]{0,1:T(8,128)S(1)}, f32[32,512]{0,1:T(8,128)S(1)}, u32[]{:S(2)}, u32[]{:S(2)}) collective-permute-start(f32[32,512]{0,1:T(8,128)S(1)} %scatter_fusion), channel_id=1, source_target_pairs={{0,64},{64,128},{128,192},{192,256},{256,320},{320,384},{384,448},... | collective-permute-start | bytes 196616 | tf_op jit(solution)/shard_map/while/body/eval_jaxpr/ppermute | solution.py:10
  76.5 23.9 %all-to-all-start = ((f32[64,8,256]{2,1,0:T(8,128)}), f32[64,8,256]{2,1,0:T(8,128)S(1)}, u32[]{:S(2)}, u32[]{:S(2)}) async-start(f32[64,8,256]{2,1,0:T(8,128)} %broadcast_in_dim.98), calls=%async_computation | async-start | bytes 1048576 | tf_op jit(solution)/shard_map/while/body/eval_jaxpr/all_to_all | solution.py:19
  101.2 1.2 copy-start
  104.3 23.4 %all-to-all-start.1 = ((f32[64,8,256]{2,1,0:T(8,128)}), f32[64,8,256]{2,1,0:T(8,128)S(1)}, u32[]{:S(2)}, u32[]{:S(2)}) async-start(f32[64,8,256]{2,1,0:T(8,128)} %broadcast_in_dim.100), calls=%async_computation.1 | async-start | bytes 1048576 | tf_op jit(solution)/shard_map/while/body/eval_jaxpr/all_to_all | solution.py:19
  128.5 1.0 copy-start.2
  131.0 10.6 %collective-permute-start = (f32[32,512]{0,1:T(8,128)S(1)}, f32[32,512]{0,1:T(8,128)S(1)}, u32[]{:S(2)}, u32[]{:S(2)}) collective-permute-start(f32[32,512]{0,1:T(8,128)S(1)} %scatter_fusion), channel_id=1, source_target_pairs={{0,64},{64,128},{128,192},{192,256},{256,320},{320,384},{384,448},... | collective-permute-start | bytes 196616 | tf_op jit(solution)/shard_map/while/body/eval_jaxpr/ppermute | solution.py:10
  142.7 23.9 %all-to-all-start = ((f32[64,8,256]{2,1,0:T(8,128)}), f32[64,8,256]{2,1,0:T(8,128)S(1)}, u32[]{:S(2)}, u32[]{:S(2)}) async-start(f32[64,8,256]{2,1,0:T(8,128)} %broadcast_in_dim.98), calls=%async_computation | async-start | bytes 1048576 | tf_op jit(solution)/shard_map/while/body/eval_jaxpr/all_to_all | solution.py:19
  167.4 1.2 copy-start
  170.5 23.4 %all-to-all-start.1 = ((f32[64,8,256]{2,1,0:T(8,128)}), f32[64,8,256]{2,1,0:T(8,128)S(1)}, u32[]{:S(2)}, u32[]{:S(2)}) async-start(f32[64,8,256]{2,1,0:T(8,128)} %broadcast_in_dim.100), calls=%async_computation.1 | async-start | bytes 1048576 | tf_op jit(solution)/shard_map/while/body/eval_jaxpr/all_to_all | solution.py:19
  194.7 1.0 copy-start.2
  197.2 10.6 %collective-permute-start = (f32[32,512]{0,1:T(8,128)S(1)}, f32[32,512]{0,1:T(8,128)S(1)}, u32[]{:S(2)}, u32[]{:S(2)}) collective-permute-start(f32[32,512]{0,1:T(8,128)S(1)} %scatter_fusion), channel_id=1, source_target_pairs={{0,64},{64,128},{128,192},{192,256},{256,320},{320,384},{384,448},... | collective-permute-start | bytes 196616 | tf_op jit(solution)/shard_map/while/body/eval_jaxpr/ppermute | solution.py:10
  208.8 23.9 %all-to-all-start = ((f32[64,8,256]{2,1,0:T(8,128)}), f32[64,8,256]{2,1,0:T(8,128)S(1)}, u32[]{:S(2)}, u32[]{:S(2)}) async-start(f32[64,8,256]{2,1,0:T(8,128)} %broadcast_in_dim.98), calls=%async_computation | async-start | bytes 1048576 | tf_op jit(solution)/shard_map/while/body/eval_jaxpr/all_to_all | solution.py:19
  233.5 1.2 copy-start
  236.6 23.4 %all-to-all-start.1 = ((f32[64,8,256]{2,1,0:T(8,128)}), f32[64,8,256]{2,1,0:T(8,128)S(1)}, u32[]{:S(2)}, u32[]{:S(2)}) async-start(f32[64,8,256]{2,1,0:T(8,128)} %broadcast_in_dim.100), calls=%async_computation.1 | async-start | bytes 1048576 | tf_op jit(solution)/shard_map/while/body/eval_jaxpr/all_to_all | solution.py:19
  260.8 1.0 copy-start.2
  263.4 10.6 %collective-permute-start = (f32[32,512]{0,1:T(8,128)S(1)}, f32[32,512]{0,1:T(8,128)S(1)}, u32[]{:S(2)}, u32[]{:S(2)}) collective-permute-start(f32[32,512]{0,1:T(8,128)S(1)} %scatter_fusion), channel_id=1, source_target_pairs={{0,64},{64,128},{128,192},{192,256},{256,320},{320,384},{384,448},... | collective-permute-start | bytes 196616 | tf_op jit(solution)/shard_map/while/body/eval_jaxpr/ppermute | solution.py:10
  275.0 23.9 %all-to-all-start = ((f32[64,8,256]{2,1,0:T(8,128)}), f32[64,8,256]{2,1,0:T(8,128)S(1)}, u32[]{:S(2)}, u32[]{:S(2)}) async-start(f32[64,8,256]{2,1,0:T(8,128)} %broadcast_in_dim.98), calls=%async_computation | async-start | bytes 1048576 | tf_op jit(solution)/shard_map/while/body/eval_jaxpr/all_to_all | solution.py:19
  299.7 1.2 copy-start
  302.8 23.4 %all-to-all-start.1 = ((f32[64,8,256]{2,1,0:T(8,128)}), f32[64,8,256]{2,1,0:T(8,128)S(1)}, u32[]{:S(2)}, u32[]{:S(2)}) async-start(f32[64,8,256]{2,1,0:T(8,128)} %broadcast_in_dim.100), calls=%async_computation.1 | async-start | bytes 1048576 | tf_op jit(solution)/shard_map/while/body/eval_jaxpr/all_to_all | solution.py:19
  327.0 1.0 copy-start.2
  329.5 10.6 %collective-permute-start = (f32[32,512]{0,1:T(8,128)S(1)}, f32[32,512]{0,1:T(8,128)S(1)}, u32[]{:S(2)}, u32[]{:S(2)}) collective-permute-start(f32[32,512]{0,1:T(8,128)S(1)} %scatter_fusion), channel_id=1, source_target_pairs={{0,64},{64,128},{128,192},{192,256},{256,320},{320,384},{384,448},... | collective-permute-start | bytes 196616 | tf_op jit(solution)/shard_map/while/body/eval_jaxpr/ppermute | solution.py:10
  341.2 23.9 %all-to-all-start = ((f32[64,8,256]{2,1,0:T(8,128)}), f32[64,8,256]{2,1,0:T(8,128)S(1)}, u32[]{:S(2)}, u32[]{:S(2)}) async-start(f32[64,8,256]{2,1,0:T(8,128)} %broadcast_in_dim.98), calls=%async_computation | async-start | bytes 1048576 | tf_op jit(solution)/shard_map/while/body/eval_jaxpr/all_to_all | solution.py:19
  365.9 1.2 copy-start
  368.9 23.4 %all-to-all-start.1 = ((f32[64,8,256]{2,1,0:T(8,128)}), f32[64,8,256]{2,1,0:T(8,128)S(1)}, u32[]{:S(2)}, u32[]{:S(2)}) async-start(f32[64,8,256]{2,1,0:T(8,128)} %broadcast_in_dim.100), calls=%async_computation.1 | async-start | bytes 1048576 | tf_op jit(solution)/shard_map/while/body/eval_jaxpr/all_to_all | solution.py:19
  393.2 1.0 copy-start.2
  395.7 10.6 %collective-permute-start = (f32[32,512]{0,1:T(8,128)S(1)}, f32[32,512]{0,1:T(8,128)S(1)}, u32[]{:S(2)}, u32[]{:S(2)}) collective-permute-start(f32[32,512]{0,1:T(8,128)S(1)} %scatter_fusion), channel_id=1, source_target_pairs={{0,64},{64,128},{128,192},{192,256},{256,320},{320,384},{384,448},... | collective-permute-start | bytes 196616 | tf_op jit(solution)/shard_map/while/body/eval_jaxpr/ppermute | solution.py:10
  407.3 23.9 %all-to-all-start = ((f32[64,8,256]{2,1,0:T(8,128)}), f32[64,8,256]{2,1,0:T(8,128)S(1)}, u32[]{:S(2)}, u32[]{:S(2)}) async-start(f32[64,8,256]{2,1,0:T(8,128)} %broadcast_in_dim.98), calls=%async_computation | async-start | bytes 1048576 | tf_op jit(solution)/shard_map/while/body/eval_jaxpr/all_to_all | solution.py:19
  432.0 1.2 copy-start
  435.1 23.4 %all-to-all-start.1 = ((f32[64,8,256]{2,1,0:T(8,128)}), f32[64,8,256]{2,1,0:T(8,128)S(1)}, u32[]{:S(2)}, u32[]{:S(2)}) async-start(f32[64,8,256]{2,1,0:T(8,128)} %broadcast_in_dim.100), calls=%async_computation.1 | async-start | bytes 1048576 | tf_op jit(solution)/shard_map/while/body/eval_jaxpr/all_to_all | solution.py:19
  459.3 1.0 copy-start.2
  461.9 10.6 %collective-permute-start = (f32[32,512]{0,1:T(8,128)S(1)}, f32[32,512]{0,1:T(8,128)S(1)}, u32[]{:S(2)}, u32[]{:S(2)}) collective-permute-start(f32[32,512]{0,1:T(8,128)S(1)} %scatter_fusion), channel_id=1, source_target_pairs={{0,64},{64,128},{128,192},{192,256},{256,320},{320,384},{384,448},... | collective-permute-start | bytes 196616 | tf_op jit(solution)/shard_map/while/body/eval_jaxpr/ppermute | solution.py:10
  472.5 0.7 copy-start.3
  474.2 23.9 %all-to-all-start.2 = ((f32[64,8,256]{2,1,0:T(8,128)}), f32[64,8,256]{2,1,0:T(8,128)S(1)}, u32[]{:S(2)}, u32[]{:S(2)}) async-start(f32[64,8,256]{2,1,0:T(8,128)} %broadcast_in_dim.80), calls=%async_computation.2 | async-start | bytes 1048576 | tf_op jit(solution)/shard_map/all_to_all | solution.py:19
  498.9 1.2 copy-start.1

commit v7 on v6

--- a/solution.py
+++ b/solution.py
@@ -29,7 +29,7 @@
     diag_rows = inverse_diag[0]
     lower_rows = lower_blocks[0]
     lower_count = lower_rows.shape[0]
-    live = jnp.arange(lower_count, dtype=jnp.int32) < counts[0, 0]
+    live = lax.optimization_barrier(jnp.arange(lower_count, dtype=jnp.int32)[None, :] < counts[0, 0])
     places = targets[0] // width * own_rows + targets[0] % own_rows
 
     def solve_piece(segment):
@@ -56,7 +56,7 @@
         solved = solve_piece(gathered(resid, ("row", "col")))
         solution = jnp.where(own_level == level, solved, solution)
         update = lower_piece(gathered(solved, ("row", "col")))
-        update = jnp.where(live[None, :], update, jnp.float32(0.0))
+        update = jnp.where(live, update, jnp.float32(0.0))
         carried = carried.at[:, places].add(update)
         return passed_along(carried, "sep", 1), solution
 

time: 504 us -> 505 us (level)
  transfers between devices with their start and end apart: 22 -> 22, of which waited for: 22 -> 22; matrix products, arithmetic and copies ran while one was open for 1% -> 0% of each run, Pallas kernels for 0% -> 0%
where the time goes in v7:
time: 505 us; the launch traced here: 502 us
  waiting for transfers between devices  325 us (64%)
  starting transfers between devices  111 us (22%)
  local copies, waits for them, and re-layouts  46 us (9%)
  matrix products  12.1 us (2%)
  other arithmetic  6.26 us (1%)
    all_to_all x15, waiting for transfers between devices, gathered(): lax.all_to_all(copies, axes, 0, 0, tiled=True)  265 us
    all_to_all x15, starting transfers between devices, gathered(): lax.all_to_all(copies, axes, 0, 0, tiled=True)  97.1 us
    ppermute x7, waiting for transfers between devices, passed_along(): return lax.ppermute(block, axis, route)  60.1 us
    ppermute x7, starting transfers between devices, passed_along(): return lax.ppermute(block, axis, route)  13.8 us
    broadcast_in_dim x30, local copies, waits for them, and re-layouts, gathered(): copies = jnp.broadcast_to(block.reshape((1,) + tile), (parts,) + tile)  13.6 us
    while x35, local copies, waits for them, and re-layouts  10.9 us
  transfers between devices with their start and end apart: 22, of which 22 were waited for; matrix products, arithmetic and copies ran while one was open for 0% of the time, Pallas kernels for 0%

profile of v7, /device:TPU:33, one launch (start us, length us, event | category | flops | bytes accessed | tf_op | source)
XLA Modules:
  0.0 502.3 jit_solution(12914950426802687447)
XLA Ops:
  2.2 471.0 %while.16 = (s32[]{:T(128)}, f32[32,512]{0,1:T(8,128)S(1)}, f32[32,64]{1,0:T(8,128)S(1)}, s32[32]{0:T(128)S(1)}, pred[1,32]{1,0:T(4,128)(4,1)S(1)}, /*index=5*/f...) while((s32[]{:T(128)}, f32[32,512]{0,1:T(8,128)S(1)}, ...), condition=%wide.region_2.3_spmd.clone, body=%wide.region_0.2_spmd.clone.sunk | while | flops 151003232 | bytes 19931908 | solution.py:65
  3.2 14.0 %all-to-all-start = ((f32[64,8,256]{2,1,0:T(8,128)}), f32[64,8,256]{2,1,0:T(8,128)S(1)}, u32[]{:S(2)}, u32[]{:S(2)}) async-start(f32[64,8,256]{2,1,0:T(8,128)} %broadcast_in_dim.101), calls=%async_computation | async-start | bytes 1048576 | tf_op jit(solution)/shard_map/while/body/eval_jaxpr/all_to_all | solution.py:19
  17.2 17.7 %all-to-all-done = f32[64,8,256]{2,1,0:T(8,128)S(1)} async-done(((f32[64,8,256]{2,1,0:T(8,128)}), f32[64,8,256]{2,1,0:T(8,128)S(1)}, u32[]{:S(2)}, u32[]{:S(2)}) %all-to-all-start) | async-done | bytes 524320 | tf_op jit(solution)/shard_map/while/body/eval_jaxpr/all_to_all | solution.py:19
  36.1 0.9 copy-done
  36.9 1.0 select_select_fusion.2
  38.8 5.7 %all-to-all-start.1 = ((f32[64,8,256]{2,1,0:T(8,128)}), f32[64,8,256]{2,1,0:T(8,128)S(1)}, u32[]{:S(2)}, u32[]{:S(2)}) async-start(f32[64,8,256]{2,1,0:T(8,128)} %broadcast_in_dim.103), calls=%async_computation.1 | async-start | bytes 1048576 | tf_op jit(solution)/shard_map/while/body/eval_jaxpr/all_to_all | solution.py:19
  44.5 17.7 %all-to-all-done.1 = f32[64,8,256]{2,1,0:T(8,128)S(1)} async-done(((f32[64,8,256]{2,1,0:T(8,128)}), f32[64,8,256]{2,1,0:T(8,128)S(1)}, u32[]{:S(2)}, u32[]{:S(2)}) %all-to-all-start.1) | async-done | bytes 524320 | tf_op jit(solution)/shard_map/while/body/eval_jaxpr/all_to_all | solution.py:19
  64.7 0.9 scatter_fusion
  65.5 2.3 collective-permute-start
  67.9 8.3 %collective-permute-done = f32[32,512]{0,1:T(8,128)S(1)} collective-permute-done((f32[32,512]{0,1:T(8,128)S(1)}, f32[32,512]{0,1:T(8,128)S(1)}, u32[]{:S(2)}, u32[]{:S(2)}) %collective-permute-start) | collective-permute-done | bytes 65568 | tf_op jit(solution)/shard_map/while/body/eval_jaxpr/ppermute | solution.py:10
  77.2 6.2 %all-to-all-start = ((f32[64,8,256]{2,1,0:T(8,128)}), f32[64,8,256]{2,1,0:T(8,128)S(1)}, u32[]{:S(2)}, u32[]{:S(2)}) async-start(f32[64,8,256]{2,1,0:T(8,128)} %broadcast_in_dim.101), calls=%async_computation | async-start | bytes 1048576 | tf_op jit(solution)/shard_map/while/body/eval_jaxpr/all_to_all | solution.py:19
  83.4 17.7 %all-to-all-done = f32[64,8,256]{2,1,0:T(8,128)S(1)} async-done(((f32[64,8,256]{2,1,0:T(8,128)}), f32[64,8,256]{2,1,0:T(8,128)S(1)}, u32[]{:S(2)}, u32[]{:S(2)}) %all-to-all-start) | async-done | bytes 524320 | tf_op jit(solution)/shard_map/while/body/eval_jaxpr/all_to_all | solution.py:19
  102.2 0.9 copy-done
  103.1 1.0 select_select_fusion.2
  105.0 5.7 %all-to-all-start.1 = ((f32[64,8,256]{2,1,0:T(8,128)}), f32[64,8,256]{2,1,0:T(8,128)S(1)}, u32[]{:S(2)}, u32[]{:S(2)}) async-start(f32[64,8,256]{2,1,0:T(8,128)} %broadcast_in_dim.103), calls=%async_computation.1 | async-start | bytes 1048576 | tf_op jit(solution)/shard_map/while/body/eval_jaxpr/all_to_all | solution.py:19
  110.7 17.7 %all-to-all-done.1 = f32[64,8,256]{2,1,0:T(8,128)S(1)} async-done(((f32[64,8,256]{2,1,0:T(8,128)}), f32[64,8,256]{2,1,0:T(8,128)S(1)}, u32[]{:S(2)}, u32[]{:S(2)}) %all-to-all-start.1) | async-done | bytes 524320 | tf_op jit(solution)/shard_map/while/body/eval_jaxpr/all_to_all | solution.py:19
  130.8 0.9 scatter_fusion
  131.7 1.9 collective-permute-start
  133.6 8.6 %collective-permute-done = f32[32,512]{0,1:T(8,128)S(1)} collective-permute-done((f32[32,512]{0,1:T(8,128)S(1)}, f32[32,512]{0,1:T(8,128)S(1)}, u32[]{:S(2)}, u32[]{:S(2)}) %collective-permute-start) | collective-permute-done | bytes 65568 | tf_op jit(solution)/shard_map/while/body/eval_jaxpr/ppermute | solution.py:10
  143.3 6.2 %all-to-all-start = ((f32[64,8,256]{2,1,0:T(8,128)}), f32[64,8,256]{2,1,0:T(8,128)S(1)}, u32[]{:S(2)}, u32[]{:S(2)}) async-start(f32[64,8,256]{2,1,0:T(8,128)} %broadcast_in_dim.101), calls=%async_computation | async-start | bytes 1048576 | tf_op jit(solution)/shard_map/while/body/eval_jaxpr/all_to_all | solution.py:19
  149.5 17.7 %all-to-all-done = f32[64,8,256]{2,1,0:T(8,128)S(1)} async-done(((f32[64,8,256]{2,1,0:T(8,128)}), f32[64,8,256]{2,1,0:T(8,128)S(1)}, u32[]{:S(2)}, u32[]{:S(2)}) %all-to-all-start) | async-done | bytes 524320 | tf_op jit(solution)/shard_map/while/body/eval_jaxpr/all_to_all | solution.py:19
  168.4 0.9 copy-done
  169.3 1.0 select_select_fusion.2
  171.1 5.7 %all-to-all-start.1 = ((f32[64,8,256]{2,1,0:T(8,128)}), f32[64,8,256]{2,1,0:T(8,128)S(1)}, u32[]{:S(2)}, u32[]{:S(2)}) async-start(f32[64,8,256]{2,1,0:T(8,128)} %broadcast_in_dim.103), calls=%async_computation.1 | async-start | bytes 1048576 | tf_op jit(solution)/shard_map/while/body/eval_jaxpr/all_to_all | solution.py:19
  176.8 17.7 %all-to-all-done.1 = f32[64,8,256]{2,1,0:T(8,128)S(1)} async-done(((f32[64,8,256]{2,1,0:T(8,128)}), f32[64,8,256]{2,1,0:T(8,128)S(1)}, u32[]{:S(2)}, u32[]{:S(2)}) %all-to-all-start.1) | async-done | bytes 524320 | tf_op jit(solution)/shard_map/while/body/eval_jaxpr/all_to_all | solution.py:19
  197.0 0.9 scatter_fusion
  197.9 1.9 collective-permute-start
  199.8 8.6 %collective-permute-done = f32[32,512]{0,1:T(8,128)S(1)} collective-permute-done((f32[32,512]{0,1:T(8,128)S(1)}, f32[32,512]{0,1:T(8,128)S(1)}, u32[]{:S(2)}, u32[]{:S(2)}) %collective-permute-start) | collective-permute-done | bytes 65568 | tf_op jit(solution)/shard_map/while/body/eval_jaxpr/ppermute | solution.py:10
  209.5 6.2 %all-to-all-start = ((f32[64,8,256]{2,1,0:T(8,128)}), f32[64,8,256]{2,1,0:T(8,128)S(1)}, u32[]{:S(2)}, u32[]{:S(2)}) async-start(f32[64,8,256]{2,1,0:T(8,128)} %broadcast_in_dim.101), calls=%async_computation | async-start | bytes 1048576 | tf_op jit(solution)/shard_map/while/body/eval_jaxpr/all_to_all | solution.py:19
  215.7 17.7 %all-to-all-done = f32[64,8,256]{2,1,0:T(8,128)S(1)} async-done(((f32[64,8,256]{2,1,0:T(8,128)}), f32[64,8,256]{2,1,0:T(8,128)S(1)}, u32[]{:S(2)}, u32[]{:S(2)}) %all-to-all-start) | async-done | bytes 524320 | tf_op jit(solution)/shard_map/while/body/eval_jaxpr/all_to_all | solution.py:19
  235.4 1.0 select_select_fusion.2
  237.3 5.7 %all-to-all-start.1 = ((f32[64,8,256]{2,1,0:T(8,128)}), f32[64,8,256]{2,1,0:T(8,128)S(1)}, u32[]{:S(2)}, u32[]{:S(2)}) async-start(f32[64,8,256]{2,1,0:T(8,128)} %broadcast_in_dim.103), calls=%async_computation.1 | async-start | bytes 1048576 | tf_op jit(solution)/shard_map/while/body/eval_jaxpr/all_to_all | solution.py:19
  243.0 17.7 %all-to-all-done.1 = f32[64,8,256]{2,1,0:T(8,128)S(1)} async-done(((f32[64,8,256]{2,1,0:T(8,128)}), f32[64,8,256]{2,1,0:T(8,128)S(1)}, u32[]{:S(2)}, u32[]{:S(2)}) %all-to-all-start.1) | async-done | bytes 524320 | tf_op jit(solution)/shard_map/while/body/eval_jaxpr/all_to_all | solution.py:19
  263.2 0.9 scatter_fusion
  264.0 1.9 collective-permute-start
  266.0 8.6 %collective-permute-done = f32[32,512]{0,1:T(8,128)S(1)} collective-permute-done((f32[32,512]{0,1:T(8,128)S(1)}, f32[32,512]{0,1:T(8,128)S(1)}, u32[]{:S(2)}, u32[]{:S(2)}) %collective-permute-start) | collective-permute-done | bytes 65568 | tf_op jit(solution)/shard_map/while/body/eval_jaxpr/ppermute | solution.py:10
  275.7 6.2 %all-to-all-start = ((f32[64,8,256]{2,1,0:T(8,128)}), f32[64,8,256]{2,1,0:T(8,128)S(1)}, u32[]{:S(2)}, u32[]{:S(2)}) async-start(f32[64,8,256]{2,1,0:T(8,128)} %broadcast_in_dim.101), calls=%async_computation | async-start | bytes 1048576 | tf_op jit(solution)/shard_map/while/body/eval_jaxpr/all_to_all | solution.py:19
  281.9 17.7 %all-to-all-done = f32[64,8,256]{2,1,0:T(8,128)S(1)} async-done(((f32[64,8,256]{2,1,0:T(8,128)}), f32[64,8,256]{2,1,0:T(8,128)S(1)}, u32[]{:S(2)}, u32[]{:S(2)}) %all-to-all-start) | async-done | bytes 524320 | tf_op jit(solution)/shard_map/while/body/eval_jaxpr/all_to_all | solution.py:19
  300.7 0.9 copy-done
  301.6 1.0 select_select_fusion.2
  303.5 5.7 %all-to-all-start.1 = ((f32[64,8,256]{2,1,0:T(8,128)}), f32[64,8,256]{2,1,0:T(8,128)S(1)}, u32[]{:S(2)}, u32[]{:S(2)}) async-start(f32[64,8,256]{2,1,0:T(8,128)} %broadcast_in_dim.103), calls=%async_computation.1 | async-start | bytes 1048576 | tf_op jit(solution)/shard_map/while/body/eval_jaxpr/all_to_all | solution.py:19
  309.2 17.7 %all-to-all-done.1 = f32[64,8,256]{2,1,0:T(8,128)S(1)} async-done(((f32[64,8,256]{2,1,0:T(8,128)}), f32[64,8,256]{2,1,0:T(8,128)S(1)}, u32[]{:S(2)}, u32[]{:S(2)}) %all-to-all-start.1) | async-done | bytes 524320 | tf_op jit(solution)/shard_map/while/body/eval_jaxpr/all_to_all | solution.py:19
  329.3 0.9 scatter_fusion
  330.2 1.9 collective-permute-start
  332.1 8.6 %collective-permute-done = f32[32,512]{0,1:T(8,128)S(1)} collective-permute-done((f32[32,512]{0,1:T(8,128)S(1)}, f32[32,512]{0,1:T(8,128)S(1)}, u32[]{:S(2)}, u32[]{:S(2)}) %collective-permute-start) | collective-permute-done | bytes 65568 | tf_op jit(solution)/shard_map/while/body/eval_jaxpr/ppermute | solution.py:10
  341.8 6.2 %all-to-all-start = ((f32[64,8,256]{2,1,0:T(8,128)}), f32[64,8,256]{2,1,0:T(8,128)S(1)}, u32[]{:S(2)}, u32[]{:S(2)}) async-start(f32[64,8,256]{2,1,0:T(8,128)} %broadcast_in_dim.101), calls=%async_computation | async-start | bytes 1048576 | tf_op jit(solution)/shard_map/while/body/eval_jaxpr/all_to_all | solution.py:19
  348.0 17.7 %all-to-all-done = f32[64,8,256]{2,1,0:T(8,128)S(1)} async-done(((f32[64,8,256]{2,1,0:T(8,128)}), f32[64,8,256]{2,1,0:T(8,128)S(1)}, u32[]{:S(2)}, u32[]{:S(2)}) %all-to-all-start) | async-done | bytes 524320 | tf_op jit(solution)/shard_map/while/body/eval_jaxpr/all_to_all | solution.py:19
  367.8 1.0 select_select_fusion.2
  369.6 5.7 %all-to-all-start.1 = ((f32[64,8,256]{2,1,0:T(8,128)}), f32[64,8,256]{2,1,0:T(8,128)S(1)}, u32[]{:S(2)}, u32[]{:S(2)}) async-start(f32[64,8,256]{2,1,0:T(8,128)} %broadcast_in_dim.103), calls=%async_computation.1 | async-start | bytes 1048576 | tf_op jit(solution)/shard_map/while/body/eval_jaxpr/all_to_all | solution.py:19
  375.3 17.7 %all-to-all-done.1 = f32[64,8,256]{2,1,0:T(8,128)S(1)} async-done(((f32[64,8,256]{2,1,0:T(8,128)}), f32[64,8,256]{2,1,0:T(8,128)S(1)}, u32[]{:S(2)}, u32[]{:S(2)}) %all-to-all-start.1) | async-done | bytes 524320 | tf_op jit(solution)/shard_map/while/body/eval_jaxpr/all_to_all | solution.py:19
  395.5 0.9 scatter_fusion
  396.4 1.9 collective-permute-start
  398.3 8.6 %collective-permute-done = f32[32,512]{0,1:T(8,128)S(1)} collective-permute-done((f32[32,512]{0,1:T(8,128)S(1)}, f32[32,512]{0,1:T(8,128)S(1)}, u32[]{:S(2)}, u32[]{:S(2)}) %collective-permute-start) | collective-permute-done | bytes 65568 | tf_op jit(solution)/shard_map/while/body/eval_jaxpr/ppermute | solution.py:10
  408.0 6.2 %all-to-all-start = ((f32[64,8,256]{2,1,0:T(8,128)}), f32[64,8,256]{2,1,0:T(8,128)S(1)}, u32[]{:S(2)}, u32[]{:S(2)}) async-start(f32[64,8,256]{2,1,0:T(8,128)} %broadcast_in_dim.101), calls=%async_computation | async-start | bytes 1048576 | tf_op jit(solution)/shard_map/while/body/eval_jaxpr/all_to_all | solution.py:19
  414.2 17.7 %all-to-all-done = f32[64,8,256]{2,1,0:T(8,128)S(1)} async-done(((f32[64,8,256]{2,1,0:T(8,128)}), f32[64,8,256]{2,1,0:T(8,128)S(1)}, u32[]{:S(2)}, u32[]{:S(2)}) %all-to-all-start) | async-done | bytes 524320 | tf_op jit(solution)/shard_map/while/body/eval_jaxpr/all_to_all | solution.py:19
  433.9 1.0 select_select_fusion.2
  435.8 5.7 %all-to-all-start.1 = ((f32[64,8,256]{2,1,0:T(8,128)}), f32[64,8,256]{2,1,0:T(8,128)S(1)}, u32[]{:S(2)}, u32[]{:S(2)}) async-start(f32[64,8,256]{2,1,0:T(8,128)} %broadcast_in_dim.103), calls=%async_computation.1 | async-start | bytes 1048576 | tf_op jit(solution)/shard_map/while/body/eval_jaxpr/all_to_all | solution.py:19
  441.5 17.7 %all-to-all-done.1 = f32[64,8,256]{2,1,0:T(8,128)S(1)} async-done(((f32[64,8,256]{2,1,0:T(8,128)}), f32[64,8,256]{2,1,0:T(8,128)S(1)}, u32[]{:S(2)}, u32[]{:S(2)}) %all-to-all-start.1) | async-done | bytes 524320 | tf_op jit(solution)/shard_map/while/body/eval_jaxpr/all_to_all | solution.py:19
  461.7 0.9 scatter_fusion
  462.5 1.9 collective-permute-start
  464.5 8.6 %collective-permute-done = f32[32,512]{0,1:T(8,128)S(1)} collective-permute-done((f32[32,512]{0,1:T(8,128)S(1)}, f32[32,512]{0,1:T(8,128)S(1)}, u32[]{:S(2)}, u32[]{:S(2)}) %collective-permute-start) | collective-permute-done | bytes 65568 | tf_op jit(solution)/shard_map/while/body/eval_jaxpr/ppermute | solution.py:10
  474.8 6.2 %all-to-all-start.2 = ((f32[64,8,256]{2,1,0:T(8,128)}), f32[64,8,256]{2,1,0:T(8,128)S(1)}, u32[]{:S(2)}, u32[]{:S(2)}) async-start(f32[64,8,256]{2,1,0:T(8,128)} %broadcast_in_dim.82), calls=%async_computation.2 | async-start | bytes 1048576 | tf_op jit(solution)/shard_map/all_to_all | solution.py:19
  481.0 17.7 %all-to-all-done.2 = f32[64,8,256]{2,1,0:T(8,128)S(1)} async-done(((f32[64,8,256]{2,1,0:T(8,128)}), f32[64,8,256]{2,1,0:T(8,128)S(1)}, u32[]{:S(2)}, u32[]{:S(2)}) %all-to-all-start.2) | async-done | bytes 524320 | tf_op jit(solution)/shard_map/all_to_all | solution.py:19
  500.8 1.6 convolution_select_fusion.1
  (154 shorter events, 46.6 us)
Async XLA Ops:
  1.5 0.7 copy-start.4
  3.2 31.7 %all-to-all-start = ((f32[64,8,256]{2,1,0:T(8,128)}), f32[64,8,256]{2,1,0:T(8,128)S(1)}, u32[]{:S(2)}, u32[]{:S(2)}) async-start(f32[64,8,256]{2,1,0:T(8,128)} %broadcast_in_dim.101), calls=%async_computation | async-start | bytes 1048576 | tf_op jit(solution)/shard_map/while/body/eval_jaxpr/all_to_all | solution.py:19
  35.7 1.2 copy-start
  38.8 23.4 %all-to-all-start.1 = ((f32[64,8,256]{2,1,0:T(8,128)}), f32[64,8,256]{2,1,0:T(8,128)S(1)}, u32[]{:S(2)}, u32[]{:S(2)}) async-start(f32[64,8,256]{2,1,0:T(8,128)} %broadcast_in_dim.103), calls=%async_computation.1 | async-start | bytes 1048576 | tf_op jit(solution)/shard_map/while/body/eval_jaxpr/all_to_all | solution.py:19
  63.0 1.0 copy-start.2
  65.5 10.6 %collective-permute-start = (f32[32,512]{0,1:T(8,128)S(1)}, f32[32,512]{0,1:T(8,128)S(1)}, u32[]{:S(2)}, u32[]{:S(2)}) collective-permute-start(f32[32,512]{0,1:T(8,128)S(1)} %scatter_fusion), channel_id=1, source_target_pairs={{0,64},{64,128},{128,192},{192,256},{256,320},{320,384},{384,448},... | collective-permute-start | bytes 196616 | tf_op jit(solution)/shard_map/while/body/eval_jaxpr/ppermute | solution.py:10
  77.2 23.9 %all-to-all-start = ((f32[64,8,256]{2,1,0:T(8,128)}), f32[64,8,256]{2,1,0:T(8,128)S(1)}, u32[]{:S(2)}, u32[]{:S(2)}) async-start(f32[64,8,256]{2,1,0:T(8,128)} %broadcast_in_dim.101), calls=%async_computation | async-start | bytes 1048576 | tf_op jit(solution)/shard_map/while/body/eval_jaxpr/all_to_all | solution.py:19
  101.9 1.2 copy-start
  105.0 23.4 %all-to-all-start.1 = ((f32[64,8,256]{2,1,0:T(8,128)}), f32[64,8,256]{2,1,0:T(8,128)S(1)}, u32[]{:S(2)}, u32[]{:S(2)}) async-start(f32[64,8,256]{2,1,0:T(8,128)} %broadcast_in_dim.103), calls=%async_computation.1 | async-start | bytes 1048576 | tf_op jit(solution)/shard_map/while/body/eval_jaxpr/all_to_all | solution.py:19
  129.2 1.0 copy-start.2
  131.7 10.6 %collective-permute-start = (f32[32,512]{0,1:T(8,128)S(1)}, f32[32,512]{0,1:T(8,128)S(1)}, u32[]{:S(2)}, u32[]{:S(2)}) collective-permute-start(f32[32,512]{0,1:T(8,128)S(1)} %scatter_fusion), channel_id=1, source_target_pairs={{0,64},{64,128},{128,192},{192,256},{256,320},{320,384},{384,448},... | collective-permute-start | bytes 196616 | tf_op jit(solution)/shard_map/while/body/eval_jaxpr/ppermute | solution.py:10
  143.3 23.9 %all-to-all-start = ((f32[64,8,256]{2,1,0:T(8,128)}), f32[64,8,256]{2,1,0:T(8,128)S(1)}, u32[]{:S(2)}, u32[]{:S(2)}) async-start(f32[64,8,256]{2,1,0:T(8,128)} %broadcast_in_dim.101), calls=%async_computation | async-start | bytes 1048576 | tf_op jit(solution)/shard_map/while/body/eval_jaxpr/all_to_all | solution.py:19
  168.0 1.2 copy-start
  171.1 23.4 %all-to-all-start.1 = ((f32[64,8,256]{2,1,0:T(8,128)}), f32[64,8,256]{2,1,0:T(8,128)S(1)}, u32[]{:S(2)}, u32[]{:S(2)}) async-start(f32[64,8,256]{2,1,0:T(8,128)} %broadcast_in_dim.103), calls=%async_computation.1 | async-start | bytes 1048576 | tf_op jit(solution)/shard_map/while/body/eval_jaxpr/all_to_all | solution.py:19
  195.3 1.0 copy-start.2
  197.9 10.6 %collective-permute-start = (f32[32,512]{0,1:T(8,128)S(1)}, f32[32,512]{0,1:T(8,128)S(1)}, u32[]{:S(2)}, u32[]{:S(2)}) collective-permute-start(f32[32,512]{0,1:T(8,128)S(1)} %scatter_fusion), channel_id=1, source_target_pairs={{0,64},{64,128},{128,192},{192,256},{256,320},{320,384},{384,448},... | collective-permute-start | bytes 196616 | tf_op jit(solution)/shard_map/while/body/eval_jaxpr/ppermute | solution.py:10
  209.5 23.9 %all-to-all-start = ((f32[64,8,256]{2,1,0:T(8,128)}), f32[64,8,256]{2,1,0:T(8,128)S(1)}, u32[]{:S(2)}, u32[]{:S(2)}) async-start(f32[64,8,256]{2,1,0:T(8,128)} %broadcast_in_dim.101), calls=%async_computation | async-start | bytes 1048576 | tf_op jit(solution)/shard_map/while/body/eval_jaxpr/all_to_all | solution.py:19
  234.2 1.2 copy-start
  237.3 23.4 %all-to-all-start.1 = ((f32[64,8,256]{2,1,0:T(8,128)}), f32[64,8,256]{2,1,0:T(8,128)S(1)}, u32[]{:S(2)}, u32[]{:S(2)}) async-start(f32[64,8,256]{2,1,0:T(8,128)} %broadcast_in_dim.103), calls=%async_computation.1 | async-start | bytes 1048576 | tf_op jit(solution)/shard_map/while/body/eval_jaxpr/all_to_all | solution.py:19
  261.5 1.0 copy-start.2
  264.0 10.6 %collective-permute-start = (f32[32,512]{0,1:T(8,128)S(1)}, f32[32,512]{0,1:T(8,128)S(1)}, u32[]{:S(2)}, u32[]{:S(2)}) collective-permute-start(f32[32,512]{0,1:T(8,128)S(1)} %scatter_fusion), channel_id=1, source_target_pairs={{0,64},{64,128},{128,192},{192,256},{256,320},{320,384},{384,448},... | collective-permute-start | bytes 196616 | tf_op jit(solution)/shard_map/while/body/eval_jaxpr/ppermute | solution.py:10
  275.7 23.9 %all-to-all-start = ((f32[64,8,256]{2,1,0:T(8,128)}), f32[64,8,256]{2,1,0:T(8,128)S(1)}, u32[]{:S(2)}, u32[]{:S(2)}) async-start(f32[64,8,256]{2,1,0:T(8,128)} %broadcast_in_dim.101), calls=%async_computation | async-start | bytes 1048576 | tf_op jit(solution)/shard_map/while/body/eval_jaxpr/all_to_all | solution.py:19
  300.4 1.2 copy-start
  303.5 23.4 %all-to-all-start.1 = ((f32[64,8,256]{2,1,0:T(8,128)}), f32[64,8,256]{2,1,0:T(8,128)S(1)}, u32[]{:S(2)}, u32[]{:S(2)}) async-start(f32[64,8,256]{2,1,0:T(8,128)} %broadcast_in_dim.103), calls=%async_computation.1 | async-start | bytes 1048576 | tf_op jit(solution)/shard_map/while/body/eval_jaxpr/all_to_all | solution.py:19
  327.7 1.0 copy-start.2
  330.2 10.6 %collective-permute-start = (f32[32,512]{0,1:T(8,128)S(1)}, f32[32,512]{0,1:T(8,128)S(1)}, u32[]{:S(2)}, u32[]{:S(2)}) collective-permute-start(f32[32,512]{0,1:T(8,128)S(1)} %scatter_fusion), channel_id=1, source_target_pairs={{0,64},{64,128},{128,192},{192,256},{256,320},{320,384},{384,448},... | collective-permute-start | bytes 196616 | tf_op jit(solution)/shard_map/while/body/eval_jaxpr/ppermute | solution.py:10
  341.8 23.9 %all-to-all-start = ((f32[64,8,256]{2,1,0:T(8,128)}), f32[64,8,256]{2,1,0:T(8,128)S(1)}, u32[]{:S(2)}, u32[]{:S(2)}) async-start(f32[64,8,256]{2,1,0:T(8,128)} %broadcast_in_dim.101), calls=%async_computation | async-start | bytes 1048576 | tf_op jit(solution)/shard_map/while/body/eval_jaxpr/all_to_all | solution.py:19
  366.5 1.2 copy-start
  369.6 23.4 %all-to-all-start.1 = ((f32[64,8,256]{2,1,0:T(8,128)}), f32[64,8,256]{2,1,0:T(8,128)S(1)}, u32[]{:S(2)}, u32[]{:S(2)}) async-start(f32[64,8,256]{2,1,0:T(8,128)} %broadcast_in_dim.103), calls=%async_computation.1 | async-start | bytes 1048576 | tf_op jit(solution)/shard_map/while/body/eval_jaxpr/all_to_all | solution.py:19
  393.8 1.0 copy-start.2
  396.4 10.6 %collective-permute-start = (f32[32,512]{0,1:T(8,128)S(1)}, f32[32,512]{0,1:T(8,128)S(1)}, u32[]{:S(2)}, u32[]{:S(2)}) collective-permute-start(f32[32,512]{0,1:T(8,128)S(1)} %scatter_fusion), channel_id=1, source_target_pairs={{0,64},{64,128},{128,192},{192,256},{256,320},{320,384},{384,448},... | collective-permute-start | bytes 196616 | tf_op jit(solution)/shard_map/while/body/eval_jaxpr/ppermute | solution.py:10
  408.0 23.9 %all-to-all-start = ((f32[64,8,256]{2,1,0:T(8,128)}), f32[64,8,256]{2,1,0:T(8,128)S(1)}, u32[]{:S(2)}, u32[]{:S(2)}) async-start(f32[64,8,256]{2,1,0:T(8,128)} %broadcast_in_dim.101), calls=%async_computation | async-start | bytes 1048576 | tf_op jit(solution)/shard_map/while/body/eval_jaxpr/all_to_all | solution.py:19
  432.7 1.2 copy-start
  435.8 23.4 %all-to-all-start.1 = ((f32[64,8,256]{2,1,0:T(8,128)}), f32[64,8,256]{2,1,0:T(8,128)S(1)}, u32[]{:S(2)}, u32[]{:S(2)}) async-start(f32[64,8,256]{2,1,0:T(8,128)} %broadcast_in_dim.103), calls=%async_computation.1 | async-start | bytes 1048576 | tf_op jit(solution)/shard_map/while/body/eval_jaxpr/all_to_all | solution.py:19
  460.0 1.0 copy-start.2
  462.5 10.6 %collective-permute-start = (f32[32,512]{0,1:T(8,128)S(1)}, f32[32,512]{0,1:T(8,128)S(1)}, u32[]{:S(2)}, u32[]{:S(2)}) collective-permute-start(f32[32,512]{0,1:T(8,128)S(1)} %scatter_fusion), channel_id=1, source_target_pairs={{0,64},{64,128},{128,192},{192,256},{256,320},{320,384},{384,448},... | collective-permute-start | bytes 196616 | tf_op jit(solution)/shard_map/while/body/eval_jaxpr/ppermute | solution.py:10
  473.1 0.7 copy-start.3
  474.8 23.9 %all-to-all-start.2 = ((f32[64,8,256]{2,1,0:T(8,128)}), f32[64,8,256]{2,1,0:T(8,128)S(1)}, u32[]{:S(2)}, u32[]{:S(2)}) async-start(f32[64,8,256]{2,1,0:T(8,128)} %broadcast_in_dim.82), calls=%async_computation.2 | async-start | bytes 1048576 | tf_op jit(solution)/shard_map/all_to_all | solution.py:19
  499.5 1.2 copy-start.1
